TPU v7x, 512 devices: a whole 4x8x8 slice. The times are simulated.
512 devices in a mesh: tok: 64 (over x, z, core), mlp: 8 (over y).
Axes of the slice: x: 4, y: 8, z: 8, core: 2. Of those that a mesh axis runs over, the one named last changes fastest.
Arguments:
- queries: bfloat16 [4096, 7168], P('tok', 'mlp')
- fresh_token_keys: bfloat16 [4096, 1024], P('tok', 'mlp'), may hold values from -6 to 6
- fresh_token_values: bfloat16 [4096, 1024], P('tok', 'mlp'), may hold values from -6 to 6
- leaf_key_block: bfloat16 [20480, 1024], P('tok', 'mlp'), may hold values from -6 to 6
- leaf_value_block: bfloat16 [20480, 1024], P('tok', 'mlp'), may hold values from -6 to 6
- shared_key_block: bfloat16 [16384, 1024], P('tok', 'mlp'), may hold values from -6 to 6
- shared_value_block: bfloat16 [16384, 1024], P('tok', 'mlp'), may hold values from -6 to 6
- out_weight: bfloat16 [7168, 7168], P('mlp', 'tok'), may hold values from -0.0625 to 0.0625
- residual: bfloat16 [4096, 7168], P('mlp', 'tok'), may hold values from -2.5 to 2.5
- token_request: int32 [4096], replicated, may hold values from 0 to 63, as said below
- positions: int32 [4096], P('tok'), may hold values from 129 to 831, as said below
- parents: int32 [74], replicated, may hold values from -1 to 9, as said below
- node_lengths: int32 [74], replicated, may hold values from 1 to 256, as said below
- node_owner: int32 [74], replicated, may hold values from 0 to 63, as said below
Outputs:
- hidden: bfloat16 [4096, 7168], P('mlp', 'tok')
- leaf_key_output: bfloat16 [20480, 1024], P('tok', 'mlp')
- leaf_value_output: bfloat16 [20480, 1024], P('tok', 'mlp')
Inputs may be any that keep to these rules, and one draw needn't show every extreme that they name: `token_request`: index d of tok holds the 64 new tokens of the request whose leaf it owns (node_owner of that leaf is d), in some order. positions = node_lengths of the token's root, middle and leaf plus the token's rank among its request's new tokens; the ranks of one request are 0 to 63, each once. `parents`: nodes 0 to 1 are roots (parent -1), the next 8 are middle nodes with a root as parent, the last 64 are the leaves of requests 0, 1, ... with a middle node as parent; every root and middle node has a child; the leaf of request 0 lies below root 0. `node_lengths`: roots and middle nodes hold 64 to 256 tokens, root 0 and the middle node above leaf 0 exactly 256; leaves hold 1 to 256, leaf 0 exactly 256. `node_owner`: the 10 roots and middle nodes have different owners; the leaves' owners are a permutation of the indices of tok; a node's cache starts at row 0 of its owner's block.
All inputs are finite; a program needn't handle non-finite values.
Results may differ from a plain program's by a relative error of at most 0.012.
Values may be sent and summed in bfloat16 or wider, within the bound.
No kernel may reach another device: no remote copies, remote signals or barrier semaphores. Data moves between devices by JAX's collectives and lax.ppermute only.
A program may use at most 64 MiB of HBM per device.

v0:
```python
import math

import jax
import jax.numpy as jnp
from jax import lax
from jax.sharding import PartitionSpec as P

HEAD_SIZE = 128
ROOTS = 2
MIDS = 8


THETA = 5000000.0
NEG = -1e30


def apply_rotary(values, position, heads):
    width = values.shape[1] // heads
    half = width // 2
    table = values.astype(jnp.float32).reshape(values.shape[0], heads, width)
    freq = THETA ** (-(jnp.arange(half, dtype=jnp.float32) * 2.0) / width)
    angle = position.astype(jnp.float32)[:, None] * freq[None, :]
    cosine = jnp.cos(angle)[:, None, :]
    sine = jnp.sin(angle)[:, None, :]
    first = table[:, :, :half]
    second = table[:, :, half:]
    turned = jnp.concatenate(
        [first * cosine - second * sine, second * cosine + first * sine], axis=2
    )
    return turned.reshape(values.shape).astype(jnp.bfloat16)


def attend_key_block(queries4, keys, values, valid):
    scale = 1.0 / math.sqrt(queries4.shape[-1])
    scores = (
        jnp.einsum("sgqd,rgd->sgqr", queries4, keys, preferred_element_type=jnp.float32) * scale
    )
    allowed = valid[:, None, None, :]
    highest = jnp.max(jnp.where(allowed, scores, NEG), axis=3)
    weights = jnp.where(allowed, jnp.exp(scores - highest[..., None]), 0.0).astype(jnp.bfloat16)
    total = jnp.sum(weights.astype(jnp.float32), axis=3)
    output = jnp.einsum("sgqr,rgd->sgqd", weights, values, preferred_element_type=jnp.float32)
    return (highest, total, output)


def merge_state(state, block):
    high_a, total_a, out_a = state
    running_peak_b, running_sum_b, partial_output_b = block
    highest = jnp.maximum(high_a, running_peak_b)
    scale_a = jnp.exp(high_a - highest)
    scale_b = jnp.exp(running_peak_b - highest)
    return (
        highest,
        scale_a * total_a + scale_b * running_sum_b,
        scale_a[..., None] * out_a + scale_b[..., None] * partial_output_b,
    )


def lookup(table, index):
    return jnp.sum(jnp.where(jnp.arange(table.shape[0]) == index, table, 0))


def body(
    queries,
    fresh_token_keys,
    fresh_token_values,
    leaf_key_block,
    leaf_value_block,
    shared_key_block,
    shared_value_block,
    out_weight,
    residual,
    token_request,
    positions,
    parents,
    node_lengths,
    node_owner,
):
    my_index = lax.axis_index("tok")
    tok_rows = queries.shape[0]
    width = HEAD_SIZE
    q_heads = queries.shape[1] // width
    kv_heads = fresh_token_keys.shape[1] // width
    group = q_heads // kv_heads
    kv_width = kv_heads * width
    shared_count = ROOTS + MIDS
    query_turned = apply_rotary(queries, positions, q_heads)
    key_turned = apply_rotary(fresh_token_keys, positions, kv_heads)
    my_request = lax.dynamic_slice_in_dim(token_request, my_index * tok_rows, 1)[0]
    leaf_node = shared_count + my_request
    middle = lookup(parents, leaf_node)
    root = lookup(parents, middle)
    leaf_length = lookup(node_lengths, leaf_node)
    root_length = lookup(node_lengths, root)
    middle_length = lookup(node_lengths, middle)
    new_index = positions - root_length - middle_length - leaf_length
    leaf_rows = leaf_key_block.shape[0]
    row_ids = jnp.arange(leaf_rows)
    place = (row_ids[:, None] == (leaf_length + new_index)[None, :]).astype(jnp.bfloat16)
    pairs = jnp.concatenate([key_turned, fresh_token_values], axis=1)
    placed = jnp.dot(place, pairs, preferred_element_type=jnp.float32).astype(jnp.bfloat16)
    keep = row_ids[:, None] < leaf_length
    leaf_key_output = jnp.where(keep, leaf_key_block, placed[:, :kv_width])
    leaf_value_output = jnp.where(keep, leaf_value_block, placed[:, kv_width:])
    token_queries = query_turned.reshape(tok_rows, kv_heads, group, width)
    leaf_row_mask = row_ids[None, :] < (leaf_length + new_index + 1)[:, None]
    leaf_state = attend_key_block(
        token_queries,
        leaf_key_output.reshape(leaf_rows, kv_heads, width),
        leaf_value_output.reshape(leaf_rows, kv_heads, width),
        leaf_row_mask,
    )
    node_rows = shared_key_block.shape[0]
    root_owner = lookup(node_owner, root)
    middle_owner = lookup(node_owner, middle)
    gathered = (
        lax.all_gather(shared_key_block, "tok", axis=0, tiled=True),
        lax.all_gather(shared_value_block, "tok", axis=0, tiled=True),
    )
    root_keys = lax.dynamic_slice_in_dim(gathered[0], root_owner * node_rows, node_rows, 0)
    root_values = lax.dynamic_slice_in_dim(gathered[1], root_owner * node_rows, node_rows, 0)
    middle_keys = lax.dynamic_slice_in_dim(gathered[0], middle_owner * node_rows, node_rows, 0)
    middle_values = lax.dynamic_slice_in_dim(gathered[1], middle_owner * node_rows, node_rows, 0)
    node_ids = jnp.arange(node_rows)
    both_keys = jnp.concatenate([root_keys, middle_keys], axis=0).reshape(
        2 * node_rows, kv_heads, width
    )
    both_values = jnp.concatenate([root_values, middle_values], axis=0).reshape(
        2 * node_rows, kv_heads, width
    )
    both_valid = jnp.concatenate([node_ids < root_length, node_ids < middle_length], axis=0)
    shared_state = attend_key_block(token_queries, both_keys, both_values, both_valid[None, :])
    final = merge_state(shared_state, leaf_state)
    attended_local = (
        (final[2] / final[1][..., None]).reshape(tok_rows, q_heads * width).astype(jnp.bfloat16)
    )
    projected = jnp.dot(
        lax.all_gather(attended_local, "tok", axis=0, tiled=True),
        out_weight,
        preferred_element_type=jnp.float32,
    )
    summed = lax.psum_scatter(projected, "mlp", scatter_dimension=0, tiled=True)
    hidden = (residual.astype(jnp.float32) + summed).astype(jnp.bfloat16)
    return (hidden, leaf_key_output, leaf_value_output)


def solution(mesh):
    placed = (
        P("tok", "mlp"),
        P("tok", "mlp"),
        P("tok", "mlp"),
        P("tok", "mlp"),
        P("tok", "mlp"),
        P("tok", "mlp"),
        P("tok", "mlp"),
        P("mlp", "tok"),
        P("mlp", "tok"),
        P(),
        P("tok"),
        P(),
        P(),
        P(),
    )
    return jax.shard_map(
        body,
        mesh=mesh,
        in_specs=placed,
        out_specs=(P("mlp", "tok"), P("tok", "mlp"), P("tok", "mlp")),
        check_vma=False,
    )
```

profile of v0, /device:TPU:1, one launch (start us, length us, event | category | flops | bytes accessed | tf_op | source)
XLA Modules:
  0.0 327.0 jit_solution(14689822310884693069)
XLA Ops:
  7.2 0.7 all-gather.4.cloned.1.call-update
  8.0 0.7 all-gather.6.cloned.1.call-update
  8.7 1.3 dynamic_slice.15
  10.6 1.3 fusion.30
  11.9 1.9 select_reduce_fusion.4
  13.9 2.7 fusion.31
  17.7 1.0 reshape.252
  18.8 0.6 iota_compare_fusion.3
  19.4 0.6 iota_compare_fusion.5
  20.0 0.6 iota_compare_fusion.4
  20.6 1.9 broadcast_add_fusion
  22.5 0.7 bitcast_convert_fusion
  23.2 0.2 fusion.22
  23.6 0.2 multiply_cosine_fusion.1
  23.8 0.9 convolution_convert_fusion
  24.7 1.1 slice_select_fusion
  25.8 0.1 fusion.42
  26.0 0.4 select_reduce_fusion.1
  26.4 0.3 convert_reduce_fusion.1
  26.7 75.8 %all-gather.4.cloned.1.call-done = bf16[16384,128]{1,0:T(8,128)(2,1)} async-done(((bf16[256,128]{1,0:T(8,128)(2,1)}), bf16[16384,128]{1,0:T(8,128)(2,1)}) %all-gather.4.cloned.1.call-update) | async-done | bytes 4194320 | tf_op jit(solution)/shard_map/all_gather | solution.py:117
  102.5 0.9 constant_dynamic-slice_fusion.3
  103.4 0.4 select_reduce_fusion
  103.8 0.3 convert_reduce_fusion
  104.1 83.5 %all-gather.6.cloned.1.call-done = bf16[16384,128]{1,0:T(8,128)(2,1)} async-done(((bf16[256,128]{1,0:T(8,128)(2,1)}), bf16[16384,128]{1,0:T(8,128)(2,1)}) %all-gather.6.cloned.1.call-update) | async-done | bytes 4194320 | tf_op jit(solution)/shard_map/all_gather | solution.py:118
  187.7 0.9 constant_dynamic-slice_fusion.1
  188.6 0.3 fusion.5
  188.9 0.3 fusion.7
  189.3 0.7 copy.28
  190.1 86.3 %all-gather.8.cloned.1.call-done = bf16[4096,896]{1,0:T(8,128)(2,1)} async-done(((bf16[64,896]{1,0:T(8,128)(2,1)}), bf16[4096,896]{1,0:T(8,128)(2,1)}) %all-gather.8.cloned.1.call-update) | async-done | bytes 7340048 | tf_op jit(solution)/shard_map/all_gather | solution.py:138
  276.4 6.7 %fusion.43 = f32[4096,112]{0,1:T(8,128)} fusion(bf16[4096,896]{1,0:T(8,128)(2,1)} %all-gather.8.cloned.1.call-done, bf16[896,112]{0,1:T(8,128)(2,1)S(1)} %copy-done), kind=kOutput, calls=%fused_computation.91 | convolution fusion | flops 822083584 | bytes 9375744 | tf_op jit(solution)/shard_map/dot_general | solution.py:137
  283.2 35.6 %reduce-scatter.2.cloned.1.call-done = f32[512,112]{0,1:T(8,128)} async-done(((f32[4096,112]{0,1:T(8,128)}), f32[512,112]{0,1:T(8,128)}) %reduce-scatter.2.cloned.1.call-update) | async-done | bytes 229392 | tf_op jit(solution)/shard_map/reduce_scatter | solution.py:142
  318.8 1.6 add_convert_fusion
  (21 shorter events, 0.6 us)
Async XLA Ops:
  7.2 269.3 %copy-start = (bf16[896,112]{0,1:T(8,128)(2,1)S(1)}, bf16[896,112]{0,1:T(8,128)(2,1)}, u32[]{:S(2)}) copy-start(bf16[896,112]{0,1:T(8,128)(2,1)} %param.21) | copy-start | bytes 602116
  7.2 95.3 %all-gather.4.cloned.1.call-start = ((), (), s32[]{:S(2)}) async-start(), calls=%async_computation.1 | async-start | bytes 4259840 | tf_op jit(solution)/shard_map/all_gather | solution.py:117
  7.9 179.8 %all-gather.6.cloned.1.call-start = ((), (), s32[]{:S(2)}) async-start(), calls=%async_computation.2 | async-start | bytes 4259840 | tf_op jit(solution)/shard_map/all_gather | solution.py:118
  8.7 267.7 %all-gather.8.cloned.1.call-start = ((), (), s32[]{:S(2)}) async-start(), calls=%async_computation.3 | async-start | bytes 7454720 | tf_op jit(solution)/shard_map/all_gather | solution.py:138
  25.8 163.5 %copy-start.1 = (bf16[320,128]{1,0:T(8,128)(2,1)}, bf16[320,128]{1,0:T(8,128)(2,1)S(1)}, u32[]{:S(2)}) copy-start(bf16[320,128]{1,0:T(8,128)(2,1)S(1)} %get-tuple-element.22) | copy-start | bytes 245764
  25.8 163.5 %copy-start.3 = (bf16[320,128]{1,0:T(8,128)(2,1)}, bf16[320,128]{1,0:T(8,128)(2,1)S(1)}, u32[]{:S(2)}) copy-start(bf16[320,128]{1,0:T(8,128)(2,1)S(1)} %get-tuple-element.21) | copy-start | bytes 245764
  190.0 128.8 %copy-start.2 = (bf16[512,112]{0,1:T(8,128)(2,1)S(1)}, bf16[512,112]{0,1:T(8,128)(2,1)}, u32[]{:S(2)}) copy-start(bf16[512,112]{0,1:T(8,128)(2,1)} %param.22) | copy-start | bytes 344068
  190.0 128.8 %reduce-scatter.2.cloned.1.call-start = ((), (), s32[]{:S(2)}) async-start(), calls=%async_computation.4 | async-start | bytes 2064384 | tf_op jit(solution)/shard_map/reduce_scatter | solution.py:142
Sparse Core Ops, SparseCore 0:
  11.4 91.0 all-gather.3
  105.9 81.7 all-gather.5
  191.6 84.7 all-gather.7
  283.3 35.4 reduce-scatter.1
where the time goes:
time: 331 us; the launch traced here: 327 us
  waiting for transfers between devices  283 us (85%)
  between operations  15.8 us (5%)
  other arithmetic  14.3 us (4%)
  matrix products  9.09 us (3%)
  local copies, waits for them, and re-layouts  4.98 us (2%)
    all_gather x1, waiting for transfers between devices, body(): lax.all_gather(attended_local, 'tok', axis=0, tiled=True)  86.3 us
    all_gather x1, waiting for transfers between devices, body(): lax.all_gather(shared_value_block, 'tok', axis=0, tiled=True)  83.5 us
    all_gather x1, waiting for transfers between devices, body(): lax.all_gather(shared_key_block, 'tok', axis=0, tiled=True)  75.8 us
    reduce_scatter x1, waiting for transfers between devices, body(): summed = lax.psum_scatter(projected, 'mlp', scatter_dimension=0, tiled=True)  35.6 us
    dot_general x1, matrix products, body(): jnp.dot(lax.all_gather(attended_local, 'tok', axis=0, tiled=True), out_we...  6.74 us
  transfers between devices with their start and end apart: 4, of which 4 were waited for; matrix products, arithmetic and copies ran while one was open for 5% of the time, Pallas kernels for 0%

commit v1 on v0

--- a/solution.py
+++ b/solution.py
@@ -113,14 +113,16 @@
     node_rows = shared_key_block.shape[0]
     root_owner = lookup(node_owner, root)
     middle_owner = lookup(node_owner, middle)
-    gathered = (
-        lax.all_gather(shared_key_block, "tok", axis=0, tiled=True),
-        lax.all_gather(shared_value_block, "tok", axis=0, tiled=True),
-    )
-    root_keys = lax.dynamic_slice_in_dim(gathered[0], root_owner * node_rows, node_rows, 0)
-    root_values = lax.dynamic_slice_in_dim(gathered[1], root_owner * node_rows, node_rows, 0)
-    middle_keys = lax.dynamic_slice_in_dim(gathered[0], middle_owner * node_rows, node_rows, 0)
-    middle_values = lax.dynamic_slice_in_dim(gathered[1], middle_owner * node_rows, node_rows, 0)
+    owned = node_owner[:shared_count] == my_index
+    my_pair = jnp.concatenate([shared_key_block, shared_value_block], axis=1)
+    slots = jnp.where(owned[:, None, None], my_pair[None], jnp.zeros_like(my_pair)[None])
+    gathered = lax.psum(slots, "tok")
+    root_pair = lax.dynamic_index_in_dim(gathered, root, 0, keepdims=False)
+    middle_pair = lax.dynamic_index_in_dim(gathered, middle, 0, keepdims=False)
+    root_keys = root_pair[:, :kv_width]
+    root_values = root_pair[:, kv_width:]
+    middle_keys = middle_pair[:, :kv_width]
+    middle_values = middle_pair[:, kv_width:]
     node_ids = jnp.arange(node_rows)
     both_keys = jnp.concatenate([root_keys, middle_keys], axis=0).reshape(
         2 * node_rows, kv_heads, width

time: 331 us -> 362 us (1.094)
  waiting for transfers between devices: 283 us -> 314 us
    psum x0 -> x1, waiting for transfers between devices: none -> 189 us  [body(): gathered = lax.psum(slots, 'tok')]
    all_gather x2 -> x0, waiting for transfers between devices: 159 us -> none  [the longest x1 83.5 us: body(): lax.all_gather(shared_value_block, 'tok', axis=0, tiled=True)]
  transfers between devices with their start and end apart: 4 -> 3, of which waited for: 4 -> 3; matrix products, arithmetic and copies ran while one was open for 5% -> 3% of each run, Pallas kernels for 0% -> 0%
where the time goes in v1:
time: 362 us; the launch traced here: 358 us
  waiting for transfers between devices  314 us (87%)
  between operations  18.3 us (5%)
  other arithmetic  13.1 us (4%)
  matrix products  8.37 us (2%)
    psum x1, waiting for transfers between devices, body(): gathered = lax.psum(slots, 'tok')  189 us
    all_gather x1, waiting for transfers between devices, body(): lax.all_gather(attended_local, 'tok', axis=0, tiled=True)  89.6 us
    reduce_scatter x1, waiting for transfers between devices, body(): summed = lax.psum_scatter(projected, 'mlp', scatter_dimension=0, tiled=True)  35.6 us
  transfers between devices with their start and end apart: 3, of which 3 were waited for; matrix products, arithmetic and copies ran while one was open for 3% of the time, Pallas kernels for 0%

profile of v1, /device:TPU:1, one launch (start us, length us, event | category | flops | bytes accessed | tf_op | source)
XLA Modules:
  0.0 357.7 jit_solution(1075422729623819962)
XLA Ops:
  7.3 0.7 slice_compare_fusion
  8.0 0.9 pad_maximum_fusion
  8.9 1.2 broadcast_select_fusion
  10.2 1.3 dynamic_slice.10
  12.2 0.6 fusion.30
  12.8 1.3 fusion.32
  14.1 1.9 fusion.31
  16.0 0.6 iota_compare_fusion.3
  16.7 1.4 broadcast_add_fusion
  18.2 0.2 multiply_cosine_fusion.1
  18.4 0.2 fusion.22
  18.6 0.1 reshape.254
  18.7 0.1 fusion.43
  18.9 0.1 maximum_bitcast_fusion.4
  19.0 0.2 convolution_convert_fusion
  19.2 0.1 slice_select_fusion
  19.3 1.4 iota_compare_fusion.4
  24.3 0.1 subtract_convert_fusion
  24.4 0.4 select_reduce_fusion.1
  24.8 0.3 convert_reduce_fusion.1
  25.1 189.2 %all-reduce.2.cloned.1.call-done = bf16[10,256,256]{2,1,0:T(8,128)(2,1)} async-done(((bf16[10,256,256]{2,1,0:T(8,128)(2,1)}), bf16[10,256,256]{2,1,0:T(8,128)(2,1)}) %all-reduce.2.cloned.1.call-update) | async-done | bytes 1310736 | tf_op jit(solution)/shard_map/psum | solution.py:119
  214.3 1.0 dynamic-slice_bitcast_fusion.1
  215.3 0.4 select_reduce_fusion
  215.8 0.3 convert_reduce_fusion
  216.1 0.3 fusion.5
  216.5 0.3 fusion.7
  216.8 0.1 copy.19
  216.9 0.7 copy.28
  217.6 89.6 %all-gather.2.cloned.1.call-done = bf16[4096,896]{1,0:T(8,128)(2,1)} async-done(((bf16[64,896]{1,0:T(8,128)(2,1)}), bf16[4096,896]{1,0:T(8,128)(2,1)}) %all-gather.2.cloned.1.call-update) | async-done | bytes 7340048 | tf_op jit(solution)/shard_map/all_gather | solution.py:140
  307.2 6.7 %fusion.46 = f32[4096,112]{0,1:T(8,128)} fusion(bf16[4096,896]{1,0:T(8,128)(2,1)} %all-gather.2.cloned.1.call-done, bf16[896,112]{0,1:T(8,128)(2,1)S(1)} %copy-done), kind=kOutput, calls=%fused_computation.92 | convolution fusion | flops 822083584 | bytes 9375744 | tf_op jit(solution)/shard_map/dot_general | solution.py:139
  313.9 35.6 %reduce-scatter.2.cloned.1.call-done = f32[512,112]{0,1:T(8,128)} async-done(((f32[4096,112]{0,1:T(8,128)}), f32[512,112]{0,1:T(8,128)}) %reduce-scatter.2.cloned.1.call-update) | async-done | bytes 229392 | tf_op jit(solution)/shard_map/reduce_scatter | solution.py:144
  349.6 1.6 add_convert_fusion
  (36 shorter events, 0.4 us)
Async XLA Ops:
  7.2 300.0 %copy-start = (bf16[896,112]{0,1:T(8,128)(2,1)S(1)}, bf16[896,112]{0,1:T(8,128)(2,1)}, u32[]{:S(2)}) copy-start(bf16[896,112]{0,1:T(8,128)(2,1)} %param.21) | copy-start | bytes 602116
  7.2 5.0 %copy-start.11 = (s32[74]{0:T(128)S(1)}, s32[74]{0:T(128)}, u32[]{:S(2)}) copy-start(s32[74]{0:T(128)} %param.25) | copy-start | bytes 892
  7.2 6.9 %copy-start.9 = (s32[74]{0:T(128)S(1)}, s32[74]{0:T(128)}, u32[]{:S(2)}) copy-start(s32[74]{0:T(128)} %param.26) | copy-start | bytes 892
  7.2 9.5 %copy-start.10 = (s32[64]{0:T(128)S(1)}, s32[64]{0:T(128)}, u32[]{:S(2)}) copy-start(s32[64]{0:T(128)} %param.24) | copy-start | bytes 772
  7.2 10.9 %copy-start.7 = (bf16[64,128]{1,0:T(8,128)(2,1)S(1)}, bf16[64,128]{1,0:T(8,128)(2,1)}, u32[]{:S(2)}) copy-start(bf16[64,128]{1,0:T(8,128)(2,1)} %param.15) | copy-start | bytes 49156
  7.2 11.4 %copy-start.3 = (bf16[64,896]{1,0:T(8,128)(2,1)S(1)}, bf16[64,896]{1,0:T(8,128)(2,1)}, u32[]{:S(2)}) copy-start(bf16[64,896]{1,0:T(8,128)(2,1)} %param.14) | copy-start | bytes 344068
  7.2 207.1 %all-reduce.2.cloned.1.call-start = ((), (), s32[]{:S(2)}) async-start(), calls=%async_computation.1 | async-start | bytes 2621440 | tf_op jit(solution)/shard_map/psum | solution.py:119
  10.1 8.8 %copy-start.8 = (bf16[64,128]{1,0:T(8,128)(2,1)S(1)}, bf16[64,128]{1,0:T(8,128)(2,1)}, u32[]{:S(2)}) copy-start(bf16[64,128]{1,0:T(8,128)(2,1)} %param.16) | copy-start | bytes 49156
  10.1 9.0 %copy-start.4 = (bf16[320,128]{1,0:T(8,128)(2,1)S(1)}, bf16[320,128]{1,0:T(8,128)(2,1)}, u32[]{:S(2)}) copy-start(bf16[320,128]{1,0:T(8,128)(2,1)} %param.18) | copy-start | bytes 245764
  10.1 9.0 %copy-start.5 = (bf16[320,128]{1,0:T(8,128)(2,1)S(1)}, bf16[320,128]{1,0:T(8,128)(2,1)}, u32[]{:S(2)}) copy-start(bf16[320,128]{1,0:T(8,128)(2,1)} %param.17) | copy-start | bytes 245764
  10.2 297.0 %all-gather.2.cloned.1.call-start = ((), (), s32[]{:S(2)}) async-start(), calls=%async_computation.2 | async-start | bytes 7454720 | tf_op jit(solution)/shard_map/all_gather | solution.py:140
  19.3 196.5 %copy-start.1 = (bf16[320,128]{1,0:T(8,128)(2,1)}, bf16[320,128]{1,0:T(8,128)(2,1)S(1)}, u32[]{:S(2)}) copy-start(bf16[320,128]{1,0:T(8,128)(2,1)S(1)} %get-tuple-element.18) | copy-start | bytes 245764
  19.3 197.2 %copy-start.6 = (bf16[320,128]{1,0:T(8,128)(2,1)}, bf16[320,128]{1,0:T(8,128)(2,1)S(1)}, u32[]{:S(2)}) copy-start(bf16[320,128]{1,0:T(8,128)(2,1)S(1)} %get-tuple-element.17) | copy-start | bytes 245764
  217.6 132.0 %reduce-scatter.2.cloned.1.call-start = ((), (), s32[]{:S(2)}) async-start(), calls=%async_computation.3 | async-start | bytes 2064384 | tf_op jit(solution)/shard_map/reduce_scatter | solution.py:144
  313.9 35.6 %copy-start.2 = (bf16[512,112]{0,1:T(8,128)(2,1)S(1)}, bf16[512,112]{0,1:T(8,128)(2,1)}, u32[]{:S(2)}) copy-start(bf16[512,112]{0,1:T(8,128)(2,1)} %param.22) | copy-start | bytes 344068
Sparse Core Ops, SparseCore 0:
  11.5 202.7 all-reduce.1
  218.7 88.4 all-gather.1
  314.1 35.4 reduce-scatter.1

commit v2 on v1

--- a/solution.py
+++ b/solution.py
@@ -76,7 +76,13 @@
     node_lengths,
     node_owner,
 ):
-    my_index = lax.axis_index("tok")
+    hi = lax.axis_index("hi")
+    lo = lax.axis_index("lo")
+    mlp = lax.axis_index("mlp")
+    lo_count = lax.axis_size("lo")
+    hi_count = lax.axis_size("hi")
+    mlp_count = lax.axis_size("mlp")
+    my_index = hi * lo_count + lo
     tok_rows = queries.shape[0]
     width = HEAD_SIZE
     q_heads = queries.shape[1] // width
@@ -84,6 +90,23 @@
     group = q_heads // kv_heads
     kv_width = kv_heads * width
     shared_count = ROOTS + MIDS
+
+    my_pair = jnp.concatenate([shared_key_block, shared_value_block], axis=1)
+    row_pairs = lax.all_gather(my_pair, "lo", axis=0, tiled=False)
+    requests = token_request.reshape(-1, tok_rows)[:, 0]
+    middles = parents[shared_count + requests]
+    roots = parents[middles]
+    root_owners = node_owner[roots]
+    middle_owners = node_owner[middles]
+    column = jnp.arange(hi_count) * lo_count + lo
+    wanted = jnp.stack(
+        [root_owners[column] % lo_count, middle_owners[column] % lo_count], axis=1
+    )
+    outgoing = jnp.take(row_pairs, wanted.reshape(-1), axis=0).reshape(
+        (hi_count, 2) + my_pair.shape
+    )
+    incoming = lax.all_to_all(outgoing, "hi", 0, 0, tiled=True)
+
     query_turned = apply_rotary(queries, positions, q_heads)
     key_turned = apply_rotary(fresh_token_keys, positions, kv_heads)
     my_request = lax.dynamic_slice_in_dim(token_request, my_index * tok_rows, 1)[0]
@@ -113,12 +136,8 @@
     node_rows = shared_key_block.shape[0]
     root_owner = lookup(node_owner, root)
     middle_owner = lookup(node_owner, middle)
-    owned = node_owner[:shared_count] == my_index
-    my_pair = jnp.concatenate([shared_key_block, shared_value_block], axis=1)
-    slots = jnp.where(owned[:, None, None], my_pair[None], jnp.zeros_like(my_pair)[None])
-    gathered = lax.psum(slots, "tok")
-    root_pair = lax.dynamic_index_in_dim(gathered, root, 0, keepdims=False)
-    middle_pair = lax.dynamic_index_in_dim(gathered, middle, 0, keepdims=False)
+    root_pair = lax.dynamic_index_in_dim(incoming, root_owner // lo_count, 0, keepdims=False)[0]
+    middle_pair = lax.dynamic_index_in_dim(incoming, middle_owner // lo_count, 0, keepdims=False)[1]
     root_keys = root_pair[:, :kv_width]
     root_values = root_pair[:, kv_width:]
     middle_keys = middle_pair[:, :kv_width]
@@ -136,37 +155,46 @@
     attended_local = (
         (final[2] / final[1][..., None]).reshape(tok_rows, q_heads * width).astype(jnp.bfloat16)
     )
-    projected = jnp.dot(
-        lax.all_gather(attended_local, "tok", axis=0, tiled=True),
-        out_weight,
-        preferred_element_type=jnp.float32,
-    )
-    summed = lax.psum_scatter(projected, "mlp", scatter_dimension=0, tiled=True)
-    hidden = (residual.astype(jnp.float32) + summed).astype(jnp.bfloat16)
+
+    swap = [
+        (h * mlp_count + m, m * mlp_count + h) for h in range(hi_count) for m in range(mlp_count)
+    ]
+    residual_here = lax.ppermute(residual, ("hi", "mlp"), swap)
+    weight_cols = lax.all_gather(out_weight, "hi", axis=1, tiled=True)
+    token_block = lax.all_gather(attended_local, "lo", axis=0, tiled=True)
+    projected = jnp.dot(token_block, weight_cols, preferred_element_type=jnp.float32)
+    summed = lax.psum_scatter(projected, "mlp", scatter_dimension=1, tiled=True)
+    result = (residual_here.astype(jnp.float32) + summed).astype(jnp.bfloat16)
+    hidden = lax.ppermute(result, ("hi", "mlp"), swap)
     return (hidden, leaf_key_output, leaf_value_output)
 
 
 def solution(mesh):
+    tok_count = mesh.shape["tok"]
+    lo_count = 8
+    grid = mesh.devices.reshape(tok_count // lo_count, lo_count, mesh.shape["mlp"])
+    split = jax.sharding.Mesh(grid, ("hi", "lo", "mlp"))
+    tok = ("hi", "lo")
     placed = (
-        P("tok", "mlp"),
-        P("tok", "mlp"),
-        P("tok", "mlp"),
-        P("tok", "mlp"),
-        P("tok", "mlp"),
-        P("tok", "mlp"),
-        P("tok", "mlp"),
-        P("mlp", "tok"),
-        P("mlp", "tok"),
-        P(),
-        P("tok"),
+        P(tok, "mlp"),
+        P(tok, "mlp"),
+        P(tok, "mlp"),
+        P(tok, "mlp"),
+        P(tok, "mlp"),
+        P(tok, "mlp"),
+        P(tok, "mlp"),
+        P("mlp", tok),
+        P("mlp", tok),
+        P(),
+        P(tok),
         P(),
         P(),
         P(),
     )
     return jax.shard_map(
         body,
-        mesh=mesh,
+        mesh=split,
         in_specs=placed,
-        out_specs=(P("mlp", "tok"), P("tok", "mlp"), P("tok", "mlp")),
+        out_specs=(P("mlp", tok), P(tok, "mlp"), P(tok, "mlp")),
         check_vma=False,
     )

time: 362 us -> 242 us (0.67)
  the two profiles are of different devices: /device:TPU:1 before, /device:TPU:110 now
where the time goes in v2:
time: 242 us; the launch traced here: 241 us
  waiting for transfers between devices  129 us (53%)
  blocking collectives  37.3 us (15%)
  starting transfers between devices  22.5 us (9%)
  between operations  21.5 us (9%)
  other arithmetic  13 us (5%)
  local copies, waits for them, and re-layouts  11.9 us (5%)
  matrix products  5.45 us (2%)
    all_gather x1, blocking collectives, body(): token_block = lax.all_gather(attended_local, 'lo', axis=0, tiled=True)  37.3 us
    all_gather x1, waiting for transfers between devices, body(): row_pairs = lax.all_gather(my_pair, 'lo', axis=0, tiled=False)  33.7 us
    ppermute x1, waiting for transfers between devices, body(): residual_here = lax.ppermute(residual, ('hi', 'mlp'), swap)  24.6 us
    all_gather x1, waiting for transfers between devices, body(): weight_cols = lax.all_gather(out_weight, 'hi', axis=1, tiled=True)  23.2 us
    all_to_all x1, waiting for transfers between devices, body(): incoming = lax.all_to_all(outgoing, 'hi', 0, 0, tiled=True)  17.9 us
    ppermute x1, waiting for transfers between devices, body(): hidden = lax.ppermute(result, ('hi', 'mlp'), swap)  17 us
    reduce_scatter x1, waiting for transfers between devices, body(): summed = lax.psum_scatter(projected, 'mlp', scatter_dimension=1, tiled=True)  12.6 us
    ppermute x1, starting transfers between devices, body(): hidden = lax.ppermute(result, ('hi', 'mlp'), swap)  11.4 us
  transfers between devices with their start and end apart: 6, of which 6 were waited for; matrix products, arithmetic and copies ran while one was open for 8% of the time, Pallas kernels for 0%

profile of v2, /device:TPU:110, one launch (start us, length us, event | category | flops | bytes accessed | tf_op | source)
XLA Modules:
  0.0 241.1 jit_solution(7159513708934547752)
XLA Ops:
  8.1 1.5 pad_maximum_fusion
  9.6 0.8 reshape.411
  10.5 1.4 gather_fusion
  12.2 1.4 gather_fusion.1
  13.7 1.4 gather_fusion.4
  15.3 0.8 gather_fusion.2
  16.1 0.6 gather_fusion.3
  16.7 0.6 gather_fusion.5
  17.7 33.7 %all-gather.6.cloned.1.call-done = bf16[2048,256]{1,0:T(8,128)(2,1)} async-done(((bf16[256,256]{1,0:T(8,128)(2,1)}), bf16[2048,256]{1,0:T(8,128)(2,1)}) %all-gather.6.cloned.1.call-update) | async-done | bytes 1048592 | tf_op jit(solution)/shard_map/all_gather | solution.py:95
  51.4 1.9 gather_fusion.6
  53.3 1.6 broadcast_select_fusion
  55.0 7.8 %all-to-all-start = ((bf16[8,2,256,256]{3,2,1,0:T(8,128)(2,1)}), bf16[8,2,256,256]{3,2,1,0:T(8,128)(2,1)S(1)}, u32[]{:S(2)}, u32[]{:S(2)}) async-start(bf16[8,2,256,256]{3,2,1,0:T(8,128)(2,1)} %broadcast_select_fusion), calls=%async_computation | async-start | bytes 4194304 | tf_op jit(solution)/shard_map/all_to_all | solution.py:108
  62.7 0.6 all-gather.4.cloned.1.call-update
  63.4 1.3 dynamic_slice.10
  65.3 0.6 fusion.33
  65.9 1.3 select_reduce_fusion.4
  67.2 2.0 fusion.34
  69.3 0.6 iota_compare_fusion.4
  69.9 0.6 iota_compare_fusion.5
  70.5 0.6 iota_compare_fusion.3
  71.2 1.2 broadcast_add_fusion
  79.5 17.9 %all-to-all-done = bf16[8,2,256,256]{3,2,1,0:T(8,128)(2,1)S(1)} async-done(((bf16[8,2,256,256]{3,2,1,0:T(8,128)(2,1)}), bf16[8,2,256,256]{3,2,1,0:T(8,128)(2,1)S(1)}, u32[]{:S(2)}, u32[]{:S(2)}) %all-to-all-start) | async-done | bytes 2097184 | tf_op jit(solution)/shard_map/all_to_all | solution.py:108
  99.0 37.3 %all_gather.14 = bf16[512,896]{1,0:T(8,128)(2,1)S(1)} all-gather(bf16[64,896]{1,0:T(8,128)(2,1)S(1)} %bitcast.82), channel_id=1, replica_groups=mesh['hi'=8,'lo'=8,'mlp'=8] {'lo'}, dimensions={0}, use_global_device_ids=true | all-gather | bytes 1032192 | tf_op jit(solution)/shard_map/all_gather | solution.py:164
  136.3 23.2 %all-gather.4.cloned.1.call-done = bf16[896,896]{0,1:T(8,128)(2,1)} async-done(((bf16[896,112]{0,1:T(8,128)(2,1)}), bf16[896,896]{0,1:T(8,128)(2,1)}) %all-gather.4.cloned.1.call-update) | async-done | bytes 1605648 | tf_op jit(solution)/shard_map/all_gather | solution.py:163
  159.4 3.8 %fusion.52 = f32[512,896]{0,1:T(8,128)} fusion(bf16[512,896]{1,0:T(8,128)(2,1)S(1)} %all_gather.14, bf16[896,896]{0,1:T(8,128)(2,1)} %all-gather.4.cloned.1.call-done), kind=kOutput, calls=%fused_computation.126 | convolution fusion | flops 822083584 | bytes 4358144 | tf_op jit(solution)/shard_map/dot_general | solution.py:165
  163.3 3.3 %collective-permute-start = (bf16[512,112]{0,1:T(8,128)(2,1)S(1)}, bf16[512,112]{0,1:T(8,128)(2,1)S(1)}, u32[]{:S(2)}, u32[]{:S(2)}) collective-permute-start(bf16[512,112]{0,1:T(8,128)(2,1)S(1)} %copy-done.11), channel_id=1, source_target_pairs={{0,0},{1,64},{2,128},{3,192},{4,256},{5,320},{6,384},{7,448},{64,1... | collective-permute-start | bytes 344072 | tf_op jit(solution)/shard_map/ppermute | solution.py:162
  166.6 24.6 %collective-permute-done = bf16[512,112]{0,1:T(8,128)(2,1)S(1)} collective-permute-done((bf16[512,112]{0,1:T(8,128)(2,1)S(1)}, bf16[512,112]{0,1:T(8,128)(2,1)S(1)}, u32[]{:S(2)}, u32[]{:S(2)}) %collective-permute-start) | collective-permute-done | bytes 114720 | tf_op jit(solution)/shard_map/ppermute | solution.py:162
  191.2 12.6 %reduce-scatter.2.cloned.1.call-done = f32[512,112]{0,1:T(8,128)} async-done(((f32[512,896]{0,1:T(8,128)}), f32[512,112]{0,1:T(8,128)}) %reduce-scatter.2.cloned.1.call-update) | async-done | bytes 229392 | tf_op jit(solution)/shard_map/reduce_scatter | solution.py:166
  203.8 1.0 add_convert_fusion
  204.7 11.4 %collective-permute-start.1 = (bf16[512,112]{0,1:T(8,128)(2,1)S(1)}, bf16[512,112]{0,1:T(8,128)(2,1)S(1)}, u32[]{:S(2)}, u32[]{:S(2)}) collective-permute-start(bf16[512,112]{0,1:T(8,128)(2,1)S(1)} %add_convert_fusion), channel_id=1, source_target_pairs={{0,0},{1,64},{2,128},{3,192},{4,256},{5,320},{6,384},{7,448},{64,1... | collective-permute-start | bytes 344072 | tf_op jit(solution)/shard_map/ppermute | solution.py:168
  216.1 17.0 %collective-permute-done.1 = bf16[512,112]{0,1:T(8,128)(2,1)S(1)} collective-permute-done((bf16[512,112]{0,1:T(8,128)(2,1)S(1)}, bf16[512,112]{0,1:T(8,128)(2,1)S(1)}, u32[]{:S(2)}, u32[]{:S(2)}) %collective-permute-start.1) | collective-permute-done | bytes 114720 | tf_op jit(solution)/shard_map/ppermute | solution.py:168
  233.1 0.6 copy.51
  (71 shorter events, 4.5 us)
Async XLA Ops:
  8.0 7.3 %copy-start = (s32[74]{0:T(128)S(1)}, s32[74]{0:T(128)}, u32[]{:S(2)}) copy-start(s32[74]{0:T(128)} %param.27) | copy-start | bytes 892
  8.0 43.4 %all-gather.6.cloned.1.call-start = ((), (), s32[]{:S(2)}) async-start(), calls=%async_computation.4 | async-start | bytes 1179648 | tf_op jit(solution)/shard_map/all_gather | solution.py:95
  54.9 10.4 %copy-start.1 = (s32[74]{0:T(128)S(1)}, s32[74]{0:T(128)}, u32[]{:S(2)}) copy-start(s32[74]{0:T(128)} %param.25) | copy-start | bytes 892
  54.9 12.3 %copy-start.9 = (s32[74]{0:T(128)S(1)}, s32[74]{0:T(128)}, u32[]{:S(2)}) copy-start(s32[74]{0:T(128)} %param.26) | copy-start | bytes 892
  54.9 16.3 %copy-start.10 = (s32[64]{0:T(128)S(1)}, s32[64]{0:T(128)}, u32[]{:S(2)}) copy-start(s32[64]{0:T(128)} %param.24) | copy-start | bytes 772
  54.9 17.5 %copy-start.7 = (bf16[64,128]{1,0:T(8,128)(2,1)S(1)}, bf16[64,128]{1,0:T(8,128)(2,1)}, u32[]{:S(2)}) copy-start(bf16[64,128]{1,0:T(8,128)(2,1)} %param.15) | copy-start | bytes 49156
  54.9 18.1 %copy-start.8 = (bf16[64,128]{1,0:T(8,128)(2,1)S(1)}, bf16[64,128]{1,0:T(8,128)(2,1)}, u32[]{:S(2)}) copy-start(bf16[64,128]{1,0:T(8,128)(2,1)} %param.16) | copy-start | bytes 49156
  54.9 18.3 %copy-start.4 = (bf16[320,128]{1,0:T(8,128)(2,1)S(1)}, bf16[320,128]{1,0:T(8,128)(2,1)}, u32[]{:S(2)}) copy-start(bf16[320,128]{1,0:T(8,128)(2,1)} %param.18) | copy-start | bytes 245764
  54.9 18.3 %copy-start.5 = (bf16[320,128]{1,0:T(8,128)(2,1)S(1)}, bf16[320,128]{1,0:T(8,128)(2,1)}, u32[]{:S(2)}) copy-start(bf16[320,128]{1,0:T(8,128)(2,1)} %param.17) | copy-start | bytes 245764
  54.9 23.4 %copy-start.3 = (bf16[64,896]{1,0:T(8,128)(2,1)S(1)}, bf16[64,896]{1,0:T(8,128)(2,1)}, u32[]{:S(2)}) copy-start(bf16[64,896]{1,0:T(8,128)(2,1)} %param.14) | copy-start | bytes 344068
  55.0 42.4 %all-to-all-start = ((bf16[8,2,256,256]{3,2,1,0:T(8,128)(2,1)}), bf16[8,2,256,256]{3,2,1,0:T(8,128)(2,1)S(1)}, u32[]{:S(2)}, u32[]{:S(2)}) async-start(bf16[8,2,256,256]{3,2,1,0:T(8,128)(2,1)} %broadcast_select_fusion), calls=%async_computation | async-start | bytes 4194304 | tf_op jit(solution)/shard_map/all_to_all | solution.py:108
  62.7 96.7 %all-gather.4.cloned.1.call-start = ((), (), s32[]{:S(2)}) async-start(), calls=%async_computation.2 | async-start | bytes 1806336 | tf_op jit(solution)/shard_map/all_gather | solution.py:163
  63.3 140.5 %reduce-scatter.2.cloned.1.call-start = ((), (), s32[]{:S(2)}) async-start(), calls=%async_computation.3 | async-start | bytes 2064384 | tf_op jit(solution)/shard_map/reduce_scatter | solution.py:166
  73.3 24.0 %copy-start.2 = (bf16[320,128]{1,0:T(8,128)(2,1)}, bf16[320,128]{1,0:T(8,128)(2,1)S(1)}, u32[]{:S(2)}) copy-start(bf16[320,128]{1,0:T(8,128)(2,1)S(1)} %get-tuple-element.42) | copy-start | bytes 245764
  73.4 25.2 %copy-start.6 = (bf16[320,128]{1,0:T(8,128)(2,1)}, bf16[320,128]{1,0:T(8,128)(2,1)S(1)}, u32[]{:S(2)}) copy-start(bf16[320,128]{1,0:T(8,128)(2,1)S(1)} %get-tuple-element.43) | copy-start | bytes 245764
  136.3 27.0 %copy-start.11 = (bf16[512,112]{0,1:T(8,128)(2,1)S(1)}, bf16[512,112]{0,1:T(8,128)(2,1)}, u32[]{:S(2)}) copy-start(bf16[512,112]{0,1:T(8,128)(2,1)} %param.22) | copy-start | bytes 344068
  163.3 27.9 %collective-permute-start = (bf16[512,112]{0,1:T(8,128)(2,1)S(1)}, bf16[512,112]{0,1:T(8,128)(2,1)S(1)}, u32[]{:S(2)}, u32[]{:S(2)}) collective-permute-start(bf16[512,112]{0,1:T(8,128)(2,1)S(1)} %copy-done.11), channel_id=1, source_target_pairs={{0,0},{1,64},{2,128},{3,192},{4,256},{5,320},{6,384},{7,448},{64,1... | collective-permute-start | bytes 344072 | tf_op jit(solution)/shard_map/ppermute | solution.py:162
  204.7 28.3 %collective-permute-start.1 = (bf16[512,112]{0,1:T(8,128)(2,1)S(1)}, bf16[512,112]{0,1:T(8,128)(2,1)S(1)}, u32[]{:S(2)}, u32[]{:S(2)}) collective-permute-start(bf16[512,112]{0,1:T(8,128)(2,1)S(1)} %add_convert_fusion), channel_id=1, source_target_pairs={{0,0},{1,64},{2,128},{3,192},{4,256},{5,320},{6,384},{7,448},{64,1... | collective-permute-start | bytes 344072 | tf_op jit(solution)/shard_map/ppermute | solution.py:168
Sparse Core Ops, SparseCore 0:
  10.9 40.3 all-gather.5
  163.4 40.3 reduce-scatter.1
Sparse Core Ops, SparseCore 1:
  66.4 93.0 all-gather.3

commit v3 on v2

--- a/solution.py
+++ b/solution.py
@@ -91,21 +91,21 @@
     kv_width = kv_heads * width
     shared_count = ROOTS + MIDS
 
+    tok_count = hi_count * lo_count
     my_pair = jnp.concatenate([shared_key_block, shared_value_block], axis=1)
-    row_pairs = lax.all_gather(my_pair, "lo", axis=0, tiled=False)
+    node_rows = my_pair.shape[0]
+    piece_rows = node_rows // tok_count
+    pieces = my_pair.reshape(tok_count, piece_rows, my_pair.shape[1])
+    spread = lax.all_to_all(pieces, ("hi", "lo"), 0, 0, tiled=True)
+    held = jnp.take(spread, node_owner[:shared_count], axis=0)
     requests = token_request.reshape(-1, tok_rows)[:, 0]
     middles = parents[shared_count + requests]
     roots = parents[middles]
-    root_owners = node_owner[roots]
-    middle_owners = node_owner[middles]
-    column = jnp.arange(hi_count) * lo_count + lo
-    wanted = jnp.stack(
-        [root_owners[column] % lo_count, middle_owners[column] % lo_count], axis=1
+    wanted = jnp.stack([roots, middles], axis=1)
+    outgoing = jnp.take(held, wanted.reshape(-1), axis=0).reshape(
+        (tok_count, 2, piece_rows, my_pair.shape[1])
     )
-    outgoing = jnp.take(row_pairs, wanted.reshape(-1), axis=0).reshape(
-        (hi_count, 2) + my_pair.shape
-    )
-    incoming = lax.all_to_all(outgoing, "hi", 0, 0, tiled=True)
+    incoming = lax.all_to_all(outgoing, ("hi", "lo"), 0, 0, tiled=True)
 
     query_turned = apply_rotary(queries, positions, q_heads)
     key_turned = apply_rotary(fresh_token_keys, positions, kv_heads)
@@ -133,11 +133,8 @@
         leaf_value_output.reshape(leaf_rows, kv_heads, width),
         leaf_row_mask,
     )
-    node_rows = shared_key_block.shape[0]
-    root_owner = lookup(node_owner, root)
-    middle_owner = lookup(node_owner, middle)
-    root_pair = lax.dynamic_index_in_dim(incoming, root_owner // lo_count, 0, keepdims=False)[0]
-    middle_pair = lax.dynamic_index_in_dim(incoming, middle_owner // lo_count, 0, keepdims=False)[1]
+    root_pair = incoming[:, 0].reshape(my_pair.shape)
+    middle_pair = incoming[:, 1].reshape(my_pair.shape)
     root_keys = root_pair[:, :kv_width]
     root_values = root_pair[:, kv_width:]
     middle_keys = middle_pair[:, :kv_width]

time: 242 us -> 186 us (0.77)
  the two profiles are of different devices: /device:TPU:110 before, /device:TPU:74 now
where the time goes in v3:
time: 186 us; the launch traced here: 185 us
  waiting for transfers between devices  85.5 us (46%)
  starting transfers between devices  34 us (18%)
  blocking collectives  21.7 us (12%)
  between operations  15.1 us (8%)
  other arithmetic  14.4 us (8%)
  local copies, waits for them, and re-layouts  9.24 us (5%)
  matrix products  5.45 us (3%)
    all_gather x1, blocking collectives, body(): token_block = lax.all_gather(attended_local, 'lo', axis=0, tiled=True)  21.7 us
    ppermute x1, waiting for transfers between devices, body(): residual_here = lax.ppermute(residual, ('hi', 'mlp'), swap)  20.5 us
    reduce_scatter x1, waiting for transfers between devices, body(): summed = lax.psum_scatter(projected, 'mlp', scatter_dimension=1, tiled=True)  18.9 us
    ppermute x1, waiting for transfers between devices, body(): hidden = lax.ppermute(result, ('hi', 'mlp'), swap)  18.1 us
    all_gather x1, waiting for transfers between devices, body(): weight_cols = lax.all_gather(out_weight, 'hi', axis=1, tiled=True)  16.7 us
    all_to_all x1, starting transfers between devices, body(): spread = lax.all_to_all(pieces, ('hi', 'lo'), 0, 0, tiled=True)  13.1 us
    all_to_all x1, waiting for transfers between devices, body(): incoming = lax.all_to_all(outgoing, ('hi', 'lo'), 0, 0, tiled=True)  10.5 us
    all_to_all x1, starting transfers between devices, body(): incoming = lax.all_to_all(outgoing, ('hi', 'lo'), 0, 0, tiled=True)  10.3 us
  transfers between devices with their start and end apart: 6, of which 5 were waited for; matrix products, arithmetic and copies ran while one was open for 11% of the time, Pallas kernels for 0%

profile of v3, /device:TPU:74, one launch (start us, length us, event | category | flops | bytes accessed | tf_op | source)
XLA Modules:
  0.0 185.4 jit_solution(10171692489538792480)
XLA Ops:
  7.2 0.9 pad_maximum_fusion
  8.1 0.7 reshape.310
  8.8 13.1 %all-to-all-start = ((bf16[64,4,256]{2,1,0:T(4,128)(2,1)}), bf16[64,4,256]{2,1,0:T(4,128)(2,1)S(1)}, u32[]{:S(2)}, u32[]{:S(2)}) async-start(bf16[64,4,256]{2,1,0:T(4,128)(2,1)} %reshape.310), calls=%async_computation | async-start | bytes 262144 | tf_op jit(solution)/shard_map/all_to_all | solution.py:99
  21.9 0.7 all-gather.2.cloned.1.call-update
  22.7 0.8 reshape.309
  23.5 1.3 dynamic_slice.3
  25.4 1.3 fusion.32
  26.7 1.9 %fusion.34 = s32[]{:T(128)} fusion(s32[74]{0:T(128)} %param.25, s32[]{:T(128)} %fusion.32), kind=kLoop, calls=%fused_computation.93 | loop fusion | flops 221 | bytes 304 | tf_op jit(solution)/shard_map/reduce_sum | solution.py:60
  28.6 2.7 %fusion.33 = (s32[]{:T(128)}, s32[]{:T(128)}, s32[]{:T(128)}) fusion(s32[74]{0:T(128)} %param.26, s32[]{:T(128)} %bitcast, s32[]{:T(128)} %fusion.34, s32[]{:T(128)} %fusion.32), kind=kLoop, calls=%fused_computation.92 | loop fusion | flops 663 | bytes 320 | tf_op jit(solution)/shard_map/reduce_sum | solution.py:60
  31.3 1.3 iota_compare_fusion.4
  32.6 2.0 %broadcast_add_fusion = (s32[64]{0:T(128)S(1)}, s32[64]{0:T(128)S(1)}, f32[64]{0:T(128)S(1)}) fusion(s32[]{:T(128)} %get-tuple-element.5, s32[64]{0:T(128)} %param.24, s32[]{:T(128)} %get-tuple-element.4), kind=kLoop, calls=%fused_computation.99 | loop fusion | flops 256 | bytes 1032 | tf_op jit(solution)/shard_map/add | solution.py:129
  34.7 1.0 reshape.319
  36.0 0.8 gather_fusion
  37.0 0.8 gather_fusion.1
  38.5 0.6 iota_compare_fusion.3
  39.7 0.6 gather_fusion.2
  40.4 0.8 gather_fusion.3
  41.2 0.9 broadcast_select_fusion
  42.2 10.3 %all-to-all-start.1 = ((bf16[64,2,4,256]{3,2,1,0:T(4,128)(2,1)}), bf16[64,2,4,256]{3,2,1,0:T(4,128)(2,1)S(1)}, u32[]{:S(2)}, u32[]{:S(2)}) async-start(bf16[64,2,4,256]{3,2,1,0:T(4,128)(2,1)} %broadcast_select_fusion), calls=%async_computation.1 | async-start | bytes 524288 | tf_op jit(solution)/shard_map/all_to_all | solution.py:108
  53.4 10.5 %all-to-all-done.1 = bf16[64,2,4,256]{3,2,1,0:T(4,128)(2,1)S(1)} async-done(((bf16[64,2,4,256]{3,2,1,0:T(4,128)(2,1)}), bf16[64,2,4,256]{3,2,1,0:T(4,128)(2,1)S(1)}, u32[]{:S(2)}, u32[]{:S(2)}) %all-to-all-start.1) | async-done | bytes 262176 | tf_op jit(solution)/shard_map/all_to_all | solution.py:108
  64.1 0.4 select_reduce_fusion
  65.6 21.7 %all_gather.6 = bf16[512,896]{1,0:T(8,128)(2,1)S(1)} all-gather(bf16[64,896]{1,0:T(8,128)(2,1)S(1)} %bitcast.70), channel_id=1, replica_groups=mesh['hi'=8,'lo'=8,'mlp'=8] {'lo'}, dimensions={0}, use_global_device_ids=true | all-gather | bytes 1032192 | tf_op jit(solution)/shard_map/all_gather | solution.py:161
  87.4 16.7 %all-gather.2.cloned.1.call-done = bf16[896,896]{0,1:T(8,128)(2,1)} async-done(((bf16[896,112]{0,1:T(8,128)(2,1)}), bf16[896,896]{0,1:T(8,128)(2,1)}) %all-gather.2.cloned.1.call-update) | async-done | bytes 1605648 | tf_op jit(solution)/shard_map/all_gather | solution.py:160
  104.1 3.8 %fusion.50 = f32[512,896]{0,1:T(8,128)} fusion(bf16[512,896]{1,0:T(8,128)(2,1)S(1)} %all_gather.6, bf16[896,896]{0,1:T(8,128)(2,1)} %all-gather.2.cloned.1.call-done), kind=kOutput, calls=%fused_computation.110 | convolution fusion | flops 822083584 | bytes 4358144 | tf_op jit(solution)/shard_map/dot_general | solution.py:162
  108.0 0.9 copy-done.7
  108.8 6.3 %collective-permute-start = (bf16[512,112]{0,1:T(8,128)(2,1)S(1)}, bf16[512,112]{0,1:T(8,128)(2,1)S(1)}, u32[]{:S(2)}, u32[]{:S(2)}) collective-permute-start(bf16[512,112]{0,1:T(8,128)(2,1)S(1)} %copy-done.7), channel_id=1, source_target_pairs={{0,0},{1,64},{2,128},{3,192},{4,256},{5,320},{6,384},{7,448},{64,1... | collective-permute-start | bytes 344072 | tf_op jit(solution)/shard_map/ppermute | solution.py:159
  115.1 20.5 %collective-permute-done = bf16[512,112]{0,1:T(8,128)(2,1)S(1)} collective-permute-done((bf16[512,112]{0,1:T(8,128)(2,1)S(1)}, bf16[512,112]{0,1:T(8,128)(2,1)S(1)}, u32[]{:S(2)}, u32[]{:S(2)}) %collective-permute-start) | collective-permute-done | bytes 114720 | tf_op jit(solution)/shard_map/ppermute | solution.py:159
  135.7 18.9 %reduce-scatter.2.cloned.1.call-done = f32[512,112]{0,1:T(8,128)} async-done(((f32[512,896]{0,1:T(8,128)}), f32[512,112]{0,1:T(8,128)}) %reduce-scatter.2.cloned.1.call-update) | async-done | bytes 229392 | tf_op jit(solution)/shard_map/reduce_scatter | solution.py:163
  154.6 1.0 add_convert_fusion
  155.6 4.2 %collective-permute-start.1 = (bf16[512,112]{0,1:T(8,128)(2,1)S(1)}, bf16[512,112]{0,1:T(8,128)(2,1)S(1)}, u32[]{:S(2)}, u32[]{:S(2)}) collective-permute-start(bf16[512,112]{0,1:T(8,128)(2,1)S(1)} %add_convert_fusion), channel_id=1, source_target_pairs={{0,0},{1,64},{2,128},{3,192},{4,256},{5,320},{6,384},{7,448},{64,1... | collective-permute-start | bytes 344072 | tf_op jit(solution)/shard_map/ppermute | solution.py:165
  159.7 18.1 %collective-permute-done.1 = bf16[512,112]{0,1:T(8,128)(2,1)S(1)} collective-permute-done((bf16[512,112]{0,1:T(8,128)(2,1)S(1)}, bf16[512,112]{0,1:T(8,128)(2,1)S(1)}, u32[]{:S(2)}, u32[]{:S(2)}) %collective-permute-start.1) | collective-permute-done | bytes 114720 | tf_op jit(solution)/shard_map/ppermute | solution.py:165
  177.9 0.6 copy.44
  (59 shorter events, 4.0 us)
Async XLA Ops:
  7.2 28.8 %copy-start = (s32[74]{0:T(128)S(1)}, s32[74]{0:T(128)}, u32[]{:S(2)}) copy-start(s32[74]{0:T(128)} %param.25) | copy-start | bytes 892
  8.7 29.3 %copy-start.8 = (s32[74]{0:T(128)S(1)}, s32[74]{0:T(128)}, u32[]{:S(2)}) copy-start(s32[74]{0:T(128)} %param.27) | copy-start | bytes 892
  8.7 29.3 %copy-start.5 = (bf16[64,128]{1,0:T(8,128)(2,1)S(1)}, bf16[64,128]{1,0:T(8,128)(2,1)}, u32[]{:S(2)}) copy-start(bf16[64,128]{1,0:T(8,128)(2,1)} %param.15) | copy-start | bytes 49156
  8.8 31.0 %all-to-all-start = ((bf16[64,4,256]{2,1,0:T(4,128)(2,1)}), bf16[64,4,256]{2,1,0:T(4,128)(2,1)S(1)}, u32[]{:S(2)}, u32[]{:S(2)}) async-start(bf16[64,4,256]{2,1,0:T(4,128)(2,1)} %reshape.310), calls=%async_computation | async-start | bytes 262144 | tf_op jit(solution)/shard_map/all_to_all | solution.py:99
  21.9 17.3 %copy-start.6 = (bf16[64,128]{1,0:T(8,128)(2,1)S(1)}, bf16[64,128]{1,0:T(8,128)(2,1)}, u32[]{:S(2)}) copy-start(bf16[64,128]{1,0:T(8,128)(2,1)} %param.16) | copy-start | bytes 49156
  21.9 82.2 %all-gather.2.cloned.1.call-start = ((), (), s32[]{:S(2)}) async-start(), calls=%async_computation.3 | async-start | bytes 1806336 | tf_op jit(solution)/shard_map/all_gather | solution.py:160
  22.6 16.7 %copy-start.2 = (bf16[320,128]{1,0:T(8,128)(2,1)S(1)}, bf16[320,128]{1,0:T(8,128)(2,1)}, u32[]{:S(2)}) copy-start(bf16[320,128]{1,0:T(8,128)(2,1)} %param.18) | copy-start | bytes 245764
  22.6 16.7 %copy-start.3 = (bf16[320,128]{1,0:T(8,128)(2,1)S(1)}, bf16[320,128]{1,0:T(8,128)(2,1)}, u32[]{:S(2)}) copy-start(bf16[320,128]{1,0:T(8,128)(2,1)} %param.17) | copy-start | bytes 245764
  39.5 13.6 %copy-start.1 = (bf16[320,128]{1,0:T(8,128)(2,1)}, bf16[320,128]{1,0:T(8,128)(2,1)S(1)}, u32[]{:S(2)}) copy-start(bf16[320,128]{1,0:T(8,128)(2,1)S(1)} %get-tuple-element.42) | copy-start | bytes 245764
  39.5 25.7 %copy-start.4 = (bf16[320,128]{1,0:T(8,128)(2,1)}, bf16[320,128]{1,0:T(8,128)(2,1)S(1)}, u32[]{:S(2)}) copy-start(bf16[320,128]{1,0:T(8,128)(2,1)S(1)} %get-tuple-element.43) | copy-start | bytes 245764
  42.2 21.7 %all-to-all-start.1 = ((bf16[64,2,4,256]{3,2,1,0:T(4,128)(2,1)}), bf16[64,2,4,256]{3,2,1,0:T(4,128)(2,1)S(1)}, u32[]{:S(2)}, u32[]{:S(2)}) async-start(bf16[64,2,4,256]{3,2,1,0:T(4,128)(2,1)} %broadcast_select_fusion), calls=%async_computation.1 | async-start | bytes 524288 | tf_op jit(solution)/shard_map/all_to_all | solution.py:108
  52.5 102.1 %reduce-scatter.2.cloned.1.call-start = ((), (), s32[]{:S(2)}) async-start(), calls=%async_computation.4 | async-start | bytes 2064384 | tf_op jit(solution)/shard_map/reduce_scatter | solution.py:163
  107.9 0.9 copy-start.7
  108.8 26.8 %collective-permute-start = (bf16[512,112]{0,1:T(8,128)(2,1)S(1)}, bf16[512,112]{0,1:T(8,128)(2,1)S(1)}, u32[]{:S(2)}, u32[]{:S(2)}) collective-permute-start(bf16[512,112]{0,1:T(8,128)(2,1)S(1)} %copy-done.7), channel_id=1, source_target_pairs={{0,0},{1,64},{2,128},{3,192},{4,256},{5,320},{6,384},{7,448},{64,1... | collective-permute-start | bytes 344072 | tf_op jit(solution)/shard_map/ppermute | solution.py:159
  155.6 22.3 %collective-permute-start.1 = (bf16[512,112]{0,1:T(8,128)(2,1)S(1)}, bf16[512,112]{0,1:T(8,128)(2,1)S(1)}, u32[]{:S(2)}, u32[]{:S(2)}) collective-permute-start(bf16[512,112]{0,1:T(8,128)(2,1)S(1)} %add_convert_fusion), channel_id=1, source_target_pairs={{0,0},{1,64},{2,128},{3,192},{4,256},{5,320},{6,384},{7,448},{64,1... | collective-permute-start | bytes 344072 | tf_op jit(solution)/shard_map/ppermute | solution.py:165
Sparse Core Ops, SparseCore 0:
  25.9 78.1 all-gather.1
  108.1 46.4 reduce-scatter.1

commit v4 on v3

--- a/solution.py
+++ b/solution.py
@@ -107,6 +107,11 @@
     )
     incoming = lax.all_to_all(outgoing, ("hi", "lo"), 0, 0, tiled=True)
 
+    swap = [
+        (h * mlp_count + m, m * mlp_count + h) for h in range(hi_count) for m in range(mlp_count)
+    ]
+    residual_here = lax.ppermute(residual, ("hi", "mlp"), swap)
+    residual_here, queries = lax.optimization_barrier((residual_here, queries))
     query_turned = apply_rotary(queries, positions, q_heads)
     key_turned = apply_rotary(fresh_token_keys, positions, kv_heads)
     my_request = lax.dynamic_slice_in_dim(token_request, my_index * tok_rows, 1)[0]
@@ -153,13 +158,11 @@
         (final[2] / final[1][..., None]).reshape(tok_rows, q_heads * width).astype(jnp.bfloat16)
     )
 
-    swap = [
-        (h * mlp_count + m, m * mlp_count + h) for h in range(hi_count) for m in range(mlp_count)
-    ]
-    residual_here = lax.ppermute(residual, ("hi", "mlp"), swap)
     weight_cols = lax.all_gather(out_weight, "hi", axis=1, tiled=True)
     token_block = lax.all_gather(attended_local, "lo", axis=0, tiled=True)
-    projected = jnp.dot(token_block, weight_cols, preferred_element_type=jnp.float32)
+    projected = jnp.dot(token_block, weight_cols, preferred_element_type=jnp.float32).astype(
+        jnp.bfloat16
+    )
     summed = lax.psum_scatter(projected, "mlp", scatter_dimension=1, tiled=True)
     result = (residual_here.astype(jnp.float32) + summed).astype(jnp.bfloat16)
     hidden = lax.ppermute(result, ("hi", "mlp"), swap)

time: 186 us -> 186 us (level)
  the two profiles are of different devices: /device:TPU:74 before, /device:TPU:30 now
where the time goes in v4:
time: 186 us
  waiting for transfers between devices  78.8 us (42%)
  starting transfers between devices  41.8 us (22%)
  blocking collectives  22.6 us (12%)
  between operations  15.1 us (8%)
  other arithmetic  14.2 us (8%)
  local copies, waits for them, and re-layouts  8.1 us (4%)
  matrix products  5.11 us (3%)
    reduce_scatter x1, waiting for transfers between devices, body(): summed = lax.psum_scatter(projected, 'mlp', scatter_dimension=1, tiled=True)  40.6 us
    all_gather x1, blocking collectives, body(): token_block = lax.all_gather(attended_local, 'lo', axis=0, tiled=True)  22.6 us
    ppermute x1, waiting for transfers between devices, body(): hidden = lax.ppermute(result, ('hi', 'mlp'), swap)  16 us
    ppermute x1, starting transfers between devices, body(): residual_here = lax.ppermute(residual, ('hi', 'mlp'), swap)  14.3 us
    all_gather x1, waiting for transfers between devices, body(): weight_cols = lax.all_gather(out_weight, 'hi', axis=1, tiled=True)  10.8 us
    all_to_all x1, waiting for transfers between devices, body(): incoming = lax.all_to_all(outgoing, ('hi', 'lo'), 0, 0, tiled=True)  10.7 us
    all_to_all x1, starting transfers between devices, body(): incoming = lax.all_to_all(outgoing, ('hi', 'lo'), 0, 0, tiled=True)  10.3 us
    ppermute x1, starting transfers between devices, body(): hidden = lax.ppermute(result, ('hi', 'mlp'), swap)  9.02 us
  transfers between devices with their start and end apart: 6, of which 4 were waited for; matrix products, arithmetic and copies ran while one was open for 12% of the time, Pallas kernels for 0%

profile of v4, /device:TPU:30, one launch (start us, length us, event | category | flops | bytes accessed | tf_op | source)
XLA Modules:
  0.0 185.7 jit_solution(15077562899353103600)
XLA Ops:
  7.2 14.3 %collective-permute-start = (bf16[512,112]{0,1:T(8,128)(2,1)}, bf16[512,112]{0,1:T(8,128)(2,1)S(1)}, u32[]{:S(2)}, u32[]{:S(2)}) collective-permute-start(bf16[512,112]{0,1:T(8,128)(2,1)} %param.22), channel_id=1, source_target_pairs={{0,0},{1,64},{2,128},{3,192},{4,256},{5,320},{6,384},{7,448},{64,1... | collective-permute-start | bytes 344072 | tf_op jit(solution)/shard_map/ppermute | solution.py:113
  21.6 0.9 pad_maximum_fusion
  22.5 0.7 reshape.310
  23.2 8.0 %all-to-all-start = ((bf16[64,4,256]{2,1,0:T(4,128)(2,1)}), bf16[64,4,256]{2,1,0:T(4,128)(2,1)S(1)}, u32[]{:S(2)}, u32[]{:S(2)}) async-start(bf16[64,4,256]{2,1,0:T(4,128)(2,1)} %reshape.310), calls=%async_computation | async-start | bytes 262144 | tf_op jit(solution)/shard_map/all_to_all | solution.py:99
  31.2 0.7 all-gather.2.cloned.1.call-update
  31.9 0.8 reshape.309
  32.7 1.3 dynamic_slice.3
  34.7 1.3 fusion.32
  35.9 1.9 %fusion.34 = s32[]{:T(128)} fusion(s32[74]{0:T(128)} %param.25, s32[]{:T(128)} %fusion.32), kind=kLoop, calls=%fused_computation.94 | loop fusion | flops 221 | bytes 304 | tf_op jit(solution)/shard_map/reduce_sum | solution.py:60
  37.9 2.6 %fusion.33 = (s32[]{:T(128)}, s32[]{:T(128)}, s32[]{:T(128)}) fusion(s32[74]{0:T(128)} %param.26, s32[]{:T(128)} %bitcast, s32[]{:T(128)} %fusion.34, s32[]{:T(128)} %fusion.32), kind=kLoop, calls=%fused_computation.93 | loop fusion | flops 663 | bytes 320 | tf_op jit(solution)/shard_map/reduce_sum | solution.py:60
  40.5 1.2 iota_compare_fusion.4
  41.7 1.9 %broadcast_add_fusion = (s32[64]{0:T(128)S(1)}, s32[64]{0:T(128)S(1)}, f32[64]{0:T(128)S(1)}) fusion(s32[]{:T(128)} %get-tuple-element.9, s32[64]{0:T(128)} %param.24, s32[]{:T(128)} %get-tuple-element.8), kind=kLoop, calls=%fused_computation.100 | loop fusion | flops 256 | bytes 1032 | tf_op jit(solution)/shard_map/add | solution.py:134
  43.8 1.4 gather_fusion
  45.4 0.8 gather_fusion.1
  47.0 0.7 iota_compare_fusion.3
  48.6 0.6 gather_fusion.2
  49.3 0.8 gather_fusion.3
  50.1 0.9 broadcast_select_fusion
  51.1 10.3 %all-to-all-start.1 = ((bf16[64,2,4,256]{3,2,1,0:T(4,128)(2,1)}), bf16[64,2,4,256]{3,2,1,0:T(4,128)(2,1)S(1)}, u32[]{:S(2)}, u32[]{:S(2)}) async-start(bf16[64,2,4,256]{3,2,1,0:T(4,128)(2,1)} %broadcast_select_fusion), calls=%async_computation.1 | async-start | bytes 524288 | tf_op jit(solution)/shard_map/all_to_all | solution.py:108
  61.6 0.4 select_reduce_fusion.1
  62.3 10.7 %all-to-all-done.1 = bf16[64,2,4,256]{3,2,1,0:T(4,128)(2,1)S(1)} async-done(((bf16[64,2,4,256]{3,2,1,0:T(4,128)(2,1)}), bf16[64,2,4,256]{3,2,1,0:T(4,128)(2,1)S(1)}, u32[]{:S(2)}, u32[]{:S(2)}) %all-to-all-start.1) | async-done | bytes 262176 | tf_op jit(solution)/shard_map/all_to_all | solution.py:108
  73.2 0.4 select_reduce_fusion
  73.6 0.3 convert_reduce_fusion
  74.0 0.3 fusion.5
  74.7 22.6 %all_gather.6 = bf16[512,896]{1,0:T(8,128)(2,1)S(1)} all-gather(bf16[64,896]{1,0:T(8,128)(2,1)S(1)} %bitcast.70), channel_id=1, replica_groups=mesh['hi'=8,'lo'=8,'mlp'=8] {'lo'}, dimensions={0}, use_global_device_ids=true | all-gather | bytes 1032192 | tf_op jit(solution)/shard_map/all_gather | solution.py:162
  97.3 10.8 %all-gather.2.cloned.1.call-done = bf16[896,896]{0,1:T(8,128)(2,1)} async-done(((bf16[896,112]{0,1:T(8,128)(2,1)}), bf16[896,896]{0,1:T(8,128)(2,1)}) %all-gather.2.cloned.1.call-update) | async-done | bytes 1605648 | tf_op jit(solution)/shard_map/all_gather | solution.py:161
  108.2 3.5 %convolution_convert_fusion = bf16[512,896]{0,1:T(8,128)(2,1)} fusion(bf16[512,896]{1,0:T(8,128)(2,1)S(1)} %all_gather.6, bf16[896,896]{0,1:T(8,128)(2,1)} %all-gather.2.cloned.1.call-done), kind=kOutput, calls=%fused_computation.4 | convolution fusion | flops 822542336 | bytes 3440640 | tf_op jit(solution)/shard_map/dot_general | solution.py:163
  111.7 40.6 %reduce-scatter.2.cloned.1.call-done = bf16[512,112]{0,1:T(8,128)(2,1)} async-done(((bf16[512,896]{0,1:T(8,128)(2,1)}), bf16[512,112]{0,1:T(8,128)(2,1)}) %reduce-scatter.2.cloned.1.call-update) | async-done | bytes 114704 | tf_op jit(solution)/shard_map/reduce_scatter | solution.py:166
  152.3 0.9 add_convert_fusion
  153.2 9.0 %collective-permute-start.1 = (bf16[512,112]{0,1:T(8,128)(2,1)S(1)}, bf16[512,112]{0,1:T(8,128)(2,1)S(1)}, u32[]{:S(2)}, u32[]{:S(2)}) collective-permute-start(bf16[512,112]{0,1:T(8,128)(2,1)S(1)} %add_convert_fusion), channel_id=1, source_target_pairs={{0,0},{1,64},{2,128},{3,192},{4,256},{5,320},{6,384},{7,448},{64,1... | collective-permute-start | bytes 344072 | tf_op jit(solution)/shard_map/ppermute | solution.py:168
  162.2 16.0 %collective-permute-done.1 = bf16[512,112]{0,1:T(8,128)(2,1)S(1)} collective-permute-done((bf16[512,112]{0,1:T(8,128)(2,1)S(1)}, bf16[512,112]{0,1:T(8,128)(2,1)S(1)}, u32[]{:S(2)}, u32[]{:S(2)}) %collective-permute-start.1) | collective-permute-done | bytes 114720 | tf_op jit(solution)/shard_map/ppermute | solution.py:168
  178.2 0.6 copy.44
  (59 shorter events, 3.1 us)
Async XLA Ops:
  7.2 38.3 %copy-start = (s32[74]{0:T(128)S(1)}, s32[74]{0:T(128)}, u32[]{:S(2)}) copy-start(s32[74]{0:T(128)} %param.25) | copy-start | bytes 892
  7.2 39.3 %copy-start.8 = (s32[74]{0:T(128)S(1)}, s32[74]{0:T(128)}, u32[]{:S(2)}) copy-start(s32[74]{0:T(128)} %param.27) | copy-start | bytes 892
  7.2 39.3 %copy-start.6 = (bf16[64,128]{1,0:T(8,128)(2,1)S(1)}, bf16[64,128]{1,0:T(8,128)(2,1)}, u32[]{:S(2)}) copy-start(bf16[64,128]{1,0:T(8,128)(2,1)} %param.15) | copy-start | bytes 49156
  7.2 40.6 %copy-start.7 = (bf16[64,128]{1,0:T(8,128)(2,1)S(1)}, bf16[64,128]{1,0:T(8,128)(2,1)}, u32[]{:S(2)}) copy-start(bf16[64,128]{1,0:T(8,128)(2,1)} %param.16) | copy-start | bytes 49156
  7.2 40.8 %copy-start.4 = (bf16[320,128]{1,0:T(8,128)(2,1)S(1)}, bf16[320,128]{1,0:T(8,128)(2,1)}, u32[]{:S(2)}) copy-start(bf16[320,128]{1,0:T(8,128)(2,1)} %param.17) | copy-start | bytes 245764
  7.2 40.8 %copy-start.3 = (bf16[320,128]{1,0:T(8,128)(2,1)S(1)}, bf16[320,128]{1,0:T(8,128)(2,1)}, u32[]{:S(2)}) copy-start(bf16[320,128]{1,0:T(8,128)(2,1)} %param.18) | copy-start | bytes 245764
  7.2 41.1 %copy-start.2 = (bf16[64,896]{1,0:T(8,128)(2,1)S(1)}, bf16[64,896]{1,0:T(8,128)(2,1)}, u32[]{:S(2)}) copy-start(bf16[64,896]{1,0:T(8,128)(2,1)} %param.14) | copy-start | bytes 344068
  7.2 41.1 %collective-permute-start = (bf16[512,112]{0,1:T(8,128)(2,1)}, bf16[512,112]{0,1:T(8,128)(2,1)S(1)}, u32[]{:S(2)}, u32[]{:S(2)}) collective-permute-start(bf16[512,112]{0,1:T(8,128)(2,1)} %param.22), channel_id=1, source_target_pairs={{0,0},{1,64},{2,128},{3,192},{4,256},{5,320},{6,384},{7,448},{64,1... | collective-permute-start | bytes 344072 | tf_op jit(solution)/shard_map/ppermute | solution.py:113
  23.2 25.4 %all-to-all-start = ((bf16[64,4,256]{2,1,0:T(4,128)(2,1)}), bf16[64,4,256]{2,1,0:T(4,128)(2,1)S(1)}, u32[]{:S(2)}, u32[]{:S(2)}) async-start(bf16[64,4,256]{2,1,0:T(4,128)(2,1)} %reshape.310), calls=%async_computation | async-start | bytes 262144 | tf_op jit(solution)/shard_map/all_to_all | solution.py:99
  31.2 77.0 %all-gather.2.cloned.1.call-start = ((), (), s32[]{:S(2)}) async-start(), calls=%async_computation.3 | async-start | bytes 1806336 | tf_op jit(solution)/shard_map/all_gather | solution.py:161
  48.1 13.4 %copy-start.1 = (bf16[320,128]{1,0:T(8,128)(2,1)}, bf16[320,128]{1,0:T(8,128)(2,1)S(1)}, u32[]{:S(2)}) copy-start(bf16[320,128]{1,0:T(8,128)(2,1)S(1)} %get-tuple-element.46) | copy-start | bytes 245764
  48.1 26.1 %copy-start.5 = (bf16[320,128]{1,0:T(8,128)(2,1)}, bf16[320,128]{1,0:T(8,128)(2,1)S(1)}, u32[]{:S(2)}) copy-start(bf16[320,128]{1,0:T(8,128)(2,1)S(1)} %get-tuple-element.47) | copy-start | bytes 245764
  51.1 21.9 %all-to-all-start.1 = ((bf16[64,2,4,256]{3,2,1,0:T(4,128)(2,1)}), bf16[64,2,4,256]{3,2,1,0:T(4,128)(2,1)S(1)}, u32[]{:S(2)}, u32[]{:S(2)}) async-start(bf16[64,2,4,256]{3,2,1,0:T(4,128)(2,1)} %broadcast_select_fusion), calls=%async_computation.1 | async-start | bytes 524288 | tf_op jit(solution)/shard_map/all_to_all | solution.py:108
  61.4 90.9 %reduce-scatter.2.cloned.1.call-start = ((), (), s32[]{:S(2)}) async-start(), calls=%async_computation.4 | async-start | bytes 1032192 | tf_op jit(solution)/shard_map/reduce_scatter | solution.py:166
  153.2 25.0 %collective-permute-start.1 = (bf16[512,112]{0,1:T(8,128)(2,1)S(1)}, bf16[512,112]{0,1:T(8,128)(2,1)S(1)}, u32[]{:S(2)}, u32[]{:S(2)}) collective-permute-start(bf16[512,112]{0,1:T(8,128)(2,1)S(1)} %add_convert_fusion), channel_id=1, source_target_pairs={{0,0},{1,64},{2,128},{3,192},{4,256},{5,320},{6,384},{7,448},{64,1... | collective-permute-start | bytes 344072 | tf_op jit(solution)/shard_map/ppermute | solution.py:168
Sparse Core Ops, SparseCore 0:
  35.2 72.8 all-gather.1
  111.8 40.4 reduce-scatter.1

commit v5 on v4

--- a/solution.py
+++ b/solution.py
@@ -163,7 +163,9 @@
     projected = jnp.dot(token_block, weight_cols, preferred_element_type=jnp.float32).astype(
         jnp.bfloat16
     )
-    summed = lax.psum_scatter(projected, "mlp", scatter_dimension=1, tiled=True)
+    parts = projected.reshape(projected.shape[0], mlp_count, -1).transpose(1, 0, 2)
+    arrived = lax.all_to_all(parts, "mlp", 0, 0, tiled=True)
+    summed = jnp.sum(arrived.astype(jnp.float32), axis=0)
     result = (residual_here.astype(jnp.float32) + summed).astype(jnp.bfloat16)
     hidden = lax.ppermute(result, ("hi", "mlp"), swap)
     return (hidden, leaf_key_output, leaf_value_output)

time: 186 us -> 176 us (0.946)
  the two profiles are of different devices: /device:TPU:30 before, /device:TPU:90 now
where the time goes in v5:
time: 176 us; the launch traced here: 175 us
  blocking collectives  48.5 us (28%)
  waiting for transfers between devices  47.7 us (27%)
  starting transfers between devices  37.3 us (21%)
  between operations  15.1 us (9%)
  other arithmetic  13.4 us (8%)
  local copies, waits for them, and re-layouts  8.63 us (5%)
  matrix products  4.27 us (2%)
    all_to_all x1, blocking collectives, body(): arrived = lax.all_to_all(parts, 'mlp', 0, 0, tiled=True)  25.8 us
    all_gather x1, blocking collectives, body(): token_block = lax.all_gather(attended_local, 'lo', axis=0, tiled=True)  22.7 us
    ppermute x1, waiting for transfers between devices, body(): hidden = lax.ppermute(result, ('hi', 'mlp'), swap)  21 us
    all_gather x1, waiting for transfers between devices, body(): weight_cols = lax.all_gather(out_weight, 'hi', axis=1, tiled=True)  15.4 us
    all_to_all x1, starting transfers between devices, body(): spread = lax.all_to_all(pieces, ('hi', 'lo'), 0, 0, tiled=True)  11.3 us
    all_to_all x1, waiting for transfers between devices, body(): incoming = lax.all_to_all(outgoing, ('hi', 'lo'), 0, 0, tiled=True)  10.5 us
    all_to_all x1, starting transfers between devices, body(): incoming = lax.all_to_all(outgoing, ('hi', 'lo'), 0, 0, tiled=True)  10.3 us
    ppermute x1, starting transfers between devices, body(): residual_here = lax.ppermute(residual, ('hi', 'mlp'), swap)  10 us
  transfers between devices with their start and end apart: 5, of which 3 were waited for; matrix products, arithmetic and copies ran while one was open for 13% of the time, Pallas kernels for 0%

profile of v5, /device:TPU:90, one launch (start us, length us, event | category | flops | bytes accessed | tf_op | source)
XLA Modules:
  0.0 174.9 jit_solution(2024262684886347701)
XLA Ops:
  7.2 10.0 %collective-permute-start = (bf16[512,112]{0,1:T(8,128)(2,1)}, bf16[512,112]{0,1:T(8,128)(2,1)S(1)}, u32[]{:S(2)}, u32[]{:S(2)}) collective-permute-start(bf16[512,112]{0,1:T(8,128)(2,1)} %param.22), channel_id=1, source_target_pairs={{0,0},{1,64},{2,128},{3,192},{4,256},{5,320},{6,384},{7,448},{64,1... | collective-permute-start | bytes 344072 | tf_op jit(solution)/shard_map/ppermute | solution.py:113
  17.3 0.9 pad_maximum_fusion
  18.2 0.7 reshape.313
  18.9 11.3 %all-to-all-start = ((bf16[64,4,256]{2,1,0:T(4,128)(2,1)}), bf16[64,4,256]{2,1,0:T(4,128)(2,1)S(1)}, u32[]{:S(2)}, u32[]{:S(2)}) async-start(bf16[64,4,256]{2,1,0:T(4,128)(2,1)} %reshape.313), calls=%async_computation | async-start | bytes 262144 | tf_op jit(solution)/shard_map/all_to_all | solution.py:99
  30.2 0.7 all-gather.2.cloned.1.call-update
  30.9 0.8 reshape.312
  31.7 1.3 dynamic_slice.3
  33.6 1.3 fusion.32
  34.9 1.9 %fusion.34 = s32[]{:T(128)} fusion(s32[74]{0:T(128)} %param.25, s32[]{:T(128)} %fusion.32), kind=kLoop, calls=%fused_computation.95 | loop fusion | flops 221 | bytes 304 | tf_op jit(solution)/shard_map/reduce_sum | solution.py:60
  36.8 2.6 %fusion.33 = (s32[]{:T(128)}, s32[]{:T(128)}, s32[]{:T(128)}) fusion(s32[74]{0:T(128)} %param.26, s32[]{:T(128)} %bitcast, s32[]{:T(128)} %fusion.34, s32[]{:T(128)} %fusion.32), kind=kLoop, calls=%fused_computation.94 | loop fusion | flops 663 | bytes 320 | tf_op jit(solution)/shard_map/reduce_sum | solution.py:60
  39.5 1.2 iota_compare_fusion.4
  40.7 1.9 %broadcast_add_fusion = (s32[64]{0:T(128)S(1)}, s32[64]{0:T(128)S(1)}, f32[64]{0:T(128)S(1)}) fusion(s32[]{:T(128)} %get-tuple-element.9, s32[64]{0:T(128)} %param.24, s32[]{:T(128)} %get-tuple-element.8), kind=kLoop, calls=%fused_computation.101 | loop fusion | flops 256 | bytes 1032 | tf_op jit(solution)/shard_map/add | solution.py:134
  42.7 1.4 gather_fusion
  44.4 0.8 gather_fusion.1
  45.9 0.7 iota_compare_fusion.3
  47.6 0.6 gather_fusion.2
  48.2 0.8 gather_fusion.3
  49.1 0.9 broadcast_select_fusion
  50.0 10.3 %all-to-all-start.1 = ((bf16[64,2,4,256]{3,2,1,0:T(4,128)(2,1)}), bf16[64,2,4,256]{3,2,1,0:T(4,128)(2,1)S(1)}, u32[]{:S(2)}, u32[]{:S(2)}) async-start(bf16[64,2,4,256]{3,2,1,0:T(4,128)(2,1)} %broadcast_select_fusion), calls=%async_computation.1 | async-start | bytes 524288 | tf_op jit(solution)/shard_map/all_to_all | solution.py:108
  60.5 0.4 select_reduce_fusion.1
  61.2 10.5 %all-to-all-done.1 = bf16[64,2,4,256]{3,2,1,0:T(4,128)(2,1)S(1)} async-done(((bf16[64,2,4,256]{3,2,1,0:T(4,128)(2,1)}), bf16[64,2,4,256]{3,2,1,0:T(4,128)(2,1)S(1)}, u32[]{:S(2)}, u32[]{:S(2)}) %all-to-all-start.1) | async-done | bytes 262176 | tf_op jit(solution)/shard_map/all_to_all | solution.py:108
  71.9 0.4 select_reduce_fusion
  72.3 0.3 convert_reduce_fusion.1
  72.7 0.3 fusion.5
  73.5 22.7 %all_gather.6 = bf16[512,896]{1,0:T(8,128)(2,1)S(1)} all-gather(bf16[64,896]{1,0:T(8,128)(2,1)S(1)} %bitcast.74), channel_id=1, replica_groups=mesh['hi'=8,'lo'=8,'mlp'=8] {'lo'}, dimensions={0}, use_global_device_ids=true | all-gather | bytes 1032192 | tf_op jit(solution)/shard_map/all_gather | solution.py:162
  96.1 15.4 %all-gather.2.cloned.1.call-done = bf16[896,896]{0,1:T(8,128)(2,1)} async-done(((bf16[896,112]{0,1:T(8,128)(2,1)}), bf16[896,896]{0,1:T(8,128)(2,1)}) %all-gather.2.cloned.1.call-update) | async-done | bytes 1605648 | tf_op jit(solution)/shard_map/all_gather | solution.py:161
  111.6 2.6 %convolution_convert_fusion = bf16[512,896]{1,0:T(8,128)(2,1)S(1)} fusion(bf16[512,896]{1,0:T(8,128)(2,1)S(1)} %all_gather.6, bf16[896,896]{0,1:T(8,128)(2,1)} %all-gather.2.cloned.1.call-done), kind=kOutput, calls=%fused_computation.5 | convolution fusion | flops 822542336 | bytes 3440640 | tf_op jit(solution)/shard_map/dot_general | solution.py:163
  114.2 0.5 copy.35
  114.8 25.8 %all_to_all.15 = bf16[8,512,112]{1,2,0:T(8,128)(2,1)S(1)} all-to-all(bf16[8,512,112]{1,2,0:T(8,128)(2,1)S(1)} %bitcast.71), channel_id=1, replica_groups=mesh['hi'=8,'lo'=8,'mlp'=8] {'mlp'}, dimensions={0} | all-to-all | bytes 1835008 | tf_op jit(solution)/shard_map/all_to_all | solution.py:167
  140.7 5.7 %collective-permute-start.1 = (bf16[512,112]{0,1:T(8,128)(2,1)S(1)}, bf16[512,112]{0,1:T(8,128)(2,1)S(1)}, u32[]{:S(2)}, u32[]{:S(2)}) collective-permute-start(bf16[512,112]{0,1:T(8,128)(2,1)S(1)} %add_convert_fusion), channel_id=1, source_target_pairs={{0,0},{1,64},{2,128},{3,192},{4,256},{5,320},{6,384},{7,448},{64,1... | collective-permute-start | bytes 344072 | tf_op jit(solution)/shard_map/ppermute | solution.py:170
  146.4 21.0 %collective-permute-done.1 = bf16[512,112]{0,1:T(8,128)(2,1)S(1)} collective-permute-done((bf16[512,112]{0,1:T(8,128)(2,1)S(1)}, bf16[512,112]{0,1:T(8,128)(2,1)S(1)}, u32[]{:S(2)}, u32[]{:S(2)}) %collective-permute-start.1) | collective-permute-done | bytes 114720 | tf_op jit(solution)/shard_map/ppermute | solution.py:170
  167.4 0.6 copy.46
  (59 shorter events, 3.2 us)
Async XLA Ops:
  7.2 37.2 %copy-start = (s32[74]{0:T(128)S(1)}, s32[74]{0:T(128)}, u32[]{:S(2)}) copy-start(s32[74]{0:T(128)} %param.25) | copy-start | bytes 892
  7.2 38.3 %copy-start.8 = (s32[74]{0:T(128)S(1)}, s32[74]{0:T(128)}, u32[]{:S(2)}) copy-start(s32[74]{0:T(128)} %param.27) | copy-start | bytes 892
  7.2 38.3 %copy-start.6 = (bf16[64,128]{1,0:T(8,128)(2,1)S(1)}, bf16[64,128]{1,0:T(8,128)(2,1)}, u32[]{:S(2)}) copy-start(bf16[64,128]{1,0:T(8,128)(2,1)} %param.15) | copy-start | bytes 49156
  7.2 39.6 %copy-start.7 = (bf16[64,128]{1,0:T(8,128)(2,1)S(1)}, bf16[64,128]{1,0:T(8,128)(2,1)}, u32[]{:S(2)}) copy-start(bf16[64,128]{1,0:T(8,128)(2,1)} %param.16) | copy-start | bytes 49156
  7.2 39.7 %copy-start.4 = (bf16[320,128]{1,0:T(8,128)(2,1)S(1)}, bf16[320,128]{1,0:T(8,128)(2,1)}, u32[]{:S(2)}) copy-start(bf16[320,128]{1,0:T(8,128)(2,1)} %param.17) | copy-start | bytes 245764
  7.2 39.7 %copy-start.3 = (bf16[320,128]{1,0:T(8,128)(2,1)S(1)}, bf16[320,128]{1,0:T(8,128)(2,1)}, u32[]{:S(2)}) copy-start(bf16[320,128]{1,0:T(8,128)(2,1)} %param.18) | copy-start | bytes 245764
  7.2 40.0 %copy-start.2 = (bf16[64,896]{1,0:T(8,128)(2,1)S(1)}, bf16[64,896]{1,0:T(8,128)(2,1)}, u32[]{:S(2)}) copy-start(bf16[64,896]{1,0:T(8,128)(2,1)} %param.14) | copy-start | bytes 344068
  7.2 40.0 %collective-permute-start = (bf16[512,112]{0,1:T(8,128)(2,1)}, bf16[512,112]{0,1:T(8,128)(2,1)S(1)}, u32[]{:S(2)}, u32[]{:S(2)}) collective-permute-start(bf16[512,112]{0,1:T(8,128)(2,1)} %param.22), channel_id=1, source_target_pairs={{0,0},{1,64},{2,128},{3,192},{4,256},{5,320},{6,384},{7,448},{64,1... | collective-permute-start | bytes 344072 | tf_op jit(solution)/shard_map/ppermute | solution.py:113
  18.9 28.7 %all-to-all-start = ((bf16[64,4,256]{2,1,0:T(4,128)(2,1)}), bf16[64,4,256]{2,1,0:T(4,128)(2,1)S(1)}, u32[]{:S(2)}, u32[]{:S(2)}) async-start(bf16[64,4,256]{2,1,0:T(4,128)(2,1)} %reshape.313), calls=%async_computation | async-start | bytes 262144 | tf_op jit(solution)/shard_map/all_to_all | solution.py:99
  30.1 81.5 %all-gather.2.cloned.1.call-start = ((), (), s32[]{:S(2)}) async-start(), calls=%async_computation.3 | async-start | bytes 1806336 | tf_op jit(solution)/shard_map/all_gather | solution.py:161
  47.1 13.4 %copy-start.1 = (bf16[320,128]{1,0:T(8,128)(2,1)}, bf16[320,128]{1,0:T(8,128)(2,1)S(1)}, u32[]{:S(2)}) copy-start(bf16[320,128]{1,0:T(8,128)(2,1)S(1)} %get-tuple-element.46) | copy-start | bytes 245764
  47.1 25.9 %copy-start.5 = (bf16[320,128]{1,0:T(8,128)(2,1)}, bf16[320,128]{1,0:T(8,128)(2,1)S(1)}, u32[]{:S(2)}) copy-start(bf16[320,128]{1,0:T(8,128)(2,1)S(1)} %get-tuple-element.47) | copy-start | bytes 245764
  50.0 21.7 %all-to-all-start.1 = ((bf16[64,2,4,256]{3,2,1,0:T(4,128)(2,1)}), bf16[64,2,4,256]{3,2,1,0:T(4,128)(2,1)S(1)}, u32[]{:S(2)}, u32[]{:S(2)}) async-start(bf16[64,2,4,256]{3,2,1,0:T(4,128)(2,1)} %broadcast_select_fusion), calls=%async_computation.1 | async-start | bytes 524288 | tf_op jit(solution)/shard_map/all_to_all | solution.py:108
  140.7 26.7 %collective-permute-start.1 = (bf16[512,112]{0,1:T(8,128)(2,1)S(1)}, bf16[512,112]{0,1:T(8,128)(2,1)S(1)}, u32[]{:S(2)}, u32[]{:S(2)}) collective-permute-start(bf16[512,112]{0,1:T(8,128)(2,1)S(1)} %add_convert_fusion), channel_id=1, source_target_pairs={{0,0},{1,64},{2,128},{3,192},{4,256},{5,320},{6,384},{7,448},{64,1... | collective-permute-start | bytes 344072 | tf_op jit(solution)/shard_map/ppermute | solution.py:170
Sparse Core Ops, SparseCore 0:
  34.2 77.3 all-gather.1

commit v6 on v4

--- a/solution.py
+++ b/solution.py
@@ -107,11 +107,6 @@
     )
     incoming = lax.all_to_all(outgoing, ("hi", "lo"), 0, 0, tiled=True)
 
-    swap = [
-        (h * mlp_count + m, m * mlp_count + h) for h in range(hi_count) for m in range(mlp_count)
-    ]
-    residual_here = lax.ppermute(residual, ("hi", "mlp"), swap)
-    residual_here, queries = lax.optimization_barrier((residual_here, queries))
     query_turned = apply_rotary(queries, positions, q_heads)
     key_turned = apply_rotary(fresh_token_keys, positions, kv_heads)
     my_request = lax.dynamic_slice_in_dim(token_request, my_index * tok_rows, 1)[0]
@@ -163,9 +158,18 @@
     projected = jnp.dot(token_block, weight_cols, preferred_element_type=jnp.float32).astype(
         jnp.bfloat16
     )
-    summed = lax.psum_scatter(projected, "mlp", scatter_dimension=1, tiled=True)
-    result = (residual_here.astype(jnp.float32) + summed).astype(jnp.bfloat16)
-    hidden = lax.ppermute(result, ("hi", "mlp"), swap)
+    sub_width = projected.shape[1] // mlp_count
+    summed = jnp.zeros((projected.shape[0], sub_width), jnp.float32)
+    for shift in range(mlp_count):
+        target = (mlp + shift) % mlp_count
+        piece = lax.dynamic_slice_in_dim(projected, target * sub_width, sub_width, 1)
+        route = [
+            (h * mlp_count + m, ((m + shift) % mlp_count) * mlp_count + h)
+            for h in range(hi_count)
+            for m in range(mlp_count)
+        ]
+        summed = summed + lax.ppermute(piece, ("hi", "mlp"), route).astype(jnp.float32)
+    hidden = (residual.astype(jnp.float32) + summed).astype(jnp.bfloat16)
     return (hidden, leaf_key_output, leaf_value_output)
 
 

time: 186 us -> 305 us (1.64)
  the two profiles are of different devices: /device:TPU:30 before, /device:TPU:388 now
where the time goes in v6:
time: 305 us; the launch traced here: 304 us
  starting transfers between devices  186 us (61%)
  waiting for transfers between devices  61.3 us (20%)
  blocking collectives  16.9 us (6%)
  between operations  15.4 us (5%)
  other arithmetic  10.7 us (4%)
  local copies, waits for them, and re-layouts  8.82 us (3%)
  matrix products  4.27 us (1%)
    ppermute x8, starting transfers between devices, body(): lax.ppermute(piece, ('hi', 'mlp'), route).astype(jnp.float32)  167 us
    ppermute x8, waiting for transfers between devices, body(): lax.ppermute(piece, ('hi', 'mlp'), route).astype(jnp.float32)  29.5 us
    all_gather x1, waiting for transfers between devices, body(): weight_cols = lax.all_gather(out_weight, 'hi', axis=1, tiled=True)  22.7 us
    all_gather x1, blocking collectives, body(): token_block = lax.all_gather(attended_local, 'lo', axis=0, tiled=True)  16.9 us
    all_to_all x1, starting transfers between devices, body(): incoming = lax.all_to_all(outgoing, ('hi', 'lo'), 0, 0, tiled=True)  10.3 us
    all_to_all x1, starting transfers between devices, body(): spread = lax.all_to_all(pieces, ('hi', 'lo'), 0, 0, tiled=True)  8.69 us
    all_to_all x1, waiting for transfers between devices, body(): incoming = lax.all_to_all(outgoing, ('hi', 'lo'), 0, 0, tiled=True)  8.42 us
  transfers between devices with their start and end apart: 11, of which 5 were waited for; matrix products, arithmetic and copies ran while one was open for 6% of the time, Pallas kernels for 0%

profile of v6, /device:TPU:388, one launch (start us, length us, event | category | flops | bytes accessed | tf_op | source)
XLA Modules:
  0.0 303.9 jit_solution(10436807851796097243)
XLA Ops:
  7.2 0.9 pad_maximum_fusion
  8.1 0.7 reshape.310
  8.8 8.7 %all-to-all-start = ((bf16[64,4,256]{2,1,0:T(4,128)(2,1)}), bf16[64,4,256]{2,1,0:T(4,128)(2,1)S(1)}, u32[]{:S(2)}, u32[]{:S(2)}) async-start(bf16[64,4,256]{2,1,0:T(4,128)(2,1)} %reshape.310), calls=%async_computation | async-start | bytes 262144 | tf_op jit(solution)/shard_map/all_to_all | solution.py:99
  17.6 0.7 all-gather.2.cloned.1.call-update
  18.3 0.8 reshape.309
  19.2 1.4 gather_fusion
  20.9 0.8 gather_fusion.1
  21.7 1.3 dynamic_slice.27
  24.3 1.3 fusion.34
  25.5 2.0 fusion.33
  27.5 1.2 iota_compare_fusion.4
  28.7 1.2 broadcast_add_fusion
  30.9 0.7 iota_compare_fusion.3
  33.0 0.8 gather_fusion.3
  33.9 0.9 broadcast_select_fusion
  34.8 10.3 %all-to-all-start.1 = ((bf16[64,2,4,256]{3,2,1,0:T(4,128)(2,1)}), bf16[64,2,4,256]{3,2,1,0:T(4,128)(2,1)S(1)}, u32[]{:S(2)}, u32[]{:S(2)}) async-start(bf16[64,2,4,256]{3,2,1,0:T(4,128)(2,1)} %broadcast_select_fusion), calls=%async_computation.1 | async-start | bytes 524288 | tf_op jit(solution)/shard_map/all_to_all | solution.py:108
  46.0 8.4 %all-to-all-done.1 = bf16[64,2,4,256]{3,2,1,0:T(4,128)(2,1)S(1)} async-done(((bf16[64,2,4,256]{3,2,1,0:T(4,128)(2,1)}), bf16[64,2,4,256]{3,2,1,0:T(4,128)(2,1)S(1)}, u32[]{:S(2)}, u32[]{:S(2)}) %all-to-all-start.1) | async-done | bytes 262176 | tf_op jit(solution)/shard_map/all_to_all | solution.py:108
  56.2 16.9 %all_gather.6 = bf16[512,896]{1,0:T(8,128)(2,1)S(1)} all-gather(bf16[64,896]{1,0:T(8,128)(2,1)S(1)} %bitcast.70), channel_id=1, replica_groups=mesh['hi'=8,'lo'=8,'mlp'=8] {'lo'}, dimensions={0}, use_global_device_ids=true | all-gather | bytes 1032192 | tf_op jit(solution)/shard_map/all_gather | solution.py:157
  73.1 22.7 %all-gather.2.cloned.1.call-done = bf16[896,896]{0,1:T(8,128)(2,1)} async-done(((bf16[896,112]{0,1:T(8,128)(2,1)}), bf16[896,896]{0,1:T(8,128)(2,1)}) %all-gather.2.cloned.1.call-update) | async-done | bytes 1605648 | tf_op jit(solution)/shard_map/all_gather | solution.py:156
  95.8 2.6 convolution_convert_fusion
  99.0 10.7 %collective-permute-start = (bf16[512,112]{1,0:T(8,128)(2,1)S(1)}, bf16[512,112]{1,0:T(8,128)(2,1)S(1)}, u32[]{:S(2)}, u32[]{:S(2)}) collective-permute-start(bf16[512,112]{1,0:T(8,128)(2,1)S(1)} %get-tuple-element.22), channel_id=1, source_target_pairs={{0,0},{1,64},{2,128},{3,192},{4,256},{5,320},{6,384},{7,448},{64,1... | collective-permute-start | bytes 344072 | tf_op jit(solution)/shard_map/ppermute | solution.py:171
  109.6 1.9 collective-permute-start.1
  111.6 8.9 %collective-permute-start.2 = (bf16[512,112]{1,0:T(8,128)(2,1)S(1)}, bf16[512,112]{1,0:T(8,128)(2,1)S(1)}, u32[]{:S(2)}, u32[]{:S(2)}) collective-permute-start(bf16[512,112]{1,0:T(8,128)(2,1)S(1)} %get-tuple-element.28), channel_id=1, source_target_pairs={{0,128},{1,192},{2,256},{3,320},{4,384},{5,448},{6,0},{7,64},{64,1... | collective-permute-start | bytes 344072 | tf_op jit(solution)/shard_map/ppermute | solution.py:171
  120.5 6.6 %collective-permute-start.3 = (bf16[512,112]{1,0:T(8,128)(2,1)S(1)}, bf16[512,112]{1,0:T(8,128)(2,1)S(1)}, u32[]{:S(2)}, u32[]{:S(2)}) collective-permute-start(bf16[512,112]{1,0:T(8,128)(2,1)S(1)} %get-tuple-element.27), channel_id=1, source_target_pairs={{0,192},{1,256},{2,320},{3,384},{4,448},{5,0},{6,64},{7,128},{64,1... | collective-permute-start | bytes 344072 | tf_op jit(solution)/shard_map/ppermute | solution.py:171
  127.1 5.7 %collective-permute-start.4 = (bf16[512,112]{1,0:T(8,128)(2,1)S(1)}, bf16[512,112]{1,0:T(8,128)(2,1)S(1)}, u32[]{:S(2)}, u32[]{:S(2)}) collective-permute-start(bf16[512,112]{1,0:T(8,128)(2,1)S(1)} %get-tuple-element.26), channel_id=1, source_target_pairs={{0,256},{1,320},{2,384},{3,448},{4,0},{5,64},{6,128},{7,192},{64,2... | collective-permute-start | bytes 344072 | tf_op jit(solution)/shard_map/ppermute | solution.py:171
  132.8 1.9 collective-permute-start.5
  134.7 15.3 %collective-permute-done.1 = bf16[512,112]{1,0:T(8,128)(2,1)S(1)} collective-permute-done((bf16[512,112]{1,0:T(8,128)(2,1)S(1)}, bf16[512,112]{1,0:T(8,128)(2,1)S(1)}, u32[]{:S(2)}, u32[]{:S(2)}) %collective-permute-start.1) | collective-permute-done | bytes 114720 | tf_op jit(solution)/shard_map/ppermute | solution.py:171
  150.0 129.8 %collective-permute-start.6 = (bf16[512,112]{1,0:T(8,128)(2,1)S(1)}, bf16[512,112]{1,0:T(8,128)(2,1)S(1)}, u32[]{:S(2)}, u32[]{:S(2)}) collective-permute-start(bf16[512,112]{1,0:T(8,128)(2,1)S(1)} %get-tuple-element.24), channel_id=1, source_target_pairs={{0,384},{1,448},{2,0},{3,64},{4,128},{5,192},{6,256},{7,320},{64,3... | collective-permute-start | bytes 344072 | tf_op jit(solution)/shard_map/ppermute | solution.py:171
  279.8 1.9 collective-permute-start.7
  281.9 1.6 collective-permute-done.6
  283.6 12.5 %collective-permute-done.7 = bf16[512,112]{1,0:T(8,128)(2,1)S(1)} collective-permute-done((bf16[512,112]{1,0:T(8,128)(2,1)S(1)}, bf16[512,112]{1,0:T(8,128)(2,1)S(1)}, u32[]{:S(2)}, u32[]{:S(2)}) %collective-permute-start.7) | collective-permute-done | bytes 114720 | tf_op jit(solution)/shard_map/ppermute | solution.py:171
  296.3 0.8 copy.39
  (76 shorter events, 6.5 us)
Async XLA Ops:
  7.2 13.7 %copy-start = (s32[74]{0:T(128)S(1)}, s32[74]{0:T(128)}, u32[]{:S(2)}) copy-start(s32[74]{0:T(128)} %param.25) | copy-start | bytes 892
  7.2 18.4 %copy-start.9 = (s32[74]{0:T(128)S(1)}, s32[74]{0:T(128)}, u32[]{:S(2)}) copy-start(s32[74]{0:T(128)} %param.26) | copy-start | bytes 892
  7.2 21.5 %copy-start.10 = (s32[64]{0:T(128)S(1)}, s32[64]{0:T(128)}, u32[]{:S(2)}) copy-start(s32[64]{0:T(128)} %param.24) | copy-start | bytes 772
  7.2 22.7 %copy-start.2 = (bf16[64,896]{1,0:T(8,128)(2,1)S(1)}, bf16[64,896]{1,0:T(8,128)(2,1)}, u32[]{:S(2)}) copy-start(bf16[64,896]{1,0:T(8,128)(2,1)} %param.14) | copy-start | bytes 344068
  8.8 21.6 %copy-start.11 = (s32[74]{0:T(128)S(1)}, s32[74]{0:T(128)}, u32[]{:S(2)}) copy-start(s32[74]{0:T(128)} %param.27) | copy-start | bytes 892
  8.8 21.6 %copy-start.7 = (bf16[64,128]{1,0:T(8,128)(2,1)S(1)}, bf16[64,128]{1,0:T(8,128)(2,1)}, u32[]{:S(2)}) copy-start(bf16[64,128]{1,0:T(8,128)(2,1)} %param.15) | copy-start | bytes 49156
  8.8 23.5 %all-to-all-start = ((bf16[64,4,256]{2,1,0:T(4,128)(2,1)}), bf16[64,4,256]{2,1,0:T(4,128)(2,1)S(1)}, u32[]{:S(2)}, u32[]{:S(2)}) async-start(bf16[64,4,256]{2,1,0:T(4,128)(2,1)} %reshape.310), calls=%async_computation | async-start | bytes 262144 | tf_op jit(solution)/shard_map/all_to_all | solution.py:99
  17.5 14.1 %copy-start.8 = (bf16[64,128]{1,0:T(8,128)(2,1)S(1)}, bf16[64,128]{1,0:T(8,128)(2,1)}, u32[]{:S(2)}) copy-start(bf16[64,128]{1,0:T(8,128)(2,1)} %param.16) | copy-start | bytes 49156
  17.5 78.3 %all-gather.2.cloned.1.call-start = ((), (), s32[]{:S(2)}) async-start(), calls=%async_computation.2 | async-start | bytes 1806336 | tf_op jit(solution)/shard_map/all_gather | solution.py:156
  19.1 12.8 %copy-start.4 = (bf16[320,128]{1,0:T(8,128)(2,1)S(1)}, bf16[320,128]{1,0:T(8,128)(2,1)}, u32[]{:S(2)}) copy-start(bf16[320,128]{1,0:T(8,128)(2,1)} %param.18) | copy-start | bytes 245764
  19.1 12.8 %copy-start.5 = (bf16[320,128]{1,0:T(8,128)(2,1)S(1)}, bf16[320,128]{1,0:T(8,128)(2,1)}, u32[]{:S(2)}) copy-start(bf16[320,128]{1,0:T(8,128)(2,1)} %param.17) | copy-start | bytes 245764
  32.0 13.7 %copy-start.1 = (bf16[320,128]{1,0:T(8,128)(2,1)}, bf16[320,128]{1,0:T(8,128)(2,1)S(1)}, u32[]{:S(2)}) copy-start(bf16[320,128]{1,0:T(8,128)(2,1)S(1)} %get-tuple-element.37) | copy-start | bytes 245764
  32.0 23.8 %copy-start.6 = (bf16[320,128]{1,0:T(8,128)(2,1)}, bf16[320,128]{1,0:T(8,128)(2,1)S(1)}, u32[]{:S(2)}) copy-start(bf16[320,128]{1,0:T(8,128)(2,1)S(1)} %get-tuple-element.36) | copy-start | bytes 245764
  34.8 19.6 %all-to-all-start.1 = ((bf16[64,2,4,256]{3,2,1,0:T(4,128)(2,1)}), bf16[64,2,4,256]{3,2,1,0:T(4,128)(2,1)S(1)}, u32[]{:S(2)}, u32[]{:S(2)}) async-start(bf16[64,2,4,256]{3,2,1,0:T(4,128)(2,1)} %broadcast_select_fusion), calls=%async_computation.1 | async-start | bytes 524288 | tf_op jit(solution)/shard_map/all_to_all | solution.py:108
  98.5 183.3 %copy-start.3 = (bf16[512,112]{0,1:T(8,128)(2,1)S(1)}, bf16[512,112]{0,1:T(8,128)(2,1)}, u32[]{:S(2)}) copy-start(bf16[512,112]{0,1:T(8,128)(2,1)} %param.22) | copy-start | bytes 344068
  99.0 33.8 %collective-permute-start = (bf16[512,112]{1,0:T(8,128)(2,1)S(1)}, bf16[512,112]{1,0:T(8,128)(2,1)S(1)}, u32[]{:S(2)}, u32[]{:S(2)}) collective-permute-start(bf16[512,112]{1,0:T(8,128)(2,1)S(1)} %get-tuple-element.22), channel_id=1, source_target_pairs={{0,0},{1,64},{2,128},{3,192},{4,256},{5,320},{6,384},{7,448},{64,1... | collective-permute-start | bytes 344072 | tf_op jit(solution)/shard_map/ppermute | solution.py:171
  109.6 40.4 %collective-permute-start.1 = (bf16[512,112]{1,0:T(8,128)(2,1)S(1)}, bf16[512,112]{1,0:T(8,128)(2,1)S(1)}, u32[]{:S(2)}, u32[]{:S(2)}) collective-permute-start(bf16[512,112]{1,0:T(8,128)(2,1)S(1)} %get-tuple-element.29), channel_id=1, source_target_pairs={{0,64},{1,128},{2,192},{3,256},{4,320},{5,384},{6,448},{7,0},{64,6... | collective-permute-start | bytes 344072 | tf_op jit(solution)/shard_map/ppermute | solution.py:171
  111.6 168.3 %collective-permute-start.2 = (bf16[512,112]{1,0:T(8,128)(2,1)S(1)}, bf16[512,112]{1,0:T(8,128)(2,1)S(1)}, u32[]{:S(2)}, u32[]{:S(2)}) collective-permute-start(bf16[512,112]{1,0:T(8,128)(2,1)S(1)} %get-tuple-element.28), channel_id=1, source_target_pairs={{0,128},{1,192},{2,256},{3,320},{4,384},{5,448},{6,0},{7,64},{64,1... | collective-permute-start | bytes 344072 | tf_op jit(solution)/shard_map/ppermute | solution.py:171
  120.5 161.4 %collective-permute-start.3 = (bf16[512,112]{1,0:T(8,128)(2,1)S(1)}, bf16[512,112]{1,0:T(8,128)(2,1)S(1)}, u32[]{:S(2)}, u32[]{:S(2)}) collective-permute-start(bf16[512,112]{1,0:T(8,128)(2,1)S(1)} %get-tuple-element.27), channel_id=1, source_target_pairs={{0,192},{1,256},{2,320},{3,384},{4,448},{5,0},{6,64},{7,128},{64,1... | collective-permute-start | bytes 344072 | tf_op jit(solution)/shard_map/ppermute | solution.py:171
  127.1 154.8 %collective-permute-start.4 = (bf16[512,112]{1,0:T(8,128)(2,1)S(1)}, bf16[512,112]{1,0:T(8,128)(2,1)S(1)}, u32[]{:S(2)}, u32[]{:S(2)}) collective-permute-start(bf16[512,112]{1,0:T(8,128)(2,1)S(1)} %get-tuple-element.26), channel_id=1, source_target_pairs={{0,256},{1,320},{2,384},{3,448},{4,0},{5,64},{6,128},{7,192},{64,2... | collective-permute-start | bytes 344072 | tf_op jit(solution)/shard_map/ppermute | solution.py:171
  132.8 149.2 %collective-permute-start.5 = (bf16[512,112]{1,0:T(8,128)(2,1)S(1)}, bf16[512,112]{1,0:T(8,128)(2,1)S(1)}, u32[]{:S(2)}, u32[]{:S(2)}) collective-permute-start(bf16[512,112]{1,0:T(8,128)(2,1)S(1)} %get-tuple-element.25), channel_id=1, source_target_pairs={{0,320},{1,384},{2,448},{3,0},{4,64},{5,128},{6,192},{7,256},{64,3... | collective-permute-start | bytes 344072 | tf_op jit(solution)/shard_map/ppermute | solution.py:171
  150.0 133.6 %collective-permute-start.6 = (bf16[512,112]{1,0:T(8,128)(2,1)S(1)}, bf16[512,112]{1,0:T(8,128)(2,1)S(1)}, u32[]{:S(2)}, u32[]{:S(2)}) collective-permute-start(bf16[512,112]{1,0:T(8,128)(2,1)S(1)} %get-tuple-element.24), channel_id=1, source_target_pairs={{0,384},{1,448},{2,0},{3,64},{4,128},{5,192},{6,256},{7,320},{64,3... | collective-permute-start | bytes 344072 | tf_op jit(solution)/shard_map/ppermute | solution.py:171
  279.8 16.3 %collective-permute-start.7 = (bf16[512,112]{1,0:T(8,128)(2,1)S(1)}, bf16[512,112]{1,0:T(8,128)(2,1)S(1)}, u32[]{:S(2)}, u32[]{:S(2)}) collective-permute-start(bf16[512,112]{1,0:T(8,128)(2,1)S(1)} %get-tuple-element.23), channel_id=1, source_target_pairs={{0,448},{1,0},{2,64},{3,128},{4,192},{5,256},{6,320},{7,384},{64,4... | collective-permute-start | bytes 344072 | tf_op jit(solution)/shard_map/ppermute | solution.py:171
Sparse Core Ops, SparseCore 0:
  21.6 74.1 all-gather.1

commit v7 on v5

--- a/solution.py
+++ b/solution.py
@@ -110,8 +110,9 @@
     swap = [
         (h * mlp_count + m, m * mlp_count + h) for h in range(hi_count) for m in range(mlp_count)
     ]
-    residual_here = lax.ppermute(residual, ("hi", "mlp"), swap)
-    residual_here, queries = lax.optimization_barrier((residual_here, queries))
+    weight_here = lax.ppermute(out_weight, ("hi", "mlp"), swap)
+    weight_here, queries = lax.optimization_barrier((weight_here, queries))
+    weight_cols = lax.all_gather(weight_here, "mlp", axis=1, tiled=True)
     query_turned = apply_rotary(queries, positions, q_heads)
     key_turned = apply_rotary(fresh_token_keys, positions, kv_heads)
     my_request = lax.dynamic_slice_in_dim(token_request, my_index * tok_rows, 1)[0]
@@ -158,16 +159,15 @@
         (final[2] / final[1][..., None]).reshape(tok_rows, q_heads * width).astype(jnp.bfloat16)
     )
 
-    weight_cols = lax.all_gather(out_weight, "hi", axis=1, tiled=True)
-    token_block = lax.all_gather(attended_local, "lo", axis=0, tiled=True)
+    token_here = lax.ppermute(attended_local, ("hi", "mlp"), swap)
+    token_block = lax.all_gather(token_here, "lo", axis=0, tiled=True)
     projected = jnp.dot(token_block, weight_cols, preferred_element_type=jnp.float32).astype(
         jnp.bfloat16
     )
-    parts = projected.reshape(projected.shape[0], mlp_count, -1).transpose(1, 0, 2)
-    arrived = lax.all_to_all(parts, "mlp", 0, 0, tiled=True)
+    parts = projected.reshape(projected.shape[0], hi_count, -1).transpose(1, 0, 2)
+    arrived = lax.all_to_all(parts, "hi", 0, 0, tiled=True)
     summed = jnp.sum(arrived.astype(jnp.float32), axis=0)
-    result = (residual_here.astype(jnp.float32) + summed).astype(jnp.bfloat16)
-    hidden = lax.ppermute(result, ("hi", "mlp"), swap)
+    hidden = (residual.astype(jnp.float32) + summed).astype(jnp.bfloat16)
     return (hidden, leaf_key_output, leaf_value_output)
 
 

time: 176 us -> 173 us (0.983)
  the two profiles are of different devices: /device:TPU:90 before, /device:TPU:112 now
where the time goes in v7:
time: 173 us; the launch traced here: 172 us
  blocking collectives  60.1 us (35%)
  waiting for transfers between devices  42.3 us (24%)
  starting transfers between devices  28.1 us (16%)
  between operations  15.1 us (9%)
  other arithmetic  14.1 us (8%)
  local copies, waits for them, and re-layouts  8.5 us (5%)
  matrix products  4.27 us (2%)
    all_to_all x1, blocking collectives, body(): arrived = lax.all_to_all(parts, 'hi', 0, 0, tiled=True)  44.9 us
    ppermute x1, waiting for transfers between devices, body(): token_here = lax.ppermute(attended_local, ('hi', 'mlp'), swap)  15.8 us
    all_to_all x1, waiting for transfers between devices, body(): spread = lax.all_to_all(pieces, ('hi', 'lo'), 0, 0, tiled=True)  15.5 us
    all_gather x1, blocking collectives, body(): token_block = lax.all_gather(token_here, 'lo', axis=0, tiled=True)  15.1 us
    all_to_all x1, starting transfers between devices, body(): spread = lax.all_to_all(pieces, ('hi', 'lo'), 0, 0, tiled=True)  12 us
    all_to_all x1, waiting for transfers between devices, body(): incoming = lax.all_to_all(outgoing, ('hi', 'lo'), 0, 0, tiled=True)  10.9 us
    all_to_all x1, starting transfers between devices, body(): incoming = lax.all_to_all(outgoing, ('hi', 'lo'), 0, 0, tiled=True)  9.67 us
    reduce_sum x3, other arithmetic, lookup(): return jnp.sum(jnp.where(jnp.arange(table.shape[0]) == index, table, 0))  5.9 us
  transfers between devices with their start and end apart: 5, of which 3 were waited for; matrix products, arithmetic and copies ran while one was open for 13% of the time, Pallas kernels for 0%

profile of v7, /device:TPU:112, one launch (start us, length us, event | category | flops | bytes accessed | tf_op | source)
XLA Modules:
  0.0 172.5 jit_solution(9443658960232221968)
XLA Ops:
  7.2 4.1 %collective-permute-start = (bf16[896,112]{0,1:T(8,128)(2,1)}, bf16[896,112]{0,1:T(8,128)(2,1)S(1)}, u32[]{:S(2)}, u32[]{:S(2)}) collective-permute-start(bf16[896,112]{0,1:T(8,128)(2,1)} %param.21), channel_id=1, source_target_pairs={{0,0},{1,64},{2,128},{3,192},{4,256},{5,320},{6,384},{7,448},{64,1... | collective-permute-start | bytes 602120 | tf_op jit(solution)/shard_map/ppermute | solution.py:113
  11.4 0.9 pad_maximum_fusion
  12.3 0.7 reshape.313
  12.9 12.0 %all-to-all-start = ((bf16[64,4,256]{2,1,0:T(4,128)(2,1)}), bf16[64,4,256]{2,1,0:T(4,128)(2,1)S(1)}, u32[]{:S(2)}, u32[]{:S(2)}) async-start(bf16[64,4,256]{2,1,0:T(4,128)(2,1)} %reshape.313), calls=%async_computation | async-start | bytes 262144 | tf_op jit(solution)/shard_map/all_to_all | solution.py:99
  25.0 0.8 reshape.312
  25.8 1.3 dynamic_slice.3
  27.7 1.3 fusion.32
  29.0 1.9 %fusion.34 = s32[]{:T(128)} fusion(s32[74]{0:T(128)} %param.25, s32[]{:T(128)} %fusion.32), kind=kLoop, calls=%fused_computation.95 | loop fusion | flops 221 | bytes 304 | tf_op jit(solution)/shard_map/reduce_sum | solution.py:60
  31.0 2.7 %fusion.33 = (s32[]{:T(128)}, s32[]{:T(128)}, s32[]{:T(128)}) fusion(s32[74]{0:T(128)} %param.26, s32[]{:T(128)} %bitcast, s32[]{:T(128)} %fusion.34, s32[]{:T(128)} %fusion.32), kind=kLoop, calls=%fused_computation.94 | loop fusion | flops 663 | bytes 320 | tf_op jit(solution)/shard_map/reduce_sum | solution.py:60
  33.6 1.2 iota_compare_fusion.4
  34.8 1.9 %broadcast_add_fusion = (s32[64]{0:T(128)S(1)}, s32[64]{0:T(128)S(1)}, f32[64]{0:T(128)S(1)}) fusion(s32[]{:T(128)} %get-tuple-element.9, s32[64]{0:T(128)} %param.24, s32[]{:T(128)} %get-tuple-element.8), kind=kLoop, calls=%fused_computation.101 | loop fusion | flops 256 | bytes 1032 | tf_op jit(solution)/shard_map/add | solution.py:135
  36.9 1.4 gather_fusion
  38.6 0.8 gather_fusion.1
  40.1 0.7 iota_compare_fusion.3
  41.6 0.5 copy-done.2
  42.3 15.5 %all-to-all-done = bf16[64,4,256]{2,1,0:T(4,128)(2,1)S(1)} async-done(((bf16[64,4,256]{2,1,0:T(4,128)(2,1)}), bf16[64,4,256]{2,1,0:T(4,128)(2,1)S(1)}, u32[]{:S(2)}, u32[]{:S(2)}) %all-to-all-start) | async-done | bytes 131104 | tf_op jit(solution)/shard_map/all_to_all | solution.py:99
  57.8 0.6 gather_fusion.2
  58.5 0.8 gather_fusion.3
  59.3 0.9 broadcast_select_fusion
  60.2 9.7 %all-to-all-start.1 = ((bf16[64,2,4,256]{3,2,1,0:T(4,128)(2,1)}), bf16[64,2,4,256]{3,2,1,0:T(4,128)(2,1)S(1)}, u32[]{:S(2)}, u32[]{:S(2)}) async-start(bf16[64,2,4,256]{3,2,1,0:T(4,128)(2,1)} %broadcast_select_fusion), calls=%async_computation.1 | async-start | bytes 524288 | tf_op jit(solution)/shard_map/all_to_all | solution.py:108
  70.0 0.4 select_reduce_fusion.1
  70.7 10.9 %all-to-all-done.1 = bf16[64,2,4,256]{3,2,1,0:T(4,128)(2,1)S(1)} async-done(((bf16[64,2,4,256]{3,2,1,0:T(4,128)(2,1)}), bf16[64,2,4,256]{3,2,1,0:T(4,128)(2,1)S(1)}, u32[]{:S(2)}, u32[]{:S(2)}) %all-to-all-start.1) | async-done | bytes 262176 | tf_op jit(solution)/shard_map/all_to_all | solution.py:108
  81.9 0.4 select_reduce_fusion
  82.3 0.3 convert_reduce_fusion.1
  82.7 0.3 fusion.5
  83.4 2.2 %collective-permute-start.1 = (bf16[64,896]{1,0:T(8,128)(2,1)S(1)}, bf16[64,896]{1,0:T(8,128)(2,1)S(1)}, u32[]{:S(2)}, u32[]{:S(2)}) collective-permute-start(bf16[64,896]{1,0:T(8,128)(2,1)S(1)} %bitcast.74), channel_id=1, source_target_pairs={{0,0},{1,64},{2,128},{3,192},{4,256},{5,320},{6,384},{7,448},{64,1... | collective-permute-start | bytes 344072 | tf_op jit(solution)/shard_map/ppermute | solution.py:162
  85.7 15.8 %collective-permute-done.1 = bf16[64,896]{1,0:T(8,128)(2,1)S(1)} collective-permute-done((bf16[64,896]{1,0:T(8,128)(2,1)S(1)}, bf16[64,896]{1,0:T(8,128)(2,1)S(1)}, u32[]{:S(2)}, u32[]{:S(2)}) %collective-permute-start.1) | collective-permute-done | bytes 114720 | tf_op jit(solution)/shard_map/ppermute | solution.py:162
  101.5 15.1 %all_gather.6 = bf16[512,896]{1,0:T(8,128)(2,1)S(1)} all-gather(bf16[64,896]{1,0:T(8,128)(2,1)S(1)} %collective-permute-done.1), channel_id=1, replica_groups=mesh['hi'=8,'lo'=8,'mlp'=8] {'lo'}, dimensions={0}, use_global_device_ids=true | all-gather | bytes 1032192 | tf_op jit(solution)/shard_map/all_gather | solution.py:163
  116.7 2.6 %convolution_convert_fusion = bf16[512,896]{1,0:T(8,128)(2,1)S(1)} fusion(bf16[512,896]{1,0:T(8,128)(2,1)S(1)} %all_gather.6, bf16[896,896]{0,1:T(8,128)(2,1)} %all-gather.2.cloned.1.call-done), kind=kOutput, calls=%fused_computation.5 | convolution fusion | flops 822542336 | bytes 3440640 | tf_op jit(solution)/shard_map/dot_general | solution.py:164
  119.3 0.5 copy.35
  119.9 44.9 %all_to_all.15 = bf16[8,512,112]{1,2,0:T(8,128)(2,1)S(1)} all-to-all(bf16[8,512,112]{1,2,0:T(8,128)(2,1)S(1)} %bitcast.71), channel_id=1, replica_groups=mesh['hi'=8,'lo'=8,'mlp'=8] {'hi'}, dimensions={0} | all-to-all | bytes 1835008 | tf_op jit(solution)/shard_map/all_to_all | solution.py:168
  164.9 0.7 add_convert_fusion
  (62 shorter events, 3.2 us)
Async XLA Ops:
  7.2 31.4 %copy-start = (s32[74]{0:T(128)S(1)}, s32[74]{0:T(128)}, u32[]{:S(2)}) copy-start(s32[74]{0:T(128)} %param.25) | copy-start | bytes 892
  7.2 32.4 %copy-start.10 = (s32[74]{0:T(128)S(1)}, s32[74]{0:T(128)}, u32[]{:S(2)}) copy-start(s32[74]{0:T(128)} %param.27) | copy-start | bytes 892
  7.2 32.5 %copy-start.8 = (bf16[64,128]{1,0:T(8,128)(2,1)S(1)}, bf16[64,128]{1,0:T(8,128)(2,1)}, u32[]{:S(2)}) copy-start(bf16[64,128]{1,0:T(8,128)(2,1)} %param.15) | copy-start | bytes 49156
  7.2 33.8 %copy-start.9 = (bf16[64,128]{1,0:T(8,128)(2,1)S(1)}, bf16[64,128]{1,0:T(8,128)(2,1)}, u32[]{:S(2)}) copy-start(bf16[64,128]{1,0:T(8,128)(2,1)} %param.16) | copy-start | bytes 49156
  7.2 33.9 %copy-start.6 = (bf16[320,128]{1,0:T(8,128)(2,1)S(1)}, bf16[320,128]{1,0:T(8,128)(2,1)}, u32[]{:S(2)}) copy-start(bf16[320,128]{1,0:T(8,128)(2,1)} %param.17) | copy-start | bytes 245764
  7.2 33.9 %copy-start.5 = (bf16[320,128]{1,0:T(8,128)(2,1)S(1)}, bf16[320,128]{1,0:T(8,128)(2,1)}, u32[]{:S(2)}) copy-start(bf16[320,128]{1,0:T(8,128)(2,1)} %param.18) | copy-start | bytes 245764
  7.2 34.2 %copy-start.4 = (bf16[64,896]{1,0:T(8,128)(2,1)S(1)}, bf16[64,896]{1,0:T(8,128)(2,1)}, u32[]{:S(2)}) copy-start(bf16[64,896]{1,0:T(8,128)(2,1)} %param.14) | copy-start | bytes 344068
  7.2 34.2 %collective-permute-start = (bf16[896,112]{0,1:T(8,128)(2,1)}, bf16[896,112]{0,1:T(8,128)(2,1)S(1)}, u32[]{:S(2)}, u32[]{:S(2)}) collective-permute-start(bf16[896,112]{0,1:T(8,128)(2,1)} %param.21), channel_id=1, source_target_pairs={{0,0},{1,64},{2,128},{3,192},{4,256},{5,320},{6,384},{7,448},{64,1... | collective-permute-start | bytes 602120 | tf_op jit(solution)/shard_map/ppermute | solution.py:113
  12.9 44.8 %all-to-all-start = ((bf16[64,4,256]{2,1,0:T(4,128)(2,1)}), bf16[64,4,256]{2,1,0:T(4,128)(2,1)S(1)}, u32[]{:S(2)}, u32[]{:S(2)}) async-start(bf16[64,4,256]{2,1,0:T(4,128)(2,1)} %reshape.313), calls=%async_computation | async-start | bytes 262144 | tf_op jit(solution)/shard_map/all_to_all | solution.py:99
  25.0 91.7 %all-gather.2.cloned.1.call-start = ((), (), s32[]{:S(2)}) async-start(), calls=%async_computation.3 | async-start | bytes 1806336 | tf_op jit(solution)/shard_map/all_gather | solution.py:115
  41.3 28.7 %copy-start.1 = (bf16[320,128]{1,0:T(8,128)(2,1)}, bf16[320,128]{1,0:T(8,128)(2,1)S(1)}, u32[]{:S(2)}) copy-start(bf16[320,128]{1,0:T(8,128)(2,1)S(1)} %get-tuple-element.24) | copy-start | bytes 245764
  41.3 41.7 %copy-start.7 = (bf16[320,128]{1,0:T(8,128)(2,1)}, bf16[320,128]{1,0:T(8,128)(2,1)S(1)}, u32[]{:S(2)}) copy-start(bf16[320,128]{1,0:T(8,128)(2,1)S(1)} %get-tuple-element.23) | copy-start | bytes 245764
  41.5 0.7 copy-start.2
  60.2 21.4 %all-to-all-start.1 = ((bf16[64,2,4,256]{3,2,1,0:T(4,128)(2,1)}), bf16[64,2,4,256]{3,2,1,0:T(4,128)(2,1)S(1)}, u32[]{:S(2)}, u32[]{:S(2)}) async-start(bf16[64,2,4,256]{3,2,1,0:T(4,128)(2,1)} %broadcast_select_fusion), calls=%async_computation.1 | async-start | bytes 524288 | tf_op jit(solution)/shard_map/all_to_all | solution.py:108
  83.4 18.1 %collective-permute-start.1 = (bf16[64,896]{1,0:T(8,128)(2,1)S(1)}, bf16[64,896]{1,0:T(8,128)(2,1)S(1)}, u32[]{:S(2)}, u32[]{:S(2)}) collective-permute-start(bf16[64,896]{1,0:T(8,128)(2,1)S(1)} %bitcast.74), channel_id=1, source_target_pairs={{0,0},{1,64},{2,128},{3,192},{4,256},{5,320},{6,384},{7,448},{64,1... | collective-permute-start | bytes 344072 | tf_op jit(solution)/shard_map/ppermute | solution.py:162
  119.8 45.1 %copy-start.3 = (bf16[512,112]{0,1:T(8,128)(2,1)S(1)}, bf16[512,112]{0,1:T(8,128)(2,1)}, u32[]{:S(2)}) copy-start(bf16[512,112]{0,1:T(8,128)(2,1)} %param.22) | copy-start | bytes 344068
Sparse Core Ops, SparseCore 0:
  42.3 60.6 all-gather.1

commit v8 on v7

--- a/solution.py
+++ b/solution.py
@@ -12,6 +12,8 @@
 
 THETA = 5000000.0
 NEG = -1e30
+HI = ("x", "zh")
+TOK = ("x", "zh", "lo")
 
 
 def apply_rotary(values, position, heads):
@@ -76,11 +78,11 @@
     node_lengths,
     node_owner,
 ):
-    hi = lax.axis_index("hi")
+    hi = lax.axis_index(HI)
     lo = lax.axis_index("lo")
     mlp = lax.axis_index("mlp")
     lo_count = lax.axis_size("lo")
-    hi_count = lax.axis_size("hi")
+    hi_count = lax.axis_size(HI)
     mlp_count = lax.axis_size("mlp")
     my_index = hi * lo_count + lo
     tok_rows = queries.shape[0]
@@ -96,7 +98,7 @@
     node_rows = my_pair.shape[0]
     piece_rows = node_rows // tok_count
     pieces = my_pair.reshape(tok_count, piece_rows, my_pair.shape[1])
-    spread = lax.all_to_all(pieces, ("hi", "lo"), 0, 0, tiled=True)
+    spread = lax.all_to_all(pieces, TOK, 0, 0, tiled=True)
     held = jnp.take(spread, node_owner[:shared_count], axis=0)
     requests = token_request.reshape(-1, tok_rows)[:, 0]
     middles = parents[shared_count + requests]
@@ -105,12 +107,12 @@
     outgoing = jnp.take(held, wanted.reshape(-1), axis=0).reshape(
         (tok_count, 2, piece_rows, my_pair.shape[1])
     )
-    incoming = lax.all_to_all(outgoing, ("hi", "lo"), 0, 0, tiled=True)
+    incoming = lax.all_to_all(outgoing, TOK, 0, 0, tiled=True)
 
     swap = [
         (h * mlp_count + m, m * mlp_count + h) for h in range(hi_count) for m in range(mlp_count)
     ]
-    weight_here = lax.ppermute(out_weight, ("hi", "mlp"), swap)
+    weight_here = lax.ppermute(out_weight, HI + ("mlp",), swap)
     weight_here, queries = lax.optimization_barrier((weight_here, queries))
     weight_cols = lax.all_gather(weight_here, "mlp", axis=1, tiled=True)
     query_turned = apply_rotary(queries, positions, q_heads)
@@ -159,13 +161,18 @@
         (final[2] / final[1][..., None]).reshape(tok_rows, q_heads * width).astype(jnp.bfloat16)
     )
 
-    token_here = lax.ppermute(attended_local, ("hi", "mlp"), swap)
+    token_here = lax.ppermute(attended_local, HI + ("mlp",), swap)
     token_block = lax.all_gather(token_here, "lo", axis=0, tiled=True)
     projected = jnp.dot(token_block, weight_cols, preferred_element_type=jnp.float32).astype(
         jnp.bfloat16
     )
-    parts = projected.reshape(projected.shape[0], hi_count, -1).transpose(1, 0, 2)
-    arrived = lax.all_to_all(parts, "hi", 0, 0, tiled=True)
+    near_count = lax.axis_size("zh")
+    far_count = hi_count // near_count
+    rows = projected.shape[0]
+    parts = projected.reshape(rows, far_count, near_count, -1).transpose(2, 0, 1, 3)
+    arrived = lax.all_to_all(parts, "zh", 0, 0, tiled=True)
+    halfway = jnp.sum(arrived.astype(jnp.float32), axis=0).astype(jnp.bfloat16)
+    arrived = lax.all_to_all(halfway.transpose(1, 0, 2), "x", 0, 0, tiled=True)
     summed = jnp.sum(arrived.astype(jnp.float32), axis=0)
     hidden = (residual.astype(jnp.float32) + summed).astype(jnp.bfloat16)
     return (hidden, leaf_key_output, leaf_value_output)
@@ -174,9 +181,12 @@
 def solution(mesh):
     tok_count = mesh.shape["tok"]
     lo_count = 8
-    grid = mesh.devices.reshape(tok_count // lo_count, lo_count, mesh.shape["mlp"])
-    split = jax.sharding.Mesh(grid, ("hi", "lo", "mlp"))
-    tok = ("hi", "lo")
+    near_count = 2
+    grid = mesh.devices.reshape(
+        tok_count // lo_count // near_count, near_count, lo_count, mesh.shape["mlp"]
+    )
+    split = jax.sharding.Mesh(grid, ("x", "zh", "lo", "mlp"))
+    tok = TOK
     placed = (
         P(tok, "mlp"),
         P(tok, "mlp"),

time: 173 us -> 181 us (1.046)
  blocking collectives: 60.1 us -> 67.3 us
    all_to_all x1 -> x2, blocking collectives: 44.9 us -> 52.2 us  [the longest x1 39 us: body(): arrived = lax.all_to_all(parts, 'zh', 0, 0, tiled=True)]
  transfers between devices with their start and end apart: 5 -> 5, of which waited for: 3 -> 3; matrix products, arithmetic and copies ran while one was open for 13% -> 12% of each run, Pallas kernels for 0% -> 0%
where the time goes in v8:
time: 181 us; the launch traced here: 180 us
  blocking collectives  67.3 us (37%)
  waiting for transfers between devices  42.3 us (23%)
  starting transfers between devices  28.1 us (16%)
  between operations  15.1 us (8%)
  other arithmetic  14.5 us (8%)
  local copies, waits for them, and re-layouts  8.57 us (5%)
  matrix products  4.27 us (2%)
    all_to_all x1, blocking collectives, body(): arrived = lax.all_to_all(parts, 'zh', 0, 0, tiled=True)  39 us
    ppermute x1, waiting for transfers between devices, body(): token_here = lax.ppermute(attended_local, HI + ('mlp',), swap)  15.8 us
    all_to_all x1, waiting for transfers between devices, body(): spread = lax.all_to_all(pieces, TOK, 0, 0, tiled=True)  15.5 us
    all_gather x1, blocking collectives, body(): token_block = lax.all_gather(token_here, 'lo', axis=0, tiled=True)  15.1 us
    all_to_all x1, blocking collectives, body(): arrived = lax.all_to_all(halfway.transpose(1, 0, 2), 'x', 0, 0, tiled=True)  13.2 us
    all_to_all x1, starting transfers between devices, body(): spread = lax.all_to_all(pieces, TOK, 0, 0, tiled=True)  12 us
    all_to_all x1, waiting for transfers between devices, body(): incoming = lax.all_to_all(outgoing, TOK, 0, 0, tiled=True)  10.9 us
    all_to_all x1, starting transfers between devices, body(): incoming = lax.all_to_all(outgoing, TOK, 0, 0, tiled=True)  9.67 us
  transfers between devices with their start and end apart: 5, of which 3 were waited for; matrix products, arithmetic and copies ran while one was open for 12% of the time, Pallas kernels for 0%

profile of v8, /device:TPU:112, one launch (start us, length us, event | category | flops | bytes accessed | tf_op | source)
XLA Modules:
  0.0 180.1 jit_solution(7049954372394747349)
XLA Ops:
  7.2 4.1 %collective-permute-start = (bf16[896,112]{0,1:T(8,128)(2,1)}, bf16[896,112]{0,1:T(8,128)(2,1)S(1)}, u32[]{:S(2)}, u32[]{:S(2)}) collective-permute-start(bf16[896,112]{0,1:T(8,128)(2,1)} %param.21), channel_id=1, source_target_pairs={{0,0},{1,64},{2,128},{3,192},{4,256},{5,320},{6,384},{7,448},{64,1... | collective-permute-start | bytes 602120 | tf_op jit(solution)/shard_map/ppermute | solution.py:115
  11.4 0.9 pad_maximum_fusion
  12.3 0.7 reshape.313
  12.9 12.0 %all-to-all-start = ((bf16[64,4,256]{2,1,0:T(4,128)(2,1)}), bf16[64,4,256]{2,1,0:T(4,128)(2,1)S(1)}, u32[]{:S(2)}, u32[]{:S(2)}) async-start(bf16[64,4,256]{2,1,0:T(4,128)(2,1)} %reshape.313), calls=%async_computation | async-start | bytes 262144 | tf_op jit(solution)/shard_map/all_to_all | solution.py:101
  25.0 0.8 reshape.312
  25.8 1.3 dynamic_slice.3
  27.8 1.3 fusion.32
  29.0 1.9 %fusion.34 = s32[]{:T(128)} fusion(s32[74]{0:T(128)} %param.25, s32[]{:T(128)} %fusion.32), kind=kLoop, calls=%fused_computation.95 | loop fusion | flops 221 | bytes 304 | tf_op jit(solution)/shard_map/reduce_sum | solution.py:62
  31.0 2.7 %fusion.33 = (s32[]{:T(128)}, s32[]{:T(128)}, s32[]{:T(128)}) fusion(s32[74]{0:T(128)} %param.26, s32[]{:T(128)} %bitcast, s32[]{:T(128)} %fusion.34, s32[]{:T(128)} %fusion.32), kind=kLoop, calls=%fused_computation.94 | loop fusion | flops 663 | bytes 320 | tf_op jit(solution)/shard_map/reduce_sum | solution.py:62
  33.6 1.2 iota_compare_fusion.4
  34.9 1.9 %broadcast_add_fusion = (s32[64]{0:T(128)S(1)}, s32[64]{0:T(128)S(1)}, f32[64]{0:T(128)S(1)}) fusion(s32[]{:T(128)} %get-tuple-element.9, s32[64]{0:T(128)} %param.24, s32[]{:T(128)} %get-tuple-element.8), kind=kLoop, calls=%fused_computation.101 | loop fusion | flops 256 | bytes 1032 | tf_op jit(solution)/shard_map/add | solution.py:137
  36.9 1.4 gather_fusion
  38.6 0.8 gather_fusion.1
  40.1 0.7 iota_compare_fusion.3
  41.6 0.5 copy-done.2
  42.3 15.5 %all-to-all-done = bf16[64,4,256]{2,1,0:T(4,128)(2,1)S(1)} async-done(((bf16[64,4,256]{2,1,0:T(4,128)(2,1)}), bf16[64,4,256]{2,1,0:T(4,128)(2,1)S(1)}, u32[]{:S(2)}, u32[]{:S(2)}) %all-to-all-start) | async-done | bytes 131104 | tf_op jit(solution)/shard_map/all_to_all | solution.py:101
  57.8 0.6 gather_fusion.2
  58.5 0.8 gather_fusion.3
  59.3 0.9 broadcast_select_fusion
  60.2 9.7 %all-to-all-start.1 = ((bf16[64,2,4,256]{3,2,1,0:T(4,128)(2,1)}), bf16[64,2,4,256]{3,2,1,0:T(4,128)(2,1)S(1)}, u32[]{:S(2)}, u32[]{:S(2)}) async-start(bf16[64,2,4,256]{3,2,1,0:T(4,128)(2,1)} %broadcast_select_fusion), calls=%async_computation.1 | async-start | bytes 524288 | tf_op jit(solution)/shard_map/all_to_all | solution.py:110
  70.0 0.4 select_reduce_fusion.1
  70.7 10.9 %all-to-all-done.1 = bf16[64,2,4,256]{3,2,1,0:T(4,128)(2,1)S(1)} async-done(((bf16[64,2,4,256]{3,2,1,0:T(4,128)(2,1)}), bf16[64,2,4,256]{3,2,1,0:T(4,128)(2,1)S(1)}, u32[]{:S(2)}, u32[]{:S(2)}) %all-to-all-start.1) | async-done | bytes 262176 | tf_op jit(solution)/shard_map/all_to_all | solution.py:110
  81.9 0.4 select_reduce_fusion
  83.4 2.2 %collective-permute-start.1 = (bf16[64,896]{1,0:T(8,128)(2,1)S(1)}, bf16[64,896]{1,0:T(8,128)(2,1)S(1)}, u32[]{:S(2)}, u32[]{:S(2)}) collective-permute-start(bf16[64,896]{1,0:T(8,128)(2,1)S(1)} %bitcast.76), channel_id=1, source_target_pairs={{0,0},{1,64},{2,128},{3,192},{4,256},{5,320},{6,384},{7,448},{64,1... | collective-permute-start | bytes 344072 | tf_op jit(solution)/shard_map/ppermute | solution.py:164
  85.7 15.8 %collective-permute-done.1 = bf16[64,896]{1,0:T(8,128)(2,1)S(1)} collective-permute-done((bf16[64,896]{1,0:T(8,128)(2,1)S(1)}, bf16[64,896]{1,0:T(8,128)(2,1)S(1)}, u32[]{:S(2)}, u32[]{:S(2)}) %collective-permute-start.1) | collective-permute-done | bytes 114720 | tf_op jit(solution)/shard_map/ppermute | solution.py:164
  101.5 15.1 %all_gather.6 = bf16[512,896]{1,0:T(8,128)(2,1)S(1)} all-gather(bf16[64,896]{1,0:T(8,128)(2,1)S(1)} %collective-permute-done.1), channel_id=1, replica_groups=mesh['x'=4,'zh'=2,'lo'=8,'mlp'=8] {'lo'}, dimensions={0}, use_global_device_ids=true | all-gather | bytes 1032192 | tf_op jit(solution)/shard_map/all_gather | solution.py:165
  116.6 2.6 %convolution_convert_fusion = bf16[512,896]{1,0:T(8,128)(2,1)S(1)} fusion(bf16[512,896]{1,0:T(8,128)(2,1)S(1)} %all_gather.6, bf16[896,896]{0,1:T(8,128)(2,1)} %all-gather.2.cloned.1.call-done), kind=kOutput, calls=%fused_computation.4 | convolution fusion | flops 822542336 | bytes 3440640 | tf_op jit(solution)/shard_map/dot_general | solution.py:166
  119.3 0.5 copy.44
  119.9 39.0 %all_to_all.20 = bf16[2,512,4,112]{1,3,2,0:T(8,128)(2,1)S(1)} all-to-all(bf16[2,512,4,112]{1,3,2,0:T(8,128)(2,1)S(1)} %copy.45), channel_id=1, replica_groups=mesh['x'=4,'zh'=2,'lo'=8,'mlp'=8] {'zh'}, dimensions={0} | all-to-all | bytes 1835008 | tf_op jit(solution)/shard_map/all_to_all | solution.py:173
  158.9 0.4 reduce_sum.91
  159.3 13.2 %all_to_all.21 = bf16[4,512,112]{1,2,0:T(8,128)(2,1)S(1)} all-to-all(bf16[4,512,112]{1,2,0:T(8,128)(2,1)S(1)} %bitcast.73), channel_id=1, replica_groups=mesh['x'=4,'zh'=2,'lo'=8,'mlp'=8] {'x'}, dimensions={0} | all-to-all | bytes 917504 | tf_op jit(solution)/shard_map/all_to_all | solution.py:175
  172.6 0.7 add_convert_fusion
  (65 shorter events, 3.9 us)
Async XLA Ops:
  7.2 31.4 %copy-start = (s32[74]{0:T(128)S(1)}, s32[74]{0:T(128)}, u32[]{:S(2)}) copy-start(s32[74]{0:T(128)} %param.25) | copy-start | bytes 892
  7.2 32.5 %copy-start.10 = (s32[74]{0:T(128)S(1)}, s32[74]{0:T(128)}, u32[]{:S(2)}) copy-start(s32[74]{0:T(128)} %param.27) | copy-start | bytes 892
  7.2 32.5 %copy-start.8 = (bf16[64,128]{1,0:T(8,128)(2,1)S(1)}, bf16[64,128]{1,0:T(8,128)(2,1)}, u32[]{:S(2)}) copy-start(bf16[64,128]{1,0:T(8,128)(2,1)} %param.15) | copy-start | bytes 49156
  7.2 33.8 %copy-start.9 = (bf16[64,128]{1,0:T(8,128)(2,1)S(1)}, bf16[64,128]{1,0:T(8,128)(2,1)}, u32[]{:S(2)}) copy-start(bf16[64,128]{1,0:T(8,128)(2,1)} %param.16) | copy-start | bytes 49156
  7.2 33.9 %copy-start.6 = (bf16[320,128]{1,0:T(8,128)(2,1)S(1)}, bf16[320,128]{1,0:T(8,128)(2,1)}, u32[]{:S(2)}) copy-start(bf16[320,128]{1,0:T(8,128)(2,1)} %param.17) | copy-start | bytes 245764
  7.2 33.9 %copy-start.5 = (bf16[320,128]{1,0:T(8,128)(2,1)S(1)}, bf16[320,128]{1,0:T(8,128)(2,1)}, u32[]{:S(2)}) copy-start(bf16[320,128]{1,0:T(8,128)(2,1)} %param.18) | copy-start | bytes 245764
  7.2 34.2 %copy-start.4 = (bf16[64,896]{1,0:T(8,128)(2,1)S(1)}, bf16[64,896]{1,0:T(8,128)(2,1)}, u32[]{:S(2)}) copy-start(bf16[64,896]{1,0:T(8,128)(2,1)} %param.14) | copy-start | bytes 344068
  7.2 34.2 %collective-permute-start = (bf16[896,112]{0,1:T(8,128)(2,1)}, bf16[896,112]{0,1:T(8,128)(2,1)S(1)}, u32[]{:S(2)}, u32[]{:S(2)}) collective-permute-start(bf16[896,112]{0,1:T(8,128)(2,1)} %param.21), channel_id=1, source_target_pairs={{0,0},{1,64},{2,128},{3,192},{4,256},{5,320},{6,384},{7,448},{64,1... | collective-permute-start | bytes 602120 | tf_op jit(solution)/shard_map/ppermute | solution.py:115
  12.9 44.8 %all-to-all-start = ((bf16[64,4,256]{2,1,0:T(4,128)(2,1)}), bf16[64,4,256]{2,1,0:T(4,128)(2,1)S(1)}, u32[]{:S(2)}, u32[]{:S(2)}) async-start(bf16[64,4,256]{2,1,0:T(4,128)(2,1)} %reshape.313), calls=%async_computation | async-start | bytes 262144 | tf_op jit(solution)/shard_map/all_to_all | solution.py:101
  25.0 91.7 %all-gather.2.cloned.1.call-start = ((), (), s32[]{:S(2)}) async-start(), calls=%async_computation.4 | async-start | bytes 1806336 | tf_op jit(solution)/shard_map/all_gather | solution.py:117
  41.3 28.7 %copy-start.1 = (bf16[320,128]{1,0:T(8,128)(2,1)}, bf16[320,128]{1,0:T(8,128)(2,1)S(1)}, u32[]{:S(2)}) copy-start(bf16[320,128]{1,0:T(8,128)(2,1)S(1)} %get-tuple-element.24) | copy-start | bytes 245764
  41.3 41.7 %copy-start.7 = (bf16[320,128]{1,0:T(8,128)(2,1)}, bf16[320,128]{1,0:T(8,128)(2,1)S(1)}, u32[]{:S(2)}) copy-start(bf16[320,128]{1,0:T(8,128)(2,1)S(1)} %get-tuple-element.23) | copy-start | bytes 245764
  41.5 0.7 copy-start.2
  60.2 21.4 %all-to-all-start.1 = ((bf16[64,2,4,256]{3,2,1,0:T(4,128)(2,1)}), bf16[64,2,4,256]{3,2,1,0:T(4,128)(2,1)S(1)}, u32[]{:S(2)}, u32[]{:S(2)}) async-start(bf16[64,2,4,256]{3,2,1,0:T(4,128)(2,1)} %broadcast_select_fusion), calls=%async_computation.1 | async-start | bytes 524288 | tf_op jit(solution)/shard_map/all_to_all | solution.py:110
  83.4 18.1 %collective-permute-start.1 = (bf16[64,896]{1,0:T(8,128)(2,1)S(1)}, bf16[64,896]{1,0:T(8,128)(2,1)S(1)}, u32[]{:S(2)}, u32[]{:S(2)}) collective-permute-start(bf16[64,896]{1,0:T(8,128)(2,1)S(1)} %bitcast.76), channel_id=1, source_target_pairs={{0,0},{1,64},{2,128},{3,192},{4,256},{5,320},{6,384},{7,448},{64,1... | collective-permute-start | bytes 344072 | tf_op jit(solution)/shard_map/ppermute | solution.py:164
  158.9 13.6 %copy-start.3 = (bf16[512,112]{0,1:T(8,128)(2,1)S(1)}, bf16[512,112]{0,1:T(8,128)(2,1)}, u32[]{:S(2)}) copy-start(bf16[512,112]{0,1:T(8,128)(2,1)} %param.22) | copy-start | bytes 344068
Sparse Core Ops, SparseCore 0:
  42.3 60.6 all-gather.1

commit v9 on v8

--- a/solution.py
+++ b/solution.py
@@ -12,8 +12,8 @@
 
 THETA = 5000000.0
 NEG = -1e30
-HI = ("x", "zh")
-TOK = ("x", "zh", "lo")
+TOK = ("x", "z", "c")
+GROUP = ("x", "c")
 
 
 def apply_rotary(values, position, heads):
@@ -78,13 +78,10 @@
     node_lengths,
     node_owner,
 ):
-    hi = lax.axis_index(HI)
-    lo = lax.axis_index("lo")
-    mlp = lax.axis_index("mlp")
-    lo_count = lax.axis_size("lo")
-    hi_count = lax.axis_size(HI)
     mlp_count = lax.axis_size("mlp")
-    my_index = hi * lo_count + lo
+    group_count = lax.axis_size(GROUP)
+    tok_count = lax.axis_size(TOK)
+    my_index = lax.axis_index(TOK)
     tok_rows = queries.shape[0]
     width = HEAD_SIZE
     q_heads = queries.shape[1] // width
@@ -93,7 +90,6 @@
     kv_width = kv_heads * width
     shared_count = ROOTS + MIDS
 
-    tok_count = hi_count * lo_count
     my_pair = jnp.concatenate([shared_key_block, shared_value_block], axis=1)
     node_rows = my_pair.shape[0]
     piece_rows = node_rows // tok_count
@@ -110,9 +106,11 @@
     incoming = lax.all_to_all(outgoing, TOK, 0, 0, tiled=True)
 
     swap = [
-        (h * mlp_count + m, m * mlp_count + h) for h in range(hi_count) for m in range(mlp_count)
+        (h * mlp_count + m, m * mlp_count + h)
+        for h in range(group_count)
+        for m in range(mlp_count)
     ]
-    weight_here = lax.ppermute(out_weight, HI + ("mlp",), swap)
+    weight_here = lax.ppermute(out_weight, GROUP + ("mlp",), swap)
     weight_here, queries = lax.optimization_barrier((weight_here, queries))
     weight_cols = lax.all_gather(weight_here, "mlp", axis=1, tiled=True)
     query_turned = apply_rotary(queries, positions, q_heads)
@@ -161,18 +159,22 @@
         (final[2] / final[1][..., None]).reshape(tok_rows, q_heads * width).astype(jnp.bfloat16)
     )
 
-    token_here = lax.ppermute(attended_local, HI + ("mlp",), swap)
-    token_block = lax.all_gather(token_here, "lo", axis=0, tiled=True)
+    z_count = tok_count // group_count
+    c_count = lax.axis_size("c")
+    spread_route = []
+    for t in range(tok_count):
+        for g in range(mlp_count):
+            x_to, c_to, z_to, m_to = g // c_count, g % c_count, t % z_count, t // z_count
+            spread_route.append(
+                (t * mlp_count + g, ((x_to * z_count + z_to) * c_count + c_to) * mlp_count + m_to)
+            )
+    token_here = lax.ppermute(attended_local, TOK + ("mlp",), spread_route)
+    token_block = lax.all_gather(token_here, "z", axis=0, tiled=True)
     projected = jnp.dot(token_block, weight_cols, preferred_element_type=jnp.float32).astype(
         jnp.bfloat16
     )
-    near_count = lax.axis_size("zh")
-    far_count = hi_count // near_count
-    rows = projected.shape[0]
-    parts = projected.reshape(rows, far_count, near_count, -1).transpose(2, 0, 1, 3)
-    arrived = lax.all_to_all(parts, "zh", 0, 0, tiled=True)
-    halfway = jnp.sum(arrived.astype(jnp.float32), axis=0).astype(jnp.bfloat16)
-    arrived = lax.all_to_all(halfway.transpose(1, 0, 2), "x", 0, 0, tiled=True)
+    parts = projected.reshape(projected.shape[0], group_count, -1).transpose(1, 0, 2)
+    arrived = lax.all_to_all(parts, GROUP, 0, 0, tiled=True)
     summed = jnp.sum(arrived.astype(jnp.float32), axis=0)
     hidden = (residual.astype(jnp.float32) + summed).astype(jnp.bfloat16)
     return (hidden, leaf_key_output, leaf_value_output)
@@ -180,12 +182,12 @@
 
 def solution(mesh):
     tok_count = mesh.shape["tok"]
-    lo_count = 8
-    near_count = 2
+    z_count = 8
+    c_count = 2
     grid = mesh.devices.reshape(
-        tok_count // lo_count // near_count, near_count, lo_count, mesh.shape["mlp"]
-    )
-    split = jax.sharding.Mesh(grid, ("x", "zh", "lo", "mlp"))
+        tok_count // z_count // c_count, z_count, c_count, mesh.shape["mlp"]
+    )
+    split = jax.sharding.Mesh(grid, ("x", "z", "c", "mlp"))
     tok = TOK
     placed = (
         P(tok, "mlp"),

time: 181 us -> 165 us (0.912)
  the two profiles are of different devices: /device:TPU:112 before, /device:TPU:1 now
where the time goes in v9:
time: 165 us
  blocking collectives  64.2 us (39%)
  starting transfers between devices  36.3 us (22%)
  waiting for transfers between devices  22 us (13%)
  between operations  15.1 us (9%)
  other arithmetic  14.1 us (9%)
  local copies, waits for them, and re-layouts  8.5 us (5%)
  matrix products  4.28 us (3%)
    all_gather x1, blocking collectives, body(): token_block = lax.all_gather(token_here, 'z', axis=0, tiled=True)  40.2 us
    all_to_all x1, blocking collectives, body(): arrived = lax.all_to_all(parts, GROUP, 0, 0, tiled=True)  24 us
    all_to_all x1, starting transfers between devices, body(): spread = lax.all_to_all(pieces, TOK, 0, 0, tiled=True)  17.9 us
    all_to_all x1, waiting for transfers between devices, body(): incoming = lax.all_to_all(outgoing, TOK, 0, 0, tiled=True)  11.2 us
    ppermute x1, waiting for transfers between devices, body(): token_here = lax.ppermute(attended_local, TOK + ('mlp',), spread_route)  10.8 us
    all_to_all x1, starting transfers between devices, body(): incoming = lax.all_to_all(outgoing, TOK, 0, 0, tiled=True)  10.3 us
    reduce_sum x3, other arithmetic, lookup(): return jnp.sum(jnp.where(jnp.arange(table.shape[0]) == index, table, 0))  5.9 us
    ppermute x1, starting transfers between devices, body(): weight_here = lax.ppermute(out_weight, GROUP + ('mlp',), swap)  4.73 us
  transfers between devices with their start and end apart: 5, of which 2 were waited for; matrix products, arithmetic and copies ran while one was open for 14% of the time, Pallas kernels for 0%

profile of v9, /device:TPU:1, one launch (start us, length us, event | category | flops | bytes accessed | tf_op | source)
XLA Modules:
  0.0 164.6 jit_solution(11092496806223945245)
XLA Ops:
  7.2 4.7 %collective-permute-start = (bf16[896,112]{0,1:T(8,128)(2,1)}, bf16[896,112]{0,1:T(8,128)(2,1)S(1)}, u32[]{:S(2)}, u32[]{:S(2)}) collective-permute-start(bf16[896,112]{0,1:T(8,128)(2,1)} %param.21), channel_id=1, source_target_pairs={{0,0},{1,8},{2,128},{3,136},{4,256},{5,264},{6,384},{7,392},{8,1},... | collective-permute-start | bytes 602120 | tf_op jit(solution)/shard_map/ppermute | solution.py:113
  12.0 0.9 pad_maximum_fusion
  12.9 0.7 reshape.313
  13.6 17.9 %all-to-all-start = ((bf16[64,4,256]{2,1,0:T(4,128)(2,1)}), bf16[64,4,256]{2,1,0:T(4,128)(2,1)S(1)}, u32[]{:S(2)}, u32[]{:S(2)}) async-start(bf16[64,4,256]{2,1,0:T(4,128)(2,1)} %reshape.313), calls=%async_computation | async-start | bytes 262144 | tf_op jit(solution)/shard_map/all_to_all | solution.py:97
  31.6 0.8 reshape.312
  32.3 1.3 dynamic_slice.3
  34.3 1.3 fusion.32
  35.6 1.9 %fusion.34 = s32[]{:T(128)} fusion(s32[74]{0:T(128)} %param.25, s32[]{:T(128)} %fusion.32), kind=kLoop, calls=%fused_computation.95 | loop fusion | flops 221 | bytes 304 | tf_op jit(solution)/shard_map/reduce_sum | solution.py:62
  37.5 2.7 %fusion.33 = (s32[]{:T(128)}, s32[]{:T(128)}, s32[]{:T(128)}) fusion(s32[74]{0:T(128)} %param.26, s32[]{:T(128)} %bitcast, s32[]{:T(128)} %fusion.34, s32[]{:T(128)} %fusion.32), kind=kLoop, calls=%fused_computation.94 | loop fusion | flops 663 | bytes 320 | tf_op jit(solution)/shard_map/reduce_sum | solution.py:62
  40.2 1.2 iota_compare_fusion.4
  41.4 1.9 %broadcast_add_fusion = (s32[64]{0:T(128)S(1)}, s32[64]{0:T(128)S(1)}, f32[64]{0:T(128)S(1)}) fusion(s32[]{:T(128)} %get-tuple-element.9, s32[64]{0:T(128)} %param.24, s32[]{:T(128)} %get-tuple-element.8), kind=kLoop, calls=%fused_computation.101 | loop fusion | flops 256 | bytes 1032 | tf_op jit(solution)/shard_map/add | solution.py:135
  43.4 1.4 gather_fusion
  45.1 0.8 gather_fusion.1
  46.6 0.7 iota_compare_fusion.3
  48.1 0.5 copy-done.2
  48.8 0.6 gather_fusion.2
  49.5 0.8 gather_fusion.3
  50.3 0.9 broadcast_select_fusion
  51.3 10.3 %all-to-all-start.1 = ((bf16[64,2,4,256]{3,2,1,0:T(4,128)(2,1)}), bf16[64,2,4,256]{3,2,1,0:T(4,128)(2,1)S(1)}, u32[]{:S(2)}, u32[]{:S(2)}) async-start(bf16[64,2,4,256]{3,2,1,0:T(4,128)(2,1)} %broadcast_select_fusion), calls=%async_computation.1 | async-start | bytes 524288 | tf_op jit(solution)/shard_map/all_to_all | solution.py:106
  61.7 0.4 select_reduce_fusion.1
  62.4 11.2 %all-to-all-done.1 = bf16[64,2,4,256]{3,2,1,0:T(4,128)(2,1)S(1)} async-done(((bf16[64,2,4,256]{3,2,1,0:T(4,128)(2,1)}), bf16[64,2,4,256]{3,2,1,0:T(4,128)(2,1)S(1)}, u32[]{:S(2)}, u32[]{:S(2)}) %all-to-all-start.1) | async-done | bytes 262176 | tf_op jit(solution)/shard_map/all_to_all | solution.py:106
  73.8 0.4 select_reduce_fusion
  74.3 0.3 convert_reduce_fusion.1
  74.6 0.3 fusion.5
  75.0 0.3 fusion.7
  75.4 3.3 %collective-permute-start.1 = (bf16[64,896]{1,0:T(8,128)(2,1)S(1)}, bf16[64,896]{1,0:T(8,128)(2,1)S(1)}, u32[]{:S(2)}, u32[]{:S(2)}) collective-permute-start(bf16[64,896]{1,0:T(8,128)(2,1)S(1)} %bitcast.74), channel_id=1, source_target_pairs={{0,0},{1,8},{2,128},{3,136},{4,256},{5,264},{6,384},{7,392},{8,16}... | collective-permute-start | bytes 344072 | tf_op jit(solution)/shard_map/ppermute | solution.py:171
  78.7 10.8 %collective-permute-done.1 = bf16[64,896]{1,0:T(8,128)(2,1)S(1)} collective-permute-done((bf16[64,896]{1,0:T(8,128)(2,1)S(1)}, bf16[64,896]{1,0:T(8,128)(2,1)S(1)}, u32[]{:S(2)}, u32[]{:S(2)}) %collective-permute-start.1) | collective-permute-done | bytes 114720 | tf_op jit(solution)/shard_map/ppermute | solution.py:171
  89.5 40.2 %all_gather.6 = bf16[512,896]{1,0:T(8,128)(2,1)S(1)} all-gather(bf16[64,896]{1,0:T(8,128)(2,1)S(1)} %collective-permute-done.1), channel_id=1, replica_groups=mesh['x'=4,'z'=8,'c'=2,'mlp'=8] {'z'}, dimensions={0}, use_global_device_ids=true | all-gather | bytes 1032192 | tf_op jit(solution)/shard_map/all_gather | solution.py:172
  129.7 2.6 %convolution_convert_fusion = bf16[512,896]{1,0:T(8,128)(2,1)S(1)} fusion(bf16[512,896]{1,0:T(8,128)(2,1)S(1)} %all_gather.6, bf16[896,896]{0,1:T(8,128)(2,1)} %all-gather.2.cloned.1.call-done), kind=kOutput, calls=%fused_computation.5 | convolution fusion | flops 822542336 | bytes 3440640 | tf_op jit(solution)/shard_map/dot_general | solution.py:173
  132.4 0.5 copy.35
  132.9 24.0 %all_to_all.15 = bf16[8,512,112]{1,2,0:T(8,128)(2,1)S(1)} all-to-all(bf16[8,512,112]{1,2,0:T(8,128)(2,1)S(1)} %bitcast.71), channel_id=1, replica_groups=mesh['x'=4,'z'=8,'c'=2,'mlp'=8] {'x','c'}, dimensions={0} | all-to-all | bytes 1835008 | tf_op jit(solution)/shard_map/all_to_all | solution.py:177
  157.0 0.7 add_convert_fusion
  (62 shorter events, 2.9 us)
Async XLA Ops:
  7.2 37.9 %copy-start = (s32[74]{0:T(128)S(1)}, s32[74]{0:T(128)}, u32[]{:S(2)}) copy-start(s32[74]{0:T(128)} %param.25) | copy-start | bytes 892
  7.2 39.0 %copy-start.10 = (s32[74]{0:T(128)S(1)}, s32[74]{0:T(128)}, u32[]{:S(2)}) copy-start(s32[74]{0:T(128)} %param.27) | copy-start | bytes 892
  7.2 39.0 %copy-start.8 = (bf16[64,128]{1,0:T(8,128)(2,1)S(1)}, bf16[64,128]{1,0:T(8,128)(2,1)}, u32[]{:S(2)}) copy-start(bf16[64,128]{1,0:T(8,128)(2,1)} %param.15) | copy-start | bytes 49156
  7.2 40.3 %copy-start.9 = (bf16[64,128]{1,0:T(8,128)(2,1)S(1)}, bf16[64,128]{1,0:T(8,128)(2,1)}, u32[]{:S(2)}) copy-start(bf16[64,128]{1,0:T(8,128)(2,1)} %param.16) | copy-start | bytes 49156
  7.2 40.4 %copy-start.6 = (bf16[320,128]{1,0:T(8,128)(2,1)S(1)}, bf16[320,128]{1,0:T(8,128)(2,1)}, u32[]{:S(2)}) copy-start(bf16[320,128]{1,0:T(8,128)(2,1)} %param.17) | copy-start | bytes 245764
  7.2 40.4 %copy-start.5 = (bf16[320,128]{1,0:T(8,128)(2,1)S(1)}, bf16[320,128]{1,0:T(8,128)(2,1)}, u32[]{:S(2)}) copy-start(bf16[320,128]{1,0:T(8,128)(2,1)} %param.18) | copy-start | bytes 245764
  7.2 40.8 %copy-start.4 = (bf16[64,896]{1,0:T(8,128)(2,1)S(1)}, bf16[64,896]{1,0:T(8,128)(2,1)}, u32[]{:S(2)}) copy-start(bf16[64,896]{1,0:T(8,128)(2,1)} %param.14) | copy-start | bytes 344068
  7.2 40.7 %collective-permute-start = (bf16[896,112]{0,1:T(8,128)(2,1)}, bf16[896,112]{0,1:T(8,128)(2,1)S(1)}, u32[]{:S(2)}, u32[]{:S(2)}) collective-permute-start(bf16[896,112]{0,1:T(8,128)(2,1)} %param.21), channel_id=1, source_target_pairs={{0,0},{1,8},{2,128},{3,136},{4,256},{5,264},{6,384},{7,392},{8,1},... | collective-permute-start | bytes 602120 | tf_op jit(solution)/shard_map/ppermute | solution.py:113
  13.6 35.3 %all-to-all-start = ((bf16[64,4,256]{2,1,0:T(4,128)(2,1)}), bf16[64,4,256]{2,1,0:T(4,128)(2,1)S(1)}, u32[]{:S(2)}, u32[]{:S(2)}) async-start(bf16[64,4,256]{2,1,0:T(4,128)(2,1)} %reshape.313), calls=%async_computation | async-start | bytes 262144 | tf_op jit(solution)/shard_map/all_to_all | solution.py:97
  31.5 98.3 %all-gather.2.cloned.1.call-start = ((), (), s32[]{:S(2)}) async-start(), calls=%async_computation.3 | async-start | bytes 1806336 | tf_op jit(solution)/shard_map/all_gather | solution.py:115
  47.8 13.9 %copy-start.1 = (bf16[320,128]{1,0:T(8,128)(2,1)}, bf16[320,128]{1,0:T(8,128)(2,1)S(1)}, u32[]{:S(2)}) copy-start(bf16[320,128]{1,0:T(8,128)(2,1)S(1)} %get-tuple-element.24) | copy-start | bytes 245764
  47.8 27.1 %copy-start.7 = (bf16[320,128]{1,0:T(8,128)(2,1)}, bf16[320,128]{1,0:T(8,128)(2,1)S(1)}, u32[]{:S(2)}) copy-start(bf16[320,128]{1,0:T(8,128)(2,1)S(1)} %get-tuple-element.23) | copy-start | bytes 245764
  48.0 0.7 copy-start.2
  51.3 22.3 %all-to-all-start.1 = ((bf16[64,2,4,256]{3,2,1,0:T(4,128)(2,1)}), bf16[64,2,4,256]{3,2,1,0:T(4,128)(2,1)S(1)}, u32[]{:S(2)}, u32[]{:S(2)}) async-start(bf16[64,2,4,256]{3,2,1,0:T(4,128)(2,1)} %broadcast_select_fusion), calls=%async_computation.1 | async-start | bytes 524288 | tf_op jit(solution)/shard_map/all_to_all | solution.py:106
  75.4 14.1 %collective-permute-start.1 = (bf16[64,896]{1,0:T(8,128)(2,1)S(1)}, bf16[64,896]{1,0:T(8,128)(2,1)S(1)}, u32[]{:S(2)}, u32[]{:S(2)}) collective-permute-start(bf16[64,896]{1,0:T(8,128)(2,1)S(1)} %bitcast.74), channel_id=1, source_target_pairs={{0,0},{1,8},{2,128},{3,136},{4,256},{5,264},{6,384},{7,392},{8,16}... | collective-permute-start | bytes 344072 | tf_op jit(solution)/shard_map/ppermute | solution.py:171
  132.9 24.1 %copy-start.3 = (bf16[512,112]{0,1:T(8,128)(2,1)S(1)}, bf16[512,112]{0,1:T(8,128)(2,1)}, u32[]{:S(2)}) copy-start(bf16[512,112]{0,1:T(8,128)(2,1)} %param.22) | copy-start | bytes 344068
Sparse Core Ops, SparseCore 0:
  48.8 41.4 all-gather.1

commit v10 on v9

--- a/solution.py
+++ b/solution.py
@@ -12,7 +12,8 @@
 
 THETA = 5000000.0
 NEG = -1e30
-TOK = ("x", "z", "c")
+TOK = ("x", "zh", "zl", "c")
+LOW = ("zl", "c")
 GROUP = ("x", "c")
 
 
@@ -166,10 +167,13 @@
         for g in range(mlp_count):
             x_to, c_to, z_to, m_to = g // c_count, g % c_count, t % z_count, t // z_count
             spread_route.append(
-                (t * mlp_count + g, ((x_to * z_count + z_to) * c_count + c_to) * mlp_count + m_to)
+                (
+                    t * mlp_count + g,
+                    ((x_to * z_count + z_to) * c_count + c_to) * mlp_count + m_to,
+                )
             )
-    token_here = lax.ppermute(attended_local, TOK + ("mlp",), spread_route)
-    token_block = lax.all_gather(token_here, "z", axis=0, tiled=True)
+    gathered_block = lax.all_gather(attended_local, LOW, axis=0, tiled=True)
+    token_block = lax.ppermute(gathered_block, TOK + ("mlp",), spread_route)
     projected = jnp.dot(token_block, weight_cols, preferred_element_type=jnp.float32).astype(
         jnp.bfloat16
     )
@@ -185,9 +189,9 @@
     z_count = 8
     c_count = 2
     grid = mesh.devices.reshape(
-        tok_count // z_count // c_count, z_count, c_count, mesh.shape["mlp"]
-    )
-    split = jax.sharding.Mesh(grid, ("x", "z", "c", "mlp"))
+        tok_count // z_count // c_count, 2, z_count // 2, c_count, mesh.shape["mlp"]
+    )
+    split = jax.sharding.Mesh(grid, ("x", "zh", "zl", "c", "mlp"))
     tok = TOK
     placed = (
         P(tok, "mlp"),

time: 165 us -> 366 us (2.22)
  the two profiles are of different devices: /device:TPU:1 before, /device:TPU:152 now
where the time goes in v10:
time: 366 us; the launch traced here: 365 us
  waiting for transfers between devices  151 us (41%)
  blocking collectives  137 us (37%)
  starting transfers between devices  35 us (10%)
  between operations  15.2 us (4%)
  other arithmetic  14.1 us (4%)
  local copies, waits for them, and re-layouts  8.51 us (2%)
  matrix products  4.28 us (1%)
    ppermute x1, waiting for transfers between devices, body(): token_block = lax.ppermute(gathered_block, TOK + ('mlp',), spread_route)  140 us
    all_to_all x1, blocking collectives, body(): arrived = lax.all_to_all(parts, GROUP, 0, 0, tiled=True)  122 us
    all_to_all x1, starting transfers between devices, body(): spread = lax.all_to_all(pieces, TOK, 0, 0, tiled=True)  14.5 us
    all_gather x1, blocking collectives, body(): gathered_block = lax.all_gather(attended_local, LOW, axis=0, tiled=True)  14.2 us
    all_to_all x1, waiting for transfers between devices, body(): incoming = lax.all_to_all(outgoing, TOK, 0, 0, tiled=True)  10.9 us
    all_to_all x1, starting transfers between devices, body(): incoming = lax.all_to_all(outgoing, TOK, 0, 0, tiled=True)  10.3 us
    ppermute x1, starting transfers between devices, body(): token_block = lax.ppermute(gathered_block, TOK + ('mlp',), spread_route)  7.51 us
  transfers between devices with their start and end apart: 5, of which 2 were waited for; matrix products, arithmetic and copies ran while one was open for 6% of the time, Pallas kernels for 0%

profile of v10, /device:TPU:152, one launch (start us, length us, event | category | flops | bytes accessed | tf_op | source)
XLA Modules:
  0.0 364.9 jit_solution(12253198127167814595)
XLA Ops:
  7.2 2.6 collective-permute-start
  9.9 0.9 pad_maximum_fusion
  10.8 0.7 reshape.313
  11.5 14.5 %all-to-all-start = ((bf16[64,4,256]{2,1,0:T(4,128)(2,1)}), bf16[64,4,256]{2,1,0:T(4,128)(2,1)S(1)}, u32[]{:S(2)}, u32[]{:S(2)}) async-start(bf16[64,4,256]{2,1,0:T(4,128)(2,1)} %reshape.313), calls=%async_computation | async-start | bytes 262144 | tf_op jit(solution)/shard_map/all_to_all | solution.py:98
  26.1 0.8 reshape.312
  26.8 1.3 dynamic_slice.3
  28.8 1.3 fusion.32
  30.1 1.9 fusion.34
  32.0 2.7 fusion.33
  34.7 1.2 iota_compare_fusion.4
  35.9 1.9 broadcast_add_fusion
  37.9 1.4 gather_fusion
  39.6 0.8 gather_fusion.1
  41.1 0.7 iota_compare_fusion.3
  42.7 0.5 copy-done.2
  43.3 0.6 gather_fusion.2
  44.0 0.8 gather_fusion.3
  44.8 0.9 broadcast_select_fusion
  45.8 10.3 %all-to-all-start.1 = ((bf16[64,2,4,256]{3,2,1,0:T(4,128)(2,1)}), bf16[64,2,4,256]{3,2,1,0:T(4,128)(2,1)S(1)}, u32[]{:S(2)}, u32[]{:S(2)}) async-start(bf16[64,2,4,256]{3,2,1,0:T(4,128)(2,1)} %broadcast_select_fusion), calls=%async_computation.1 | async-start | bytes 524288 | tf_op jit(solution)/shard_map/all_to_all | solution.py:107
  56.2 0.4 select_reduce_fusion.1
  56.9 10.9 %all-to-all-done.1 = bf16[64,2,4,256]{3,2,1,0:T(4,128)(2,1)S(1)} async-done(((bf16[64,2,4,256]{3,2,1,0:T(4,128)(2,1)}), bf16[64,2,4,256]{3,2,1,0:T(4,128)(2,1)S(1)}, u32[]{:S(2)}, u32[]{:S(2)}) %all-to-all-start.1) | async-done | bytes 262176 | tf_op jit(solution)/shard_map/all_to_all | solution.py:107
  68.1 0.4 select_reduce_fusion
  68.5 0.3 convert_reduce_fusion.1
  68.8 0.3 fusion.5
  69.2 0.3 fusion.7
  69.6 14.2 %all_gather.6 = bf16[512,896]{1,0:T(8,128)(2,1)S(1)} all-gather(bf16[64,896]{1,0:T(8,128)(2,1)S(1)} %bitcast.74), channel_id=1, replica_groups=mesh['x'=4,'zh'=2,'zl'=4,'c'=2,'mlp'=8] {'zl','c'}, dimensions={0}, use_global_device_ids=true | all-gather | bytes 1032192 | tf_op jit(solution)/shard_map/all_gather | solution.py:175
  83.8 7.5 %collective-permute-start.1 = (bf16[512,896]{1,0:T(8,128)(2,1)S(1)}, bf16[512,896]{1,0:T(8,128)(2,1)S(1)}, u32[]{:S(2)}, u32[]{:S(2)}) collective-permute-start(bf16[512,896]{1,0:T(8,128)(2,1)S(1)} %all_gather.6), channel_id=1, source_target_pairs={{0,0},{1,8},{2,128},{3,136},{4,256},{5,264},{6,384},{7,392},{8,16}... | collective-permute-start | bytes 2752520 | tf_op jit(solution)/shard_map/ppermute | solution.py:176
  91.3 140.3 %collective-permute-done.1 = bf16[512,896]{1,0:T(8,128)(2,1)S(1)} collective-permute-done((bf16[512,896]{1,0:T(8,128)(2,1)S(1)}, bf16[512,896]{1,0:T(8,128)(2,1)S(1)}, u32[]{:S(2)}, u32[]{:S(2)}) %collective-permute-start.1) | collective-permute-done | bytes 917536 | tf_op jit(solution)/shard_map/ppermute | solution.py:176
  231.7 2.6 convolution_convert_fusion
  234.3 0.5 copy.35
  234.9 122.4 %all_to_all.15 = bf16[8,512,112]{1,2,0:T(8,128)(2,1)S(1)} all-to-all(bf16[8,512,112]{1,2,0:T(8,128)(2,1)S(1)} %bitcast.71), channel_id=1, replica_groups=mesh['x'=4,'zh'=2,'zl'=4,'c'=2,'mlp'=8] {'x','c'}, dimensions={0} | all-to-all | bytes 1835008 | tf_op jit(solution)/shard_map/all_to_all | solution.py:181
  357.4 0.7 add_convert_fusion
  (62 shorter events, 2.9 us)
Async XLA Ops:
  7.2 32.4 %copy-start = (s32[74]{0:T(128)S(1)}, s32[74]{0:T(128)}, u32[]{:S(2)}) copy-start(s32[74]{0:T(128)} %param.25) | copy-start | bytes 892
  7.2 33.5 %copy-start.10 = (s32[74]{0:T(128)S(1)}, s32[74]{0:T(128)}, u32[]{:S(2)}) copy-start(s32[74]{0:T(128)} %param.27) | copy-start | bytes 892
  7.2 33.5 %copy-start.8 = (bf16[64,128]{1,0:T(8,128)(2,1)S(1)}, bf16[64,128]{1,0:T(8,128)(2,1)}, u32[]{:S(2)}) copy-start(bf16[64,128]{1,0:T(8,128)(2,1)} %param.15) | copy-start | bytes 49156
  7.2 34.8 %copy-start.9 = (bf16[64,128]{1,0:T(8,128)(2,1)S(1)}, bf16[64,128]{1,0:T(8,128)(2,1)}, u32[]{:S(2)}) copy-start(bf16[64,128]{1,0:T(8,128)(2,1)} %param.16) | copy-start | bytes 49156
  7.2 34.9 %copy-start.6 = (bf16[320,128]{1,0:T(8,128)(2,1)S(1)}, bf16[320,128]{1,0:T(8,128)(2,1)}, u32[]{:S(2)}) copy-start(bf16[320,128]{1,0:T(8,128)(2,1)} %param.17) | copy-start | bytes 245764
  7.2 34.9 %copy-start.5 = (bf16[320,128]{1,0:T(8,128)(2,1)S(1)}, bf16[320,128]{1,0:T(8,128)(2,1)}, u32[]{:S(2)}) copy-start(bf16[320,128]{1,0:T(8,128)(2,1)} %param.18) | copy-start | bytes 245764
  7.2 35.3 %copy-start.4 = (bf16[64,896]{1,0:T(8,128)(2,1)S(1)}, bf16[64,896]{1,0:T(8,128)(2,1)}, u32[]{:S(2)}) copy-start(bf16[64,896]{1,0:T(8,128)(2,1)} %param.14) | copy-start | bytes 344068
  7.2 35.2 %collective-permute-start = (bf16[896,112]{0,1:T(8,128)(2,1)}, bf16[896,112]{0,1:T(8,128)(2,1)S(1)}, u32[]{:S(2)}, u32[]{:S(2)}) collective-permute-start(bf16[896,112]{0,1:T(8,128)(2,1)} %param.21), channel_id=1, source_target_pairs={{0,0},{1,8},{2,128},{3,136},{4,256},{5,264},{6,384},{7,392},{8,1},... | collective-permute-start | bytes 602120 | tf_op jit(solution)/shard_map/ppermute | solution.py:114
  11.5 31.9 %all-to-all-start = ((bf16[64,4,256]{2,1,0:T(4,128)(2,1)}), bf16[64,4,256]{2,1,0:T(4,128)(2,1)S(1)}, u32[]{:S(2)}, u32[]{:S(2)}) async-start(bf16[64,4,256]{2,1,0:T(4,128)(2,1)} %reshape.313), calls=%async_computation | async-start | bytes 262144 | tf_op jit(solution)/shard_map/all_to_all | solution.py:98
  26.0 205.7 %all-gather.2.cloned.1.call-start = ((), (), s32[]{:S(2)}) async-start(), calls=%async_computation.3 | async-start | bytes 1806336 | tf_op jit(solution)/shard_map/all_gather | solution.py:116
  42.3 13.9 %copy-start.1 = (bf16[320,128]{1,0:T(8,128)(2,1)}, bf16[320,128]{1,0:T(8,128)(2,1)S(1)}, u32[]{:S(2)}) copy-start(bf16[320,128]{1,0:T(8,128)(2,1)S(1)} %get-tuple-element.24) | copy-start | bytes 245764
  42.3 26.9 %copy-start.7 = (bf16[320,128]{1,0:T(8,128)(2,1)}, bf16[320,128]{1,0:T(8,128)(2,1)S(1)}, u32[]{:S(2)}) copy-start(bf16[320,128]{1,0:T(8,128)(2,1)S(1)} %get-tuple-element.23) | copy-start | bytes 245764
  42.5 0.7 copy-start.2
  45.8 22.0 %all-to-all-start.1 = ((bf16[64,2,4,256]{3,2,1,0:T(4,128)(2,1)}), bf16[64,2,4,256]{3,2,1,0:T(4,128)(2,1)S(1)}, u32[]{:S(2)}, u32[]{:S(2)}) async-start(bf16[64,2,4,256]{3,2,1,0:T(4,128)(2,1)} %broadcast_select_fusion), calls=%async_computation.1 | async-start | bytes 524288 | tf_op jit(solution)/shard_map/all_to_all | solution.py:107
  83.8 147.8 %collective-permute-start.1 = (bf16[512,896]{1,0:T(8,128)(2,1)S(1)}, bf16[512,896]{1,0:T(8,128)(2,1)S(1)}, u32[]{:S(2)}, u32[]{:S(2)}) collective-permute-start(bf16[512,896]{1,0:T(8,128)(2,1)S(1)} %all_gather.6), channel_id=1, source_target_pairs={{0,0},{1,8},{2,128},{3,136},{4,256},{5,264},{6,384},{7,392},{8,16}... | collective-permute-start | bytes 2752520 | tf_op jit(solution)/shard_map/ppermute | solution.py:176
  234.8 122.6 %copy-start.3 = (bf16[512,112]{0,1:T(8,128)(2,1)S(1)}, bf16[512,112]{0,1:T(8,128)(2,1)}, u32[]{:S(2)}) copy-start(bf16[512,112]{0,1:T(8,128)(2,1)} %param.22) | copy-start | bytes 344068
Sparse Core Ops, SparseCore 0:
  43.3 41.8 all-gather.1

commit v11 on v9

--- a/solution.py
+++ b/solution.py
@@ -169,7 +169,8 @@
                 (t * mlp_count + g, ((x_to * z_count + z_to) * c_count + c_to) * mlp_count + m_to)
             )
     token_here = lax.ppermute(attended_local, TOK + ("mlp",), spread_route)
-    token_block = lax.all_gather(token_here, "z", axis=0, tiled=True)
+    copies = jnp.broadcast_to(token_here[None], (z_count,) + token_here.shape)
+    token_block = lax.all_to_all(copies, "z", 0, 0, tiled=True).reshape(-1, token_here.shape[1])
     projected = jnp.dot(token_block, weight_cols, preferred_element_type=jnp.float32).astype(
         jnp.bfloat16
     )

time: 165 us -> 168 us (1.018)
  blocking collectives: 64.2 us -> 67.3 us
    all_to_all x0 -> x1, blocking collectives: none -> 46.5 us  [body(): lax.all_to_all(copies, 'z', 0, 0, tiled=True)]
    all_gather x1 -> x0, blocking collectives: 40.2 us -> none  [body(): token_block = lax.all_gather(token_here, 'z', axis=0, tiled=True)]
    all_to_all x1, blocking collectives: 24 us -> 20.9 us  [body(): arrived = lax.all_to_all(parts, GROUP, 0, 0, tiled=True)]
  transfers between devices with their start and end apart: 5 -> 5, of which waited for: 2 -> 2; matrix products, arithmetic and copies ran while one was open for 14% -> 13% of each run, Pallas kernels for 0% -> 0%
where the time goes in v11:
time: 168 us
  blocking collectives  67.3 us (40%)
  starting transfers between devices  36.3 us (22%)
  waiting for transfers between devices  22 us (13%)
  between operations  15.2 us (9%)
  other arithmetic  14.1 us (8%)
  local copies, waits for them, and re-layouts  8.62 us (5%)
  matrix products  4.28 us (3%)
    all_to_all x1, blocking collectives, body(): lax.all_to_all(copies, 'z', 0, 0, tiled=True)  46.5 us
    all_to_all x1, blocking collectives, body(): arrived = lax.all_to_all(parts, GROUP, 0, 0, tiled=True)  20.9 us
    all_to_all x1, starting transfers between devices, body(): spread = lax.all_to_all(pieces, TOK, 0, 0, tiled=True)  17.9 us
    all_to_all x1, waiting for transfers between devices, body(): incoming = lax.all_to_all(outgoing, TOK, 0, 0, tiled=True)  11.2 us
    ppermute x1, waiting for transfers between devices, body(): token_here = lax.ppermute(attended_local, TOK + ('mlp',), spread_route)  10.8 us
    all_to_all x1, starting transfers between devices, body(): incoming = lax.all_to_all(outgoing, TOK, 0, 0, tiled=True)  10.3 us
    reduce_sum x3, other arithmetic, lookup(): return jnp.sum(jnp.where(jnp.arange(table.shape[0]) == index, table, 0))  5.9 us
    ppermute x1, starting transfers between devices, body(): weight_here = lax.ppermute(out_weight, GROUP + ('mlp',), swap)  4.73 us
  transfers between devices with their start and end apart: 5, of which 2 were waited for; matrix products, arithmetic and copies ran while one was open for 13% of the time, Pallas kernels for 0%

profile of v11, /device:TPU:1, one launch (start us, length us, event | category | flops | bytes accessed | tf_op | source)
XLA Modules:
  0.0 167.8 jit_solution(6000820598839761122)
XLA Ops:
  7.2 4.7 %collective-permute-start = (bf16[896,112]{0,1:T(8,128)(2,1)}, bf16[896,112]{0,1:T(8,128)(2,1)S(1)}, u32[]{:S(2)}, u32[]{:S(2)}) collective-permute-start(bf16[896,112]{0,1:T(8,128)(2,1)} %param.21), channel_id=1, source_target_pairs={{0,0},{1,8},{2,128},{3,136},{4,256},{5,264},{6,384},{7,392},{8,1},... | collective-permute-start | bytes 602120 | tf_op jit(solution)/shard_map/ppermute | solution.py:113
  12.0 0.9 pad_maximum_fusion
  12.9 0.7 reshape.317
  13.6 17.9 %all-to-all-start = ((bf16[64,4,256]{2,1,0:T(4,128)(2,1)}), bf16[64,4,256]{2,1,0:T(4,128)(2,1)S(1)}, u32[]{:S(2)}, u32[]{:S(2)}) async-start(bf16[64,4,256]{2,1,0:T(4,128)(2,1)} %reshape.317), calls=%async_computation | async-start | bytes 262144 | tf_op jit(solution)/shard_map/all_to_all | solution.py:97
  31.6 0.8 reshape.316
  32.3 1.3 dynamic_slice.3
  34.3 1.3 fusion.32
  35.6 1.9 %fusion.34 = s32[]{:T(128)} fusion(s32[74]{0:T(128)} %param.25, s32[]{:T(128)} %fusion.32), kind=kLoop, calls=%fused_computation.95 | loop fusion | flops 221 | bytes 304 | tf_op jit(solution)/shard_map/reduce_sum | solution.py:62
  37.5 2.7 %fusion.33 = (s32[]{:T(128)}, s32[]{:T(128)}, s32[]{:T(128)}) fusion(s32[74]{0:T(128)} %param.26, s32[]{:T(128)} %bitcast, s32[]{:T(128)} %fusion.34, s32[]{:T(128)} %fusion.32), kind=kLoop, calls=%fused_computation.94 | loop fusion | flops 663 | bytes 320 | tf_op jit(solution)/shard_map/reduce_sum | solution.py:62
  40.2 1.2 iota_compare_fusion.4
  41.4 1.9 %broadcast_add_fusion = (s32[64]{0:T(128)S(1)}, s32[64]{0:T(128)S(1)}, f32[64]{0:T(128)S(1)}) fusion(s32[]{:T(128)} %get-tuple-element.9, s32[64]{0:T(128)} %param.24, s32[]{:T(128)} %get-tuple-element.8), kind=kLoop, calls=%fused_computation.101 | loop fusion | flops 256 | bytes 1032 | tf_op jit(solution)/shard_map/add | solution.py:135
  43.4 1.4 gather_fusion
  45.1 0.8 gather_fusion.1
  46.6 0.7 iota_compare_fusion.3
  48.1 0.5 copy-done.2
  48.8 0.6 gather_fusion.2
  49.5 0.8 gather_fusion.3
  50.3 0.9 broadcast_select_fusion
  51.3 10.3 %all-to-all-start.1 = ((bf16[64,2,4,256]{3,2,1,0:T(4,128)(2,1)}), bf16[64,2,4,256]{3,2,1,0:T(4,128)(2,1)S(1)}, u32[]{:S(2)}, u32[]{:S(2)}) async-start(bf16[64,2,4,256]{3,2,1,0:T(4,128)(2,1)} %broadcast_select_fusion), calls=%async_computation.1 | async-start | bytes 524288 | tf_op jit(solution)/shard_map/all_to_all | solution.py:106
  61.7 0.4 select_reduce_fusion.1
  62.4 11.2 %all-to-all-done.1 = bf16[64,2,4,256]{3,2,1,0:T(4,128)(2,1)S(1)} async-done(((bf16[64,2,4,256]{3,2,1,0:T(4,128)(2,1)}), bf16[64,2,4,256]{3,2,1,0:T(4,128)(2,1)S(1)}, u32[]{:S(2)}, u32[]{:S(2)}) %all-to-all-start.1) | async-done | bytes 262176 | tf_op jit(solution)/shard_map/all_to_all | solution.py:106
  73.8 0.4 select_reduce_fusion
  74.3 0.3 convert_reduce_fusion.1
  74.6 0.3 fusion.5
  75.0 0.3 fusion.7
  75.4 3.3 %collective-permute-start.1 = (bf16[64,896]{1,0:T(8,128)(2,1)S(1)}, bf16[64,896]{1,0:T(8,128)(2,1)S(1)}, u32[]{:S(2)}, u32[]{:S(2)}) collective-permute-start(bf16[64,896]{1,0:T(8,128)(2,1)S(1)} %bitcast.76), channel_id=1, source_target_pairs={{0,0},{1,8},{2,128},{3,136},{4,256},{5,264},{6,384},{7,392},{8,16}... | collective-permute-start | bytes 344072 | tf_op jit(solution)/shard_map/ppermute | solution.py:171
  78.7 10.8 %collective-permute-done.1 = bf16[64,896]{1,0:T(8,128)(2,1)S(1)} collective-permute-done((bf16[64,896]{1,0:T(8,128)(2,1)S(1)}, bf16[64,896]{1,0:T(8,128)(2,1)S(1)}, u32[]{:S(2)}, u32[]{:S(2)}) %collective-permute-start.1) | collective-permute-done | bytes 114720 | tf_op jit(solution)/shard_map/ppermute | solution.py:171
  89.6 46.5 %all_to_all.20 = bf16[8,64,896]{2,1,0:T(8,128)(2,1)S(1)} all-to-all(bf16[8,64,896]{2,1,0:T(8,128)(2,1)S(1)} %broadcast_in_dim.117), channel_id=1, replica_groups=mesh['x'=4,'z'=8,'c'=2,'mlp'=8] {'z'}, dimensions={0} | all-to-all | bytes 1835008 | tf_op jit(solution)/shard_map/all_to_all | solution.py:173
  136.1 2.6 %convolution_convert_fusion = bf16[512,896]{1,0:T(8,128)(2,1)S(1)} fusion(bf16[512,896]{1,0:T(8,128)(2,1)S(1)} %bitcast.74, bf16[896,896]{0,1:T(8,128)(2,1)} %all-gather.2.cloned.1.call-done), kind=kOutput, calls=%fused_computation.5 | convolution fusion | flops 822542336 | bytes 3440640 | tf_op jit(solution)/shard_map/dot_general | solution.py:174
  138.7 0.5 copy.35
  139.3 20.9 %all_to_all.21 = bf16[8,512,112]{1,2,0:T(8,128)(2,1)S(1)} all-to-all(bf16[8,512,112]{1,2,0:T(8,128)(2,1)S(1)} %bitcast.72), channel_id=1, replica_groups=mesh['x'=4,'z'=8,'c'=2,'mlp'=8] {'x','c'}, dimensions={0} | all-to-all | bytes 1835008 | tf_op jit(solution)/shard_map/all_to_all | solution.py:178
  160.3 0.7 add_convert_fusion
  (63 shorter events, 3.0 us)
Async XLA Ops:
  7.2 37.9 %copy-start = (s32[74]{0:T(128)S(1)}, s32[74]{0:T(128)}, u32[]{:S(2)}) copy-start(s32[74]{0:T(128)} %param.25) | copy-start | bytes 892
  7.2 39.0 %copy-start.10 = (s32[74]{0:T(128)S(1)}, s32[74]{0:T(128)}, u32[]{:S(2)}) copy-start(s32[74]{0:T(128)} %param.27) | copy-start | bytes 892
  7.2 39.0 %copy-start.8 = (bf16[64,128]{1,0:T(8,128)(2,1)S(1)}, bf16[64,128]{1,0:T(8,128)(2,1)}, u32[]{:S(2)}) copy-start(bf16[64,128]{1,0:T(8,128)(2,1)} %param.15) | copy-start | bytes 49156
  7.2 40.3 %copy-start.9 = (bf16[64,128]{1,0:T(8,128)(2,1)S(1)}, bf16[64,128]{1,0:T(8,128)(2,1)}, u32[]{:S(2)}) copy-start(bf16[64,128]{1,0:T(8,128)(2,1)} %param.16) | copy-start | bytes 49156
  7.2 40.4 %copy-start.6 = (bf16[320,128]{1,0:T(8,128)(2,1)S(1)}, bf16[320,128]{1,0:T(8,128)(2,1)}, u32[]{:S(2)}) copy-start(bf16[320,128]{1,0:T(8,128)(2,1)} %param.17) | copy-start | bytes 245764
  7.2 40.4 %copy-start.5 = (bf16[320,128]{1,0:T(8,128)(2,1)S(1)}, bf16[320,128]{1,0:T(8,128)(2,1)}, u32[]{:S(2)}) copy-start(bf16[320,128]{1,0:T(8,128)(2,1)} %param.18) | copy-start | bytes 245764
  7.2 40.8 %copy-start.4 = (bf16[64,896]{1,0:T(8,128)(2,1)S(1)}, bf16[64,896]{1,0:T(8,128)(2,1)}, u32[]{:S(2)}) copy-start(bf16[64,896]{1,0:T(8,128)(2,1)} %param.14) | copy-start | bytes 344068
  7.2 40.7 %collective-permute-start = (bf16[896,112]{0,1:T(8,128)(2,1)}, bf16[896,112]{0,1:T(8,128)(2,1)S(1)}, u32[]{:S(2)}, u32[]{:S(2)}) collective-permute-start(bf16[896,112]{0,1:T(8,128)(2,1)} %param.21), channel_id=1, source_target_pairs={{0,0},{1,8},{2,128},{3,136},{4,256},{5,264},{6,384},{7,392},{8,1},... | collective-permute-start | bytes 602120 | tf_op jit(solution)/shard_map/ppermute | solution.py:113
  13.6 35.3 %all-to-all-start = ((bf16[64,4,256]{2,1,0:T(4,128)(2,1)}), bf16[64,4,256]{2,1,0:T(4,128)(2,1)S(1)}, u32[]{:S(2)}, u32[]{:S(2)}) async-start(bf16[64,4,256]{2,1,0:T(4,128)(2,1)} %reshape.317), calls=%async_computation | async-start | bytes 262144 | tf_op jit(solution)/shard_map/all_to_all | solution.py:97
  31.5 104.6 %all-gather.2.cloned.1.call-start = ((), (), s32[]{:S(2)}) async-start(), calls=%async_computation.4 | async-start | bytes 1806336 | tf_op jit(solution)/shard_map/all_gather | solution.py:115
  47.8 13.9 %copy-start.1 = (bf16[320,128]{1,0:T(8,128)(2,1)}, bf16[320,128]{1,0:T(8,128)(2,1)S(1)}, u32[]{:S(2)}) copy-start(bf16[320,128]{1,0:T(8,128)(2,1)S(1)} %get-tuple-element.24) | copy-start | bytes 245764
  47.8 27.1 %copy-start.7 = (bf16[320,128]{1,0:T(8,128)(2,1)}, bf16[320,128]{1,0:T(8,128)(2,1)S(1)}, u32[]{:S(2)}) copy-start(bf16[320,128]{1,0:T(8,128)(2,1)S(1)} %get-tuple-element.23) | copy-start | bytes 245764
  48.0 0.7 copy-start.2
  51.3 22.3 %all-to-all-start.1 = ((bf16[64,2,4,256]{3,2,1,0:T(4,128)(2,1)}), bf16[64,2,4,256]{3,2,1,0:T(4,128)(2,1)S(1)}, u32[]{:S(2)}, u32[]{:S(2)}) async-start(bf16[64,2,4,256]{3,2,1,0:T(4,128)(2,1)} %broadcast_select_fusion), calls=%async_computation.1 | async-start | bytes 524288 | tf_op jit(solution)/shard_map/all_to_all | solution.py:106
  75.4 14.1 %collective-permute-start.1 = (bf16[64,896]{1,0:T(8,128)(2,1)S(1)}, bf16[64,896]{1,0:T(8,128)(2,1)S(1)}, u32[]{:S(2)}, u32[]{:S(2)}) collective-permute-start(bf16[64,896]{1,0:T(8,128)(2,1)S(1)} %bitcast.76), channel_id=1, source_target_pairs={{0,0},{1,8},{2,128},{3,136},{4,256},{5,264},{6,384},{7,392},{8,16}... | collective-permute-start | bytes 344072 | tf_op jit(solution)/shard_map/ppermute | solution.py:171
  139.3 21.0 %copy-start.3 = (bf16[512,112]{0,1:T(8,128)(2,1)S(1)}, bf16[512,112]{0,1:T(8,128)(2,1)}, u32[]{:S(2)}) copy-start(bf16[512,112]{0,1:T(8,128)(2,1)} %param.22) | copy-start | bytes 344068
Sparse Core Ops, SparseCore 0:
  48.8 41.4 all-gather.1

commit v12 on v9

--- a/solution.py
+++ b/solution.py
@@ -13,7 +13,7 @@
 THETA = 5000000.0
 NEG = -1e30
 TOK = ("x", "z", "c")
-GROUP = ("x", "c")
+GROUP = ("z",)
 
 
 def apply_rotary(values, position, heads):
@@ -159,17 +159,20 @@
         (final[2] / final[1][..., None]).reshape(tok_rows, q_heads * width).astype(jnp.bfloat16)
     )
 
-    z_count = tok_count // group_count
     c_count = lax.axis_size("c")
     spread_route = []
     for t in range(tok_count):
         for g in range(mlp_count):
-            x_to, c_to, z_to, m_to = g // c_count, g % c_count, t % z_count, t // z_count
+            piece, m_to = t % group_count, t // group_count
+            x_to, c_to = piece // c_count, piece % c_count
             spread_route.append(
-                (t * mlp_count + g, ((x_to * z_count + z_to) * c_count + c_to) * mlp_count + m_to)
+                (
+                    t * mlp_count + g,
+                    ((x_to * group_count + g) * c_count + c_to) * mlp_count + m_to,
+                )
             )
     token_here = lax.ppermute(attended_local, TOK + ("mlp",), spread_route)
-    token_block = lax.all_gather(token_here, "z", axis=0, tiled=True)
+    token_block = lax.all_gather(token_here, ("x", "c"), axis=0, tiled=True)
     projected = jnp.dot(token_block, weight_cols, preferred_element_type=jnp.float32).astype(
         jnp.bfloat16
     )

time: 165 us -> 159 us (0.964)
  blocking collectives: 64.2 us -> 75.3 us
  waiting for transfers between devices: 22 us -> 11.2 us
  starting transfers between devices: 36.3 us -> 30.1 us
    ppermute x1, waiting for transfers between devices: 10.8 us -> 0.01 us  [body(): token_here = lax.ppermute(attended_local, TOK + ('mlp',), spread_route)]
    all_to_all x1, blocking collectives: 24 us -> 32.1 us  [body(): arrived = lax.all_to_all(parts, GROUP, 0, 0, tiled=True)]
    ppermute x1, starting transfers between devices: 4.73 us -> 1.72 us  [body(): weight_here = lax.ppermute(out_weight, GROUP + ('mlp',), swap)]
    all_gather x1, blocking collectives: 40.2 us -> 43.1 us  [body(): token_block = lax.all_gather(token_here, ('x', 'c'), axis=0, tiled=True)]
    ppermute x1, starting transfers between devices: 3.29 us -> 0.67 us  [body(): token_here = lax.ppermute(attended_local, TOK + ('mlp',), spread_route)]
  transfers between devices with their start and end apart: 5 -> 5, of which waited for: 2 -> 1; matrix products, arithmetic and copies ran while one was open for 14% -> 14% of each run, Pallas kernels for 0% -> 0%
where the time goes in v12:
time: 159 us
  blocking collectives  75.3 us (47%)
  starting transfers between devices  30.1 us (19%)
  between operations  15.1 us (9%)
  other arithmetic  14.1 us (9%)
  waiting for transfers between devices  11.2 us (7%)
  local copies, waits for them, and re-layouts  8.5 us (5%)
  matrix products  4.28 us (3%)
    all_gather x1, blocking collectives, body(): token_block = lax.all_gather(token_here, ('x', 'c'), axis=0, tiled=True)  43.1 us
    all_to_all x1, blocking collectives, body(): arrived = lax.all_to_all(parts, GROUP, 0, 0, tiled=True)  32.1 us
    all_to_all x1, starting transfers between devices, body(): spread = lax.all_to_all(pieces, TOK, 0, 0, tiled=True)  17.3 us
    all_to_all x1, waiting for transfers between devices, body(): incoming = lax.all_to_all(outgoing, TOK, 0, 0, tiled=True)  11.2 us
    all_to_all x1, starting transfers between devices, body(): incoming = lax.all_to_all(outgoing, TOK, 0, 0, tiled=True)  10.3 us
    reduce_sum x3, other arithmetic, lookup(): return jnp.sum(jnp.where(jnp.arange(table.shape[0]) == index, table, 0))  5.9 us
  transfers between devices with their start and end apart: 5, of which 1 were waited for; matrix products, arithmetic and copies ran while one was open for 14% of the time, Pallas kernels for 0%

profile of v12, /device:TPU:1, one launch (start us, length us, event | category | flops | bytes accessed | tf_op | source)
XLA Modules:
  0.0 158.6 jit_solution(6479278825931612464)
XLA Ops:
  7.2 1.7 %collective-permute-start = (bf16[896,112]{0,1:T(8,128)(2,1)}, bf16[896,112]{0,1:T(8,128)(2,1)S(1)}, u32[]{:S(2)}, u32[]{:S(2)}) collective-permute-start(bf16[896,112]{0,1:T(8,128)(2,1)} %param.21), channel_id=1, source_target_pairs={{0,0},{1,16},{2,32},{3,48},{4,64},{5,80},{6,96},{7,112},{16,1},{17... | collective-permute-start | bytes 602120 | tf_op jit(solution)/shard_map/ppermute | solution.py:113
  9.0 0.9 pad_maximum_fusion
  9.8 0.7 reshape.313
  10.5 17.3 %all-to-all-start = ((bf16[64,4,256]{2,1,0:T(4,128)(2,1)}), bf16[64,4,256]{2,1,0:T(4,128)(2,1)S(1)}, u32[]{:S(2)}, u32[]{:S(2)}) async-start(bf16[64,4,256]{2,1,0:T(4,128)(2,1)} %reshape.313), calls=%async_computation | async-start | bytes 262144 | tf_op jit(solution)/shard_map/all_to_all | solution.py:97
  27.9 0.8 reshape.312
  28.7 1.3 dynamic_slice.3
  30.6 1.3 fusion.32
  31.9 1.9 %fusion.34 = s32[]{:T(128)} fusion(s32[74]{0:T(128)} %param.25, s32[]{:T(128)} %fusion.32), kind=kLoop, calls=%fused_computation.95 | loop fusion | flops 221 | bytes 304 | tf_op jit(solution)/shard_map/reduce_sum | solution.py:62
  33.9 2.7 %fusion.33 = (s32[]{:T(128)}, s32[]{:T(128)}, s32[]{:T(128)}) fusion(s32[74]{0:T(128)} %param.26, s32[]{:T(128)} %bitcast, s32[]{:T(128)} %fusion.34, s32[]{:T(128)} %fusion.32), kind=kLoop, calls=%fused_computation.94 | loop fusion | flops 663 | bytes 320 | tf_op jit(solution)/shard_map/reduce_sum | solution.py:62
  36.5 1.2 iota_compare_fusion.4
  37.7 1.9 %broadcast_add_fusion = (s32[64]{0:T(128)S(1)}, s32[64]{0:T(128)S(1)}, f32[64]{0:T(128)S(1)}) fusion(s32[]{:T(128)} %get-tuple-element.9, s32[64]{0:T(128)} %param.24, s32[]{:T(128)} %get-tuple-element.8), kind=kLoop, calls=%fused_computation.101 | loop fusion | flops 256 | bytes 1032 | tf_op jit(solution)/shard_map/add | solution.py:135
  39.8 1.4 gather_fusion
  41.5 0.8 gather_fusion.1
  43.0 0.7 iota_compare_fusion.3
  44.5 0.5 copy-done.2
  45.2 0.6 gather_fusion.2
  45.9 0.8 gather_fusion.3
  46.7 0.9 broadcast_select_fusion
  47.7 10.3 %all-to-all-start.1 = ((bf16[64,2,4,256]{3,2,1,0:T(4,128)(2,1)}), bf16[64,2,4,256]{3,2,1,0:T(4,128)(2,1)S(1)}, u32[]{:S(2)}, u32[]{:S(2)}) async-start(bf16[64,2,4,256]{3,2,1,0:T(4,128)(2,1)} %broadcast_select_fusion), calls=%async_computation.1 | async-start | bytes 524288 | tf_op jit(solution)/shard_map/all_to_all | solution.py:106
  58.1 0.4 select_reduce_fusion.1
  58.5 0.3 convert_reduce_fusion.2
  58.8 11.2 %all-to-all-done.1 = bf16[64,2,4,256]{3,2,1,0:T(4,128)(2,1)S(1)} async-done(((bf16[64,2,4,256]{3,2,1,0:T(4,128)(2,1)}), bf16[64,2,4,256]{3,2,1,0:T(4,128)(2,1)S(1)}, u32[]{:S(2)}, u32[]{:S(2)}) %all-to-all-start.1) | async-done | bytes 262176 | tf_op jit(solution)/shard_map/all_to_all | solution.py:106
  70.2 0.4 select_reduce_fusion
  70.6 0.3 convert_reduce_fusion.1
  71.0 0.3 fusion.5
  71.3 0.3 fusion.7
  71.8 0.7 collective-permute-start.1
  72.5 43.1 %all_gather.6 = bf16[512,896]{1,0:T(8,128)(2,1)S(1)} all-gather(bf16[64,896]{1,0:T(8,128)(2,1)S(1)} %collective-permute-done.1), channel_id=1, replica_groups=mesh['x'=4,'z'=8,'c'=2,'mlp'=8] {'x','c'}, dimensions={0}, use_global_device_ids=true | all-gather | bytes 1032192 | tf_op jit(solution)/shard_map/all_gather | solution.py:175
  115.6 2.6 %convolution_convert_fusion = bf16[512,896]{1,0:T(8,128)(2,1)S(1)} fusion(bf16[512,896]{1,0:T(8,128)(2,1)S(1)} %all_gather.6, bf16[896,896]{0,1:T(8,128)(2,1)} %all-gather.2.cloned.1.call-done), kind=kOutput, calls=%fused_computation.5 | convolution fusion | flops 822542336 | bytes 3440640 | tf_op jit(solution)/shard_map/dot_general | solution.py:176
  118.3 0.5 copy.35
  118.8 32.1 %all_to_all.15 = bf16[8,512,112]{1,2,0:T(8,128)(2,1)S(1)} all-to-all(bf16[8,512,112]{1,2,0:T(8,128)(2,1)S(1)} %bitcast.71), channel_id=1, replica_groups=mesh['x'=4,'z'=8,'c'=2,'mlp'=8] {'z'}, dimensions={0} | all-to-all | bytes 1835008 | tf_op jit(solution)/shard_map/all_to_all | solution.py:180
  151.1 0.7 add_convert_fusion
  (62 shorter events, 2.6 us)
Async XLA Ops:
  7.2 34.3 %copy-start = (s32[74]{0:T(128)S(1)}, s32[74]{0:T(128)}, u32[]{:S(2)}) copy-start(s32[74]{0:T(128)} %param.25) | copy-start | bytes 892
  7.2 35.3 %copy-start.10 = (s32[74]{0:T(128)S(1)}, s32[74]{0:T(128)}, u32[]{:S(2)}) copy-start(s32[74]{0:T(128)} %param.27) | copy-start | bytes 892
  7.2 35.4 %copy-start.8 = (bf16[64,128]{1,0:T(8,128)(2,1)S(1)}, bf16[64,128]{1,0:T(8,128)(2,1)}, u32[]{:S(2)}) copy-start(bf16[64,128]{1,0:T(8,128)(2,1)} %param.15) | copy-start | bytes 49156
  7.2 36.7 %copy-start.9 = (bf16[64,128]{1,0:T(8,128)(2,1)S(1)}, bf16[64,128]{1,0:T(8,128)(2,1)}, u32[]{:S(2)}) copy-start(bf16[64,128]{1,0:T(8,128)(2,1)} %param.16) | copy-start | bytes 49156
  7.2 36.8 %copy-start.6 = (bf16[320,128]{1,0:T(8,128)(2,1)S(1)}, bf16[320,128]{1,0:T(8,128)(2,1)}, u32[]{:S(2)}) copy-start(bf16[320,128]{1,0:T(8,128)(2,1)} %param.17) | copy-start | bytes 245764
  7.2 36.8 %copy-start.5 = (bf16[320,128]{1,0:T(8,128)(2,1)S(1)}, bf16[320,128]{1,0:T(8,128)(2,1)}, u32[]{:S(2)}) copy-start(bf16[320,128]{1,0:T(8,128)(2,1)} %param.18) | copy-start | bytes 245764
  7.2 37.1 %copy-start.4 = (bf16[64,896]{1,0:T(8,128)(2,1)S(1)}, bf16[64,896]{1,0:T(8,128)(2,1)}, u32[]{:S(2)}) copy-start(bf16[64,896]{1,0:T(8,128)(2,1)} %param.14) | copy-start | bytes 344068
  7.2 37.1 %collective-permute-start = (bf16[896,112]{0,1:T(8,128)(2,1)}, bf16[896,112]{0,1:T(8,128)(2,1)S(1)}, u32[]{:S(2)}, u32[]{:S(2)}) collective-permute-start(bf16[896,112]{0,1:T(8,128)(2,1)} %param.21), channel_id=1, source_target_pairs={{0,0},{1,16},{2,32},{3,48},{4,64},{5,80},{6,96},{7,112},{16,1},{17... | collective-permute-start | bytes 602120 | tf_op jit(solution)/shard_map/ppermute | solution.py:113
  10.5 34.7 %all-to-all-start = ((bf16[64,4,256]{2,1,0:T(4,128)(2,1)}), bf16[64,4,256]{2,1,0:T(4,128)(2,1)S(1)}, u32[]{:S(2)}, u32[]{:S(2)}) async-start(bf16[64,4,256]{2,1,0:T(4,128)(2,1)} %reshape.313), calls=%async_computation | async-start | bytes 262144 | tf_op jit(solution)/shard_map/all_to_all | solution.py:97
  27.9 87.7 %all-gather.2.cloned.1.call-start = ((), (), s32[]{:S(2)}) async-start(), calls=%async_computation.3 | async-start | bytes 1806336 | tf_op jit(solution)/shard_map/all_gather | solution.py:115
  44.2 13.9 %copy-start.1 = (bf16[320,128]{1,0:T(8,128)(2,1)}, bf16[320,128]{1,0:T(8,128)(2,1)S(1)}, u32[]{:S(2)}) copy-start(bf16[320,128]{1,0:T(8,128)(2,1)S(1)} %get-tuple-element.24) | copy-start | bytes 245764
  44.2 27.1 %copy-start.7 = (bf16[320,128]{1,0:T(8,128)(2,1)}, bf16[320,128]{1,0:T(8,128)(2,1)S(1)}, u32[]{:S(2)}) copy-start(bf16[320,128]{1,0:T(8,128)(2,1)S(1)} %get-tuple-element.23) | copy-start | bytes 245764
  44.4 0.7 copy-start.2
  47.7 22.3 %all-to-all-start.1 = ((bf16[64,2,4,256]{3,2,1,0:T(4,128)(2,1)}), bf16[64,2,4,256]{3,2,1,0:T(4,128)(2,1)S(1)}, u32[]{:S(2)}, u32[]{:S(2)}) async-start(bf16[64,2,4,256]{3,2,1,0:T(4,128)(2,1)} %broadcast_select_fusion), calls=%async_computation.1 | async-start | bytes 524288 | tf_op jit(solution)/shard_map/all_to_all | solution.py:106
  71.8 0.7 collective-permute-start.1
  118.8 32.3 %copy-start.3 = (bf16[512,112]{0,1:T(8,128)(2,1)S(1)}, bf16[512,112]{0,1:T(8,128)(2,1)}, u32[]{:S(2)}) copy-start(bf16[512,112]{0,1:T(8,128)(2,1)} %param.22) | copy-start | bytes 344068
Sparse Core Ops, SparseCore 0:
  45.2 60.5 all-gather.1

commit v13 on v12

--- a/solution.py
+++ b/solution.py
@@ -95,6 +95,7 @@
     piece_rows = node_rows // tok_count
     pieces = my_pair.reshape(tok_count, piece_rows, my_pair.shape[1])
     spread = lax.all_to_all(pieces, TOK, 0, 0, tiled=True)
+    spread, queries = lax.optimization_barrier((spread, queries))
     held = jnp.take(spread, node_owner[:shared_count], axis=0)
     requests = token_request.reshape(-1, tok_rows)[:, 0]
     middles = parents[shared_count + requests]

time: 159 us -> 162 us (1.019)
  starting transfers between devices: 30.1 us -> 34.9 us
  other arithmetic: 14.1 us -> 11.6 us
    all_to_all x1, starting transfers between devices: 10.3 us -> 17.8 us  [body(): incoming = lax.all_to_all(outgoing, TOK, 0, 0, tiled=True)]
    all_to_all x1, starting transfers between devices: 17.3 us -> 14.8 us  [body(): spread = lax.all_to_all(pieces, TOK, 0, 0, tiled=True)]
    reduce_sum x3, other arithmetic: 5.9 us -> 3.9 us  [lookup(): return jnp.sum(jnp.where(jnp.arange(table.shape[0]) == index, table, 0))]
  transfers between devices with their start and end apart: 5 -> 5, of which waited for: 1 -> 1; matrix products, arithmetic and copies ran while one was open for 14% -> 11% of each run, Pallas kernels for 0% -> 0%
where the time goes in v13:
time: 162 us; the launch traced here: 161 us
  blocking collectives  75.4 us (47%)
  starting transfers between devices  34.9 us (22%)
  between operations  15.2 us (9%)
  other arithmetic  11.6 us (7%)
  waiting for transfers between devices  11.1 us (7%)
  local copies, waits for them, and re-layouts  8.68 us (5%)
  matrix products  4.27 us (3%)
    all_gather x1, blocking collectives, body(): token_block = lax.all_gather(token_here, ('x', 'c'), axis=0, tiled=True)  42.3 us
    all_to_all x1, blocking collectives, body(): arrived = lax.all_to_all(parts, GROUP, 0, 0, tiled=True)  33.1 us
    all_to_all x1, starting transfers between devices, body(): incoming = lax.all_to_all(outgoing, TOK, 0, 0, tiled=True)  17.8 us
    all_to_all x1, starting transfers between devices, body(): spread = lax.all_to_all(pieces, TOK, 0, 0, tiled=True)  14.8 us
    all_to_all x1, waiting for transfers between devices, body(): incoming = lax.all_to_all(outgoing, TOK, 0, 0, tiled=True)  11 us
    reduce_sum x3, other arithmetic, lookup(): return jnp.sum(jnp.where(jnp.arange(table.shape[0]) == index, table, 0))  3.9 us
  transfers between devices with their start and end apart: 5, of which 1 were waited for; matrix products, arithmetic and copies ran while one was open for 11% of the time, Pallas kernels for 0%

profile of v13, /device:TPU:1, one launch (start us, length us, event | category | flops | bytes accessed | tf_op | source)
XLA Modules:
  0.0 161.0 jit_solution(1132799021262604380)
XLA Ops:
  7.2 1.0 pad_maximum_fusion
  8.2 0.7 reshape.313
  8.9 14.8 %all-to-all-start = ((bf16[64,4,256]{2,1,0:T(4,128)(2,1)}), bf16[64,4,256]{2,1,0:T(4,128)(2,1)S(1)}, u32[]{:S(2)}, u32[]{:S(2)}) async-start(bf16[64,4,256]{2,1,0:T(4,128)(2,1)} %reshape.313), calls=%async_computation | async-start | bytes 262144 | tf_op jit(solution)/shard_map/all_to_all | solution.py:97
  23.8 1.6 collective-permute-start
  25.4 0.8 reshape.312
  26.3 1.4 gather_fusion
  28.0 0.8 gather_fusion.1
  28.8 1.3 dynamic_slice.3
  30.7 0.6 fusion.32
  31.3 1.3 fusion.34
  32.6 2.0 %fusion.33 = (s32[]{:T(128)}, s32[]{:T(128)}, s32[]{:T(128)}) fusion(s32[74]{0:T(128)S(1)} %copy-done.10, s32[]{:T(128)} %bitcast, s32[]{:T(128)} %fusion.34, s32[]{:T(128)} %fusion.32), kind=kLoop, calls=%fused_computation.94 | loop fusion | flops 663 | bytes 320 | tf_op jit(solution)/shard_map/reduce_sum | solution.py:62
  34.6 1.3 iota_compare_fusion.4
  35.9 1.3 broadcast_add_fusion
  37.9 0.7 iota_compare_fusion.3
  39.3 0.7 copy-done.2
  40.0 0.6 gather_fusion.2
  40.6 0.8 gather_fusion.3
  41.5 0.9 broadcast_select_fusion
  42.6 17.8 %all-to-all-start.1 = ((bf16[64,2,4,256]{3,2,1,0:T(4,128)(2,1)}), bf16[64,2,4,256]{3,2,1,0:T(4,128)(2,1)S(1)}, u32[]{:S(2)}, u32[]{:S(2)}) async-start(bf16[64,2,4,256]{3,2,1,0:T(4,128)(2,1)} %broadcast_select_fusion), calls=%async_computation.1 | async-start | bytes 524288 | tf_op jit(solution)/shard_map/all_to_all | solution.py:107
  60.6 0.4 select_reduce_fusion.1
  61.0 0.3 convert_reduce_fusion.2
  61.3 11.0 %all-to-all-done.1 = bf16[64,2,4,256]{3,2,1,0:T(4,128)(2,1)S(1)} async-done(((bf16[64,2,4,256]{3,2,1,0:T(4,128)(2,1)}), bf16[64,2,4,256]{3,2,1,0:T(4,128)(2,1)S(1)}, u32[]{:S(2)}, u32[]{:S(2)}) %all-to-all-start.1) | async-done | bytes 262176 | tf_op jit(solution)/shard_map/all_to_all | solution.py:107
  72.5 0.4 select_reduce_fusion
  73.0 0.3 convert_reduce_fusion.1
  73.3 0.3 fusion.5
  73.7 0.3 fusion.7
  74.1 0.7 collective-permute-start.1
  74.8 42.3 %all_gather.6 = bf16[512,896]{1,0:T(8,128)(2,1)S(1)} all-gather(bf16[64,896]{1,0:T(8,128)(2,1)S(1)} %collective-permute-done.1), channel_id=1, replica_groups=mesh['x'=4,'z'=8,'c'=2,'mlp'=8] {'x','c'}, dimensions={0}, use_global_device_ids=true | all-gather | bytes 1032192 | tf_op jit(solution)/shard_map/all_gather | solution.py:176
  117.1 2.6 %convolution_convert_fusion = bf16[512,896]{1,0:T(8,128)(2,1)S(1)} fusion(bf16[512,896]{1,0:T(8,128)(2,1)S(1)} %all_gather.6, bf16[896,896]{0,1:T(8,128)(2,1)} %all-gather.2.cloned.1.call-done), kind=kOutput, calls=%fused_computation.5 | convolution fusion | flops 822542336 | bytes 3440640 | tf_op jit(solution)/shard_map/dot_general | solution.py:177
  119.7 0.5 copy.35
  120.3 33.1 %all_to_all.15 = bf16[8,512,112]{1,2,0:T(8,128)(2,1)S(1)} all-to-all(bf16[8,512,112]{1,2,0:T(8,128)(2,1)S(1)} %bitcast.71), channel_id=1, replica_groups=mesh['x'=4,'z'=8,'c'=2,'mlp'=8] {'z'}, dimensions={0} | all-to-all | bytes 1835008 | tf_op jit(solution)/shard_map/all_to_all | solution.py:181
  153.5 0.7 add_convert_fusion
  (66 shorter events, 2.6 us)
Async XLA Ops:
  7.2 20.8 %copy-start = (s32[74]{0:T(128)S(1)}, s32[74]{0:T(128)}, u32[]{:S(2)}) copy-start(s32[74]{0:T(128)} %param.25) | copy-start | bytes 892
  7.2 25.4 %copy-start.10 = (s32[74]{0:T(128)S(1)}, s32[74]{0:T(128)}, u32[]{:S(2)}) copy-start(s32[74]{0:T(128)} %param.26) | copy-start | bytes 892
  7.2 28.7 %copy-start.11 = (s32[64]{0:T(128)S(1)}, s32[64]{0:T(128)}, u32[]{:S(2)}) copy-start(s32[64]{0:T(128)} %param.24) | copy-start | bytes 772
  7.2 30.2 %copy-start.12 = (s32[74]{0:T(128)S(1)}, s32[74]{0:T(128)}, u32[]{:S(2)}) copy-start(s32[74]{0:T(128)} %param.27) | copy-start | bytes 892
  7.2 30.3 %copy-start.8 = (bf16[64,128]{1,0:T(8,128)(2,1)S(1)}, bf16[64,128]{1,0:T(8,128)(2,1)}, u32[]{:S(2)}) copy-start(bf16[64,128]{1,0:T(8,128)(2,1)} %param.15) | copy-start | bytes 49156
  7.2 31.4 %copy-start.9 = (bf16[64,128]{1,0:T(8,128)(2,1)S(1)}, bf16[64,128]{1,0:T(8,128)(2,1)}, u32[]{:S(2)}) copy-start(bf16[64,128]{1,0:T(8,128)(2,1)} %param.16) | copy-start | bytes 49156
  7.2 31.6 %copy-start.6 = (bf16[320,128]{1,0:T(8,128)(2,1)S(1)}, bf16[320,128]{1,0:T(8,128)(2,1)}, u32[]{:S(2)}) copy-start(bf16[320,128]{1,0:T(8,128)(2,1)} %param.17) | copy-start | bytes 245764
  7.2 31.6 %copy-start.5 = (bf16[320,128]{1,0:T(8,128)(2,1)S(1)}, bf16[320,128]{1,0:T(8,128)(2,1)}, u32[]{:S(2)}) copy-start(bf16[320,128]{1,0:T(8,128)(2,1)} %param.18) | copy-start | bytes 245764
  8.9 30.3 %all-to-all-start = ((bf16[64,4,256]{2,1,0:T(4,128)(2,1)}), bf16[64,4,256]{2,1,0:T(4,128)(2,1)S(1)}, u32[]{:S(2)}, u32[]{:S(2)}) async-start(bf16[64,4,256]{2,1,0:T(4,128)(2,1)} %reshape.313), calls=%async_computation | async-start | bytes 262144 | tf_op jit(solution)/shard_map/all_to_all | solution.py:97
  23.7 93.4 %all-gather.2.cloned.1.call-start = ((), (), s32[]{:S(2)}) async-start(), calls=%async_computation.3 | async-start | bytes 1806336 | tf_op jit(solution)/shard_map/all_gather | solution.py:116
  23.8 15.5 %collective-permute-start = (bf16[896,112]{0,1:T(8,128)(2,1)}, bf16[896,112]{0,1:T(8,128)(2,1)S(1)}, u32[]{:S(2)}, u32[]{:S(2)}) collective-permute-start(bf16[896,112]{0,1:T(8,128)(2,1)} %param.21), channel_id=1, source_target_pairs={{0,0},{1,16},{2,32},{3,48},{4,64},{5,80},{6,96},{7,112},{16,1},{17... | collective-permute-start | bytes 602120 | tf_op jit(solution)/shard_map/ppermute | solution.py:114
  27.7 14.7 %copy-start.4 = (bf16[64,896]{1,0:T(8,128)(2,1)S(1)}, bf16[64,896]{1,0:T(8,128)(2,1)}, u32[]{:S(2)}) copy-start(bf16[64,896]{1,0:T(8,128)(2,1)} %param.14) | copy-start | bytes 344068
  39.0 21.6 %copy-start.1 = (bf16[320,128]{1,0:T(8,128)(2,1)}, bf16[320,128]{1,0:T(8,128)(2,1)S(1)}, u32[]{:S(2)}) copy-start(bf16[320,128]{1,0:T(8,128)(2,1)S(1)} %get-tuple-element.28) | copy-start | bytes 245764
  39.0 34.7 %copy-start.7 = (bf16[320,128]{1,0:T(8,128)(2,1)}, bf16[320,128]{1,0:T(8,128)(2,1)S(1)}, u32[]{:S(2)}) copy-start(bf16[320,128]{1,0:T(8,128)(2,1)S(1)} %get-tuple-element.27) | copy-start | bytes 245764
  39.2 0.7 copy-start.2
  42.6 29.8 %all-to-all-start.1 = ((bf16[64,2,4,256]{3,2,1,0:T(4,128)(2,1)}), bf16[64,2,4,256]{3,2,1,0:T(4,128)(2,1)S(1)}, u32[]{:S(2)}, u32[]{:S(2)}) async-start(bf16[64,2,4,256]{3,2,1,0:T(4,128)(2,1)} %broadcast_select_fusion), calls=%async_computation.1 | async-start | bytes 524288 | tf_op jit(solution)/shard_map/all_to_all | solution.py:107
  74.1 0.7 collective-permute-start.1
  120.3 33.2 %copy-start.3 = (bf16[512,112]{0,1:T(8,128)(2,1)S(1)}, bf16[512,112]{0,1:T(8,128)(2,1)}, u32[]{:S(2)}) copy-start(bf16[512,112]{0,1:T(8,128)(2,1)} %param.22) | copy-start | bytes 344068
Sparse Core Ops, SparseCore 0:
  40.1 66.9 all-gather.1

commit v14 on v12

--- a/solution.py
+++ b/solution.py
@@ -112,7 +112,14 @@
     ]
     weight_here = lax.ppermute(out_weight, GROUP + ("mlp",), swap)
     weight_here, queries = lax.optimization_barrier((weight_here, queries))
-    weight_cols = lax.all_gather(weight_here, "mlp", axis=1, tiled=True)
+    arrivals = [weight_here]
+    for shift in range(1, mlp_count):
+        ring = [(m, (m + shift) % mlp_count) for m in range(mlp_count)]
+        arrivals.append(lax.ppermute(weight_here, "mlp", ring))
+    order = (lax.axis_index("mlp") - jnp.arange(mlp_count)) % mlp_count
+    weight_cols = jnp.concatenate(
+        list(jnp.take(jnp.stack(arrivals), order, axis=0)), axis=1
+    )
     query_turned = apply_rotary(queries, positions, q_heads)
     key_turned = apply_rotary(fresh_token_keys, positions, kv_heads)
     my_request = lax.dynamic_slice_in_dim(token_request, my_index * tok_rows, 1)[0]

time: 159 us -> 184 us (1.16)
  starting transfers between devices: 30.1 us -> 59.2 us
  between operations: 15.1 us -> 2.04 us
  local copies, waits for them, and re-layouts: 8.5 us -> 15.5 us
    ppermute x0 -> x7, starting transfers between devices: none -> 27.8 us  [body(): arrivals.append(lax.ppermute(weight_here, 'mlp', ring))]
    ppermute x0 -> x7, waiting for transfers between devices: none -> 11.7 us  [body(): arrivals.append(lax.ppermute(weight_here, 'mlp', ring))]
    all_to_all x1, waiting for transfers between devices: 11.2 us -> 0.01 us  [body(): incoming = lax.all_to_all(outgoing, TOK, 0, 0, tiled=True)]
    unnamed x23 -> x63, local copies, waits for them, and re-layouts: 0.58 us -> 5.99 us
    reduce_sum x3, other arithmetic: 5.9 us -> 3.91 us  [lookup(): return jnp.sum(jnp.where(jnp.arange(table.shape[0]) == index, table, 0))]
  transfers between devices with their start and end apart: 5 -> 11, of which waited for: 1 -> 2; matrix products, arithmetic and copies ran while one was open for 14% -> 15% of each run, Pallas kernels for 0% -> 0%
where the time goes in v14:
time: 184 us
  blocking collectives  76.7 us (42%)
  starting transfers between devices  59.2 us (32%)
  local copies, waits for them, and re-layouts  15.5 us (8%)
  other arithmetic  14.2 us (8%)
  waiting for transfers between devices  11.7 us (6%)
  matrix products  4.28 us (2%)
  between operations  2.04 us (1%)
    all_gather x1, blocking collectives, body(): token_block = lax.all_gather(token_here, ('x', 'c'), axis=0, tiled=True)  43.7 us
    all_to_all x1, blocking collectives, body(): arrived = lax.all_to_all(parts, GROUP, 0, 0, tiled=True)  33 us
    ppermute x7, starting transfers between devices, body(): arrivals.append(lax.ppermute(weight_here, 'mlp', ring))  27.8 us
    all_to_all x1, starting transfers between devices, body(): spread = lax.all_to_all(pieces, TOK, 0, 0, tiled=True)  17.3 us
    all_to_all x1, starting transfers between devices, body(): incoming = lax.all_to_all(outgoing, TOK, 0, 0, tiled=True)  11.7 us
    ppermute x7, waiting for transfers between devices, body(): arrivals.append(lax.ppermute(weight_here, 'mlp', ring))  11.7 us
    unnamed x63, local copies, waits for them, and re-layouts  5.99 us
    reduce_sum x3, other arithmetic, lookup(): return jnp.sum(jnp.where(jnp.arange(table.shape[0]) == index, table, 0))  3.91 us
  transfers between devices with their start and end apart: 11, of which 2 were waited for; matrix products, arithmetic and copies ran while one was open for 15% of the time, Pallas kernels for 0%

profile of v14, /device:TPU:1, one launch (start us, length us, event | category | flops | bytes accessed | tf_op | source)
XLA Modules:
  0.0 183.6 jit_solution(14066550684761673121)
XLA Ops:
  0.7 1.7 collective-permute-start
  2.4 0.9 pad_maximum_fusion
  4.0 17.3 %all-to-all-start = ((bf16[64,4,256]{2,1,0:T(4,128)(2,1)}), bf16[64,4,256]{2,1,0:T(4,128)(2,1)S(1)}, u32[]{:S(2)}, u32[]{:S(2)}) async-start(bf16[64,4,256]{2,1,0:T(4,128)(2,1)} %reshape.367), calls=%async_computation | async-start | bytes 262144 | tf_op jit(solution)/shard_map/all_to_all | solution.py:97
  21.9 0.8 reshape.366
  22.8 1.4 gather_fusion
  24.5 0.8 gather_fusion.1
  25.9 1.3 dynamic_slice.3
  28.5 1.3 fusion.42
  29.7 2.0 %fusion.41 = (s32[]{:T(128)}, s32[]{:T(128)}, s32[]{:T(128)}) fusion(s32[74]{0:T(128)S(1)} %copy-done.20, s32[]{:T(128)} %bitcast, s32[]{:T(128)} %fusion.42, s32[]{:T(128)} %fusion.40), kind=kLoop, calls=%fused_computation.130 | loop fusion | flops 663 | bytes 320 | tf_op jit(solution)/shard_map/reduce_sum | solution.py:62
  31.7 1.3 iota_compare_fusion.4
  33.1 1.3 broadcast_add_fusion
  36.8 0.8 slice_select_fusion
  37.6 3.2 %collective-permute-start.2 = (bf16[896,112]{0,1:T(8,128)(2,1)S(1)}, bf16[896,112]{0,1:T(8,128)(2,1)S(1)}, u32[]{:S(2)}, u32[]{:S(2)}) collective-permute-start(bf16[896,112]{0,1:T(8,128)(2,1)S(1)} %collective-permute-done), channel_id=1, source_target_pairs={{0,1},{1,2},{2,3},{3,4},{4,5},{5,6},{6,7},{7,0},{8,9},{9,10},{10,1... | collective-permute-start | bytes 602120 | tf_op jit(solution)/shard_map/ppermute | solution.py:118
  40.8 4.2 %collective-permute-start.3 = (bf16[896,112]{0,1:T(8,128)(2,1)S(1)}, bf16[896,112]{0,1:T(8,128)(2,1)S(1)}, u32[]{:S(2)}, u32[]{:S(2)}) collective-permute-start(bf16[896,112]{0,1:T(8,128)(2,1)S(1)} %collective-permute-done), channel_id=1, source_target_pairs={{0,2},{1,3},{2,4},{3,5},{4,6},{5,7},{6,0},{7,1},{8,10},{9,11},{10,... | collective-permute-start | bytes 602120 | tf_op jit(solution)/shard_map/ppermute | solution.py:118
  45.1 6.4 %collective-permute-start.4 = (bf16[896,112]{0,1:T(8,128)(2,1)S(1)}, bf16[896,112]{0,1:T(8,128)(2,1)S(1)}, u32[]{:S(2)}, u32[]{:S(2)}) collective-permute-start(bf16[896,112]{0,1:T(8,128)(2,1)S(1)} %collective-permute-done), channel_id=1, source_target_pairs={{0,3},{1,4},{2,5},{3,6},{4,7},{5,0},{6,1},{7,2},{8,11},{9,12},{10,... | collective-permute-start | bytes 602120 | tf_op jit(solution)/shard_map/ppermute | solution.py:118
  51.5 3.7 %collective-permute-start.5 = (bf16[896,112]{0,1:T(8,128)(2,1)S(1)}, bf16[896,112]{0,1:T(8,128)(2,1)S(1)}, u32[]{:S(2)}, u32[]{:S(2)}) collective-permute-start(bf16[896,112]{0,1:T(8,128)(2,1)S(1)} %collective-permute-done), channel_id=1, source_target_pairs={{0,4},{1,5},{2,6},{3,7},{4,0},{5,1},{6,2},{7,3},{8,12},{9,13},{10,... | collective-permute-start | bytes 602120 | tf_op jit(solution)/shard_map/ppermute | solution.py:118
  55.2 6.4 %collective-permute-start.6 = (bf16[896,112]{0,1:T(8,128)(2,1)S(1)}, bf16[896,112]{0,1:T(8,128)(2,1)S(1)}, u32[]{:S(2)}, u32[]{:S(2)}) collective-permute-start(bf16[896,112]{0,1:T(8,128)(2,1)S(1)} %collective-permute-done), channel_id=1, source_target_pairs={{0,5},{1,6},{2,7},{3,0},{4,1},{5,2},{6,3},{7,4},{8,13},{9,14},{10,... | collective-permute-start | bytes 602120 | tf_op jit(solution)/shard_map/ppermute | solution.py:118
  62.5 0.8 copy-done.1
  64.3 0.8 gather_fusion.3
  65.1 0.9 broadcast_select_fusion.1
  66.1 11.7 %all-to-all-start.1 = ((bf16[64,2,4,256]{3,2,1,0:T(4,128)(2,1)}), bf16[64,2,4,256]{3,2,1,0:T(4,128)(2,1)S(1)}, u32[]{:S(2)}, u32[]{:S(2)}) async-start(bf16[64,2,4,256]{3,2,1,0:T(4,128)(2,1)} %broadcast_select_fusion.1), calls=%async_computation.1 | async-start | bytes 524288 | tf_op jit(solution)/shard_map/all_to_all | solution.py:106
  77.8 1.9 %collective-permute-start.7 = (bf16[896,112]{0,1:T(8,128)(2,1)S(1)}, bf16[896,112]{0,1:T(8,128)(2,1)S(1)}, u32[]{:S(2)}, u32[]{:S(2)}) collective-permute-start(bf16[896,112]{0,1:T(8,128)(2,1)S(1)} %collective-permute-done), channel_id=1, source_target_pairs={{0,6},{1,7},{2,0},{3,1},{4,2},{5,3},{6,4},{7,5},{8,14},{9,15},{10,... | collective-permute-start | bytes 602120 | tf_op jit(solution)/shard_map/ppermute | solution.py:118
  79.8 1.9 %collective-permute-start.8 = (bf16[896,112]{0,1:T(8,128)(2,1)S(1)}, bf16[896,112]{0,1:T(8,128)(2,1)S(1)}, u32[]{:S(2)}, u32[]{:S(2)}) collective-permute-start(bf16[896,112]{0,1:T(8,128)(2,1)S(1)} %collective-permute-done), channel_id=1, source_target_pairs={{0,7},{1,0},{2,1},{3,2},{4,3},{5,4},{6,5},{7,6},{8,15},{9,8},{10,9... | collective-permute-start | bytes 602120 | tf_op jit(solution)/shard_map/ppermute | solution.py:118
  81.9 9.5 %collective-permute-done.7 = bf16[896,112]{0,1:T(8,128)(2,1)S(1)} collective-permute-done((bf16[896,112]{0,1:T(8,128)(2,1)S(1)}, bf16[896,112]{0,1:T(8,128)(2,1)S(1)}, u32[]{:S(2)}, u32[]{:S(2)}) %collective-permute-start.7) | collective-permute-done | bytes 200736 | tf_op jit(solution)/shard_map/ppermute | solution.py:118
  91.4 2.2 %collective-permute-done.8 = bf16[896,112]{0,1:T(8,128)(2,1)S(1)} collective-permute-done((bf16[896,112]{0,1:T(8,128)(2,1)S(1)}, bf16[896,112]{0,1:T(8,128)(2,1)S(1)}, u32[]{:S(2)}, u32[]{:S(2)}) %collective-permute-start.8) | collective-permute-done | bytes 200736 | tf_op jit(solution)/shard_map/ppermute | solution.py:118
  93.6 0.9 gather_fusion.4
  94.8 0.7 fusion.17
  97.6 0.7 fusion.13
  102.2 0.7 fusion.10
  102.9 43.7 %all_gather.3 = bf16[512,896]{1,0:T(8,128)(2,1)S(1)} all-gather(bf16[64,896]{1,0:T(8,128)(2,1)S(1)} %collective-permute-done.1), channel_id=1, replica_groups=mesh['x'=4,'z'=8,'c'=2,'mlp'=8] {'x','c'}, dimensions={0}, use_global_device_ids=true | all-gather | bytes 1032192 | tf_op jit(solution)/shard_map/all_gather | solution.py:182
  146.6 2.6 %convolution_convert_fusion = bf16[512,896]{1,0:T(8,128)(2,1)S(1)} fusion(bf16[512,896]{1,0:T(8,128)(2,1)S(1)} %all_gather.3, bf16[896,896]{0,1:T(8,128)(2,1)} %fusion.10), kind=kOutput, calls=%fused_computation.7 | convolution fusion | flops 822542336 | bytes 3440640 | tf_op jit(solution)/shard_map/dot_general | solution.py:183
  149.8 33.0 %all_to_all.15 = bf16[8,512,112]{1,2,0:T(8,128)(2,1)S(1)} all-to-all(bf16[8,512,112]{1,2,0:T(8,128)(2,1)S(1)} %bitcast.121), channel_id=1, replica_groups=mesh['x'=4,'z'=8,'c'=2,'mlp'=8] {'z'}, dimensions={0} | all-to-all | bytes 1835008 | tf_op jit(solution)/shard_map/all_to_all | solution.py:187
  (120 shorter events, 14.6 us)
Async XLA Ops:
  0.6 23.9 %copy-start = (s32[74]{0:T(128)S(1)}, s32[74]{0:T(128)}, u32[]{:S(2)}) copy-start(s32[74]{0:T(128)} %param.25) | copy-start | bytes 892
  0.6 29.1 %copy-start.20 = (s32[74]{0:T(128)S(1)}, s32[74]{0:T(128)}, u32[]{:S(2)}) copy-start(s32[74]{0:T(128)} %param.26) | copy-start | bytes 892
  0.7 32.4 %copy-start.21 = (s32[64]{0:T(128)S(1)}, s32[64]{0:T(128)}, u32[]{:S(2)}) copy-start(s32[64]{0:T(128)} %param.24) | copy-start | bytes 772
  0.7 34.0 %copy-start.23 = (s32[74]{0:T(128)S(1)}, s32[74]{0:T(128)}, u32[]{:S(2)}) copy-start(s32[74]{0:T(128)} %param.27) | copy-start | bytes 892
  0.7 34.1 %copy-start.17 = (bf16[64,128]{1,0:T(8,128)(2,1)S(1)}, bf16[64,128]{1,0:T(8,128)(2,1)}, u32[]{:S(2)}) copy-start(bf16[64,128]{1,0:T(8,128)(2,1)} %param.15) | copy-start | bytes 49156
  0.7 35.9 %copy-start.18 = (bf16[64,128]{1,0:T(8,128)(2,1)S(1)}, bf16[64,128]{1,0:T(8,128)(2,1)}, u32[]{:S(2)}) copy-start(bf16[64,128]{1,0:T(8,128)(2,1)} %param.16) | copy-start | bytes 49156
  0.7 36.0 %copy-start.13 = (bf16[320,128]{1,0:T(8,128)(2,1)S(1)}, bf16[320,128]{1,0:T(8,128)(2,1)}, u32[]{:S(2)}) copy-start(bf16[320,128]{1,0:T(8,128)(2,1)} %param.17) | copy-start | bytes 245764
  0.7 36.0 %copy-start.12 = (bf16[320,128]{1,0:T(8,128)(2,1)S(1)}, bf16[320,128]{1,0:T(8,128)(2,1)}, u32[]{:S(2)}) copy-start(bf16[320,128]{1,0:T(8,128)(2,1)} %param.18) | copy-start | bytes 245764
  0.7 60.9 %copy-start.11 = (bf16[64,896]{1,0:T(8,128)(2,1)S(1)}, bf16[64,896]{1,0:T(8,128)(2,1)}, u32[]{:S(2)}) copy-start(bf16[64,896]{1,0:T(8,128)(2,1)} %param.14) | copy-start | bytes 344068
  0.7 36.9 %collective-permute-start = (bf16[896,112]{0,1:T(8,128)(2,1)}, bf16[896,112]{0,1:T(8,128)(2,1)S(1)}, u32[]{:S(2)}, u32[]{:S(2)}) collective-permute-start(bf16[896,112]{0,1:T(8,128)(2,1)} %param.21), channel_id=1, source_target_pairs={{0,0},{1,16},{2,32},{3,48},{4,64},{5,80},{6,96},{7,112},{16,1},{17... | collective-permute-start | bytes 602120 | tf_op jit(solution)/shard_map/ppermute | solution.py:113
  4.0 59.6 %all-to-all-start = ((bf16[64,4,256]{2,1,0:T(4,128)(2,1)}), bf16[64,4,256]{2,1,0:T(4,128)(2,1)S(1)}, u32[]{:S(2)}, u32[]{:S(2)}) async-start(bf16[64,4,256]{2,1,0:T(4,128)(2,1)} %reshape.367), calls=%async_computation | async-start | bytes 262144 | tf_op jit(solution)/shard_map/all_to_all | solution.py:97
  37.5 24.9 %copy-start.7 = (bf16[320,128]{1,0:T(8,128)(2,1)}, bf16[320,128]{1,0:T(8,128)(2,1)S(1)}, u32[]{:S(2)}) copy-start(bf16[320,128]{1,0:T(8,128)(2,1)S(1)} %get-tuple-element.24) | copy-start | bytes 245764
  37.6 24.9 %copy-start.8 = (pred[64,320]{1,0:T(8,128)(4,1)}, pred[64,320]{1,0:T(8,128)(4,1)S(1)}, u32[]{:S(2)}) copy-start(pred[64,320]{1,0:T(8,128)(4,1)S(1)} %iota_compare_fusion.2) | copy-start | bytes 61444
  37.6 40.2 %collective-permute-start.2 = (bf16[896,112]{0,1:T(8,128)(2,1)S(1)}, bf16[896,112]{0,1:T(8,128)(2,1)S(1)}, u32[]{:S(2)}, u32[]{:S(2)}) collective-permute-start(bf16[896,112]{0,1:T(8,128)(2,1)S(1)} %collective-permute-done), channel_id=1, source_target_pairs={{0,1},{1,2},{2,3},{3,4},{4,5},{5,6},{6,7},{7,0},{8,9},{9,10},{10,1... | collective-permute-start | bytes 602120 | tf_op jit(solution)/shard_map/ppermute | solution.py:118
  40.8 38.9 %collective-permute-start.3 = (bf16[896,112]{0,1:T(8,128)(2,1)S(1)}, bf16[896,112]{0,1:T(8,128)(2,1)S(1)}, u32[]{:S(2)}, u32[]{:S(2)}) collective-permute-start(bf16[896,112]{0,1:T(8,128)(2,1)S(1)} %collective-permute-done), channel_id=1, source_target_pairs={{0,2},{1,3},{2,4},{3,5},{4,6},{5,7},{6,0},{7,1},{8,10},{9,11},{10,... | collective-permute-start | bytes 602120 | tf_op jit(solution)/shard_map/ppermute | solution.py:118
  45.1 36.7 %collective-permute-start.4 = (bf16[896,112]{0,1:T(8,128)(2,1)S(1)}, bf16[896,112]{0,1:T(8,128)(2,1)S(1)}, u32[]{:S(2)}, u32[]{:S(2)}) collective-permute-start(bf16[896,112]{0,1:T(8,128)(2,1)S(1)} %collective-permute-done), channel_id=1, source_target_pairs={{0,3},{1,4},{2,5},{3,6},{4,7},{5,0},{6,1},{7,2},{8,11},{9,12},{10,... | collective-permute-start | bytes 602120 | tf_op jit(solution)/shard_map/ppermute | solution.py:118
  51.5 30.3 %collective-permute-start.5 = (bf16[896,112]{0,1:T(8,128)(2,1)S(1)}, bf16[896,112]{0,1:T(8,128)(2,1)S(1)}, u32[]{:S(2)}, u32[]{:S(2)}) collective-permute-start(bf16[896,112]{0,1:T(8,128)(2,1)S(1)} %collective-permute-done), channel_id=1, source_target_pairs={{0,4},{1,5},{2,6},{3,7},{4,0},{5,1},{6,2},{7,3},{8,12},{9,13},{10,... | collective-permute-start | bytes 602120 | tf_op jit(solution)/shard_map/ppermute | solution.py:118
  55.2 26.6 %collective-permute-start.6 = (bf16[896,112]{0,1:T(8,128)(2,1)S(1)}, bf16[896,112]{0,1:T(8,128)(2,1)S(1)}, u32[]{:S(2)}, u32[]{:S(2)}) collective-permute-start(bf16[896,112]{0,1:T(8,128)(2,1)S(1)} %collective-permute-done), channel_id=1, source_target_pairs={{0,5},{1,6},{2,7},{3,0},{4,1},{5,2},{6,3},{7,4},{8,13},{9,14},{10,... | collective-permute-start | bytes 602120 | tf_op jit(solution)/shard_map/ppermute | solution.py:118
  62.0 1.6 copy-start.3
  62.0 1.6 copy-start.5
  62.4 3.6 %copy-start.15 = (f32[64,7]{0,1:T(8,128)}, f32[64,7]{0,1:T(8,128)S(1)}, u32[]{:S(2)}) copy-start(f32[64,7]{0,1:T(8,128)S(1)} %get-tuple-element.34) | copy-start | bytes 5380
  66.1 33.6 %all-to-all-start.1 = ((bf16[64,2,4,256]{3,2,1,0:T(4,128)(2,1)}), bf16[64,2,4,256]{3,2,1,0:T(4,128)(2,1)S(1)}, u32[]{:S(2)}, u32[]{:S(2)}) async-start(bf16[64,2,4,256]{3,2,1,0:T(4,128)(2,1)} %broadcast_select_fusion.1), calls=%async_computation.1 | async-start | bytes 524288 | tf_op jit(solution)/shard_map/all_to_all | solution.py:106
  77.8 13.5 %collective-permute-start.7 = (bf16[896,112]{0,1:T(8,128)(2,1)S(1)}, bf16[896,112]{0,1:T(8,128)(2,1)S(1)}, u32[]{:S(2)}, u32[]{:S(2)}) collective-permute-start(bf16[896,112]{0,1:T(8,128)(2,1)S(1)} %collective-permute-done), channel_id=1, source_target_pairs={{0,6},{1,7},{2,0},{3,1},{4,2},{5,3},{6,4},{7,5},{8,14},{9,15},{10,... | collective-permute-start | bytes 602120 | tf_op jit(solution)/shard_map/ppermute | solution.py:118
  79.8 13.8 %collective-permute-start.8 = (bf16[896,112]{0,1:T(8,128)(2,1)S(1)}, bf16[896,112]{0,1:T(8,128)(2,1)S(1)}, u32[]{:S(2)}, u32[]{:S(2)}) collective-permute-start(bf16[896,112]{0,1:T(8,128)(2,1)S(1)} %collective-permute-done), channel_id=1, source_target_pairs={{0,7},{1,0},{2,1},{3,2},{4,3},{5,4},{6,5},{7,6},{8,15},{9,8},{10,9... | collective-permute-start | bytes 602120 | tf_op jit(solution)/shard_map/ppermute | solution.py:118
  96.9 3.0 %copy-start.4 = (bf16[64,7,64]{2,0,1:T(8,128)(2,1)S(1)}, bf16[64,7,64]{2,0,1:T(8,128)(2,1)}, u32[]{:S(2)}) copy-start(bf16[64,7,64]{2,0,1:T(8,128)(2,1)} %copy-done.3) | copy-start | bytes 172036
  96.9 3.0 %copy-start.6 = (bf16[64,7,64]{2,0,1:T(8,128)(2,1)S(1)}, bf16[64,7,64]{2,0,1:T(8,128)(2,1)}, u32[]{:S(2)}) copy-start(bf16[64,7,64]{2,0,1:T(8,128)(2,1)} %copy-done.5) | copy-start | bytes 172036
  96.9 3.0 %copy-start.19 = (pred[512]{0:T(512)(128)(4,1)S(1)}, pred[512]{0:T(512)(128)(4,1)}, u32[]{:S(2)}) copy-start(pred[512]{0:T(512)(128)(4,1)} %pad_add_fusion) | copy-start | bytes 1540
  99.9 1.1 copy-start.2
  99.9 1.1 copy-start.9
  100.0 1.1 copy-start.14
  101.5 1.4 collective-permute-start.1
  149.8 33.2 %copy-start.10 = (bf16[512,112]{0,1:T(8,128)(2,1)S(1)}, bf16[512,112]{0,1:T(8,128)(2,1)}, u32[]{:S(2)}) copy-start(bf16[512,112]{0,1:T(8,128)(2,1)} %param.22) | copy-start | bytes 344068
  (3 other events, 2.7 us)

commit v15 on v12

--- a/solution.py
+++ b/solution.py
@@ -89,21 +89,6 @@
     group = q_heads // kv_heads
     kv_width = kv_heads * width
     shared_count = ROOTS + MIDS
-
-    my_pair = jnp.concatenate([shared_key_block, shared_value_block], axis=1)
-    node_rows = my_pair.shape[0]
-    piece_rows = node_rows // tok_count
-    pieces = my_pair.reshape(tok_count, piece_rows, my_pair.shape[1])
-    spread = lax.all_to_all(pieces, TOK, 0, 0, tiled=True)
-    held = jnp.take(spread, node_owner[:shared_count], axis=0)
-    requests = token_request.reshape(-1, tok_rows)[:, 0]
-    middles = parents[shared_count + requests]
-    roots = parents[middles]
-    wanted = jnp.stack([roots, middles], axis=1)
-    outgoing = jnp.take(held, wanted.reshape(-1), axis=0).reshape(
-        (tok_count, 2, piece_rows, my_pair.shape[1])
-    )
-    incoming = lax.all_to_all(outgoing, TOK, 0, 0, tiled=True)
 
     swap = [
         (h * mlp_count + m, m * mlp_count + h)
@@ -139,6 +124,22 @@
         leaf_value_output.reshape(leaf_rows, kv_heads, width),
         leaf_row_mask,
     )
+    my_pair = jnp.concatenate([shared_key_block, shared_value_block], axis=1)
+    my_pair, leaf_state = lax.optimization_barrier((my_pair, leaf_state))
+    node_rows = my_pair.shape[0]
+    piece_rows = node_rows // tok_count
+    pieces = my_pair.reshape(tok_count, piece_rows, my_pair.shape[1])
+    spread = lax.all_to_all(pieces, TOK, 0, 0, tiled=True)
+    held = jnp.take(spread, node_owner[:shared_count], axis=0)
+    requests = token_request.reshape(-1, tok_rows)[:, 0]
+    middles = parents[shared_count + requests]
+    roots = parents[middles]
+    wanted = jnp.stack([roots, middles], axis=1)
+    outgoing = jnp.take(held, wanted.reshape(-1), axis=0).reshape(
+        (tok_count, 2, piece_rows, my_pair.shape[1])
+    )
+    incoming = lax.all_to_all(outgoing, TOK, 0, 0, tiled=True)
+
     root_pair = incoming[:, 0].reshape(my_pair.shape)
     middle_pair = incoming[:, 1].reshape(my_pair.shape)
     root_keys = root_pair[:, :kv_width]

time: 159 us -> 168 us (1.057)
  waiting for transfers between devices: 11.2 us -> 21 us
    all_to_all x1, waiting for transfers between devices: 0.01 us -> 9.61 us  [body(): spread = lax.all_to_all(pieces, TOK, 0, 0, tiled=True)]
    all_to_all x1, starting transfers between devices: 10.3 us -> 4.88 us  [body(): incoming = lax.all_to_all(outgoing, TOK, 0, 0, tiled=True)]
    all_to_all x1, starting transfers between devices: 17.3 us -> 21.2 us  [body(): spread = lax.all_to_all(pieces, TOK, 0, 0, tiled=True)]
  transfers between devices with their start and end apart: 5 -> 5, of which waited for: 1 -> 2; matrix products, arithmetic and copies ran while one was open for 14% -> 13% of each run, Pallas kernels for 0% -> 0%
where the time goes in v15:
time: 168 us; the launch traced here: 167 us
  blocking collectives  74.9 us (45%)
  starting transfers between devices  28.5 us (17%)
  waiting for transfers between devices  21 us (12%)
  between operations  15.1 us (9%)
  other arithmetic  14.6 us (9%)
  local copies, waits for them, and re-layouts  8.65 us (5%)
  matrix products  4.27 us (3%)
    all_gather x1, blocking collectives, body(): token_block = lax.all_gather(token_here, ('x', 'c'), axis=0, tiled=True)  42.4 us
    all_to_all x1, blocking collectives, body(): arrived = lax.all_to_all(parts, GROUP, 0, 0, tiled=True)  32.5 us
    all_to_all x1, starting transfers between devices, body(): spread = lax.all_to_all(pieces, TOK, 0, 0, tiled=True)  21.2 us
    all_to_all x1, waiting for transfers between devices, body(): incoming = lax.all_to_all(outgoing, TOK, 0, 0, tiled=True)  10.8 us
    all_to_all x1, waiting for transfers between devices, body(): spread = lax.all_to_all(pieces, TOK, 0, 0, tiled=True)  9.61 us
    reduce_sum x3, other arithmetic, lookup(): return jnp.sum(jnp.where(jnp.arange(table.shape[0]) == index, table, 0))  5.9 us
    all_to_all x1, starting transfers between devices, body(): incoming = lax.all_to_all(outgoing, TOK, 0, 0, tiled=True)  4.88 us
  transfers between devices with their start and end apart: 5, of which 2 were waited for; matrix products, arithmetic and copies ran while one was open for 13% of the time, Pallas kernels for 0%

profile of v15, /device:TPU:1, one launch (start us, length us, event | category | flops | bytes accessed | tf_op | source)
XLA Modules:
  0.0 166.9 jit_solution(6926777526180771928)
XLA Ops:
  7.2 1.7 %collective-permute-start = (bf16[896,112]{0,1:T(8,128)(2,1)}, bf16[896,112]{0,1:T(8,128)(2,1)S(1)}, u32[]{:S(2)}, u32[]{:S(2)}) collective-permute-start(bf16[896,112]{0,1:T(8,128)(2,1)} %param.21), channel_id=1, source_target_pairs={{0,0},{1,16},{2,32},{3,48},{4,64},{5,80},{6,96},{7,112},{16,1},{17... | collective-permute-start | bytes 602120 | tf_op jit(solution)/shard_map/ppermute | solution.py:98
  9.0 0.8 reshape.269
  9.7 1.3 dynamic_slice.3
  11.7 1.3 fusion.35
  13.0 1.9 %fusion.37 = s32[]{:T(128)} fusion(s32[74]{0:T(128)} %param.25, s32[]{:T(128)} %fusion.35), kind=kLoop, calls=%fused_computation.98 | loop fusion | flops 221 | bytes 304 | tf_op jit(solution)/shard_map/reduce_sum | solution.py:62
  14.9 2.7 %fusion.36 = (s32[]{:T(128)}, s32[]{:T(128)}, s32[]{:T(128)}) fusion(s32[74]{0:T(128)} %param.26, s32[]{:T(128)} %bitcast, s32[]{:T(128)} %fusion.37, s32[]{:T(128)} %fusion.35), kind=kLoop, calls=%fused_computation.97 | loop fusion | flops 663 | bytes 320 | tf_op jit(solution)/shard_map/reduce_sum | solution.py:62
  17.6 0.7 iota_compare_fusion.3
  18.3 0.7 compare_and_fusion
  18.9 1.9 %broadcast_add_fusion = (s32[64]{0:T(128)S(1)}, s32[64]{0:T(128)S(1)}, f32[64]{0:T(128)S(1)}) fusion(s32[]{:T(128)} %get-tuple-element.17, s32[64]{0:T(128)} %param.24, s32[]{:T(128)} %get-tuple-element.16), kind=kLoop, calls=%fused_computation.104 | loop fusion | flops 256 | bytes 1032 | tf_op jit(solution)/shard_map/add | solution.py:120
  20.9 0.7 bitcast_convert_fusion
  22.2 1.4 gather_fusion
  23.8 1.4 gather_fusion.1
  26.4 0.4 select_reduce_fusion.1
  27.5 0.7 reshape.275
  28.2 21.2 %all-to-all-start = ((bf16[64,4,256]{2,1,0:T(4,128)(2,1)}), bf16[64,4,256]{2,1,0:T(4,128)(2,1)S(1)}, u32[]{:S(2)}, u32[]{:S(2)}) async-start(bf16[64,4,256]{2,1,0:T(4,128)(2,1)} %reshape.275), calls=%async_computation | async-start | bytes 262144 | tf_op jit(solution)/shard_map/all_to_all | solution.py:132
  49.6 0.5 all-gather.2.cloned.1.call-update
  50.1 9.6 %all-to-all-done = bf16[64,4,256]{2,1,0:T(4,128)(2,1)S(1)} async-done(((bf16[64,4,256]{2,1,0:T(4,128)(2,1)}), bf16[64,4,256]{2,1,0:T(4,128)(2,1)S(1)}, u32[]{:S(2)}, u32[]{:S(2)}) %all-to-all-start) | async-done | bytes 131104 | tf_op jit(solution)/shard_map/all_to_all | solution.py:132
  59.7 0.6 gather_fusion.2
  60.4 0.8 gather_fusion.3
  61.2 0.9 broadcast_select_fusion
  62.2 4.9 %all-to-all-start.1 = ((bf16[64,2,4,256]{3,2,1,0:T(4,128)(2,1)}), bf16[64,2,4,256]{3,2,1,0:T(4,128)(2,1)S(1)}, u32[]{:S(2)}, u32[]{:S(2)}) async-start(bf16[64,2,4,256]{3,2,1,0:T(4,128)(2,1)} %broadcast_select_fusion), calls=%async_computation.1 | async-start | bytes 524288 | tf_op jit(solution)/shard_map/all_to_all | solution.py:141
  67.1 1.2 iota_compare_fusion.4
  68.3 10.8 %all-to-all-done.1 = bf16[64,2,4,256]{3,2,1,0:T(4,128)(2,1)S(1)} async-done(((bf16[64,2,4,256]{3,2,1,0:T(4,128)(2,1)}), bf16[64,2,4,256]{3,2,1,0:T(4,128)(2,1)S(1)}, u32[]{:S(2)}, u32[]{:S(2)}) %all-to-all-start.1) | async-done | bytes 262176 | tf_op jit(solution)/shard_map/all_to_all | solution.py:141
  79.3 0.4 select_reduce_fusion
  79.7 0.3 convert_reduce_fusion.1
  80.1 0.3 fusion.6
  80.5 0.7 collective-permute-start.1
  81.2 42.4 %all_gather.6 = bf16[512,896]{1,0:T(8,128)(2,1)S(1)} all-gather(bf16[64,896]{1,0:T(8,128)(2,1)S(1)} %collective-permute-done.1), channel_id=1, replica_groups=mesh['x'=4,'z'=8,'c'=2,'mlp'=8] {'x','c'}, dimensions={0}, use_global_device_ids=true | all-gather | bytes 1032192 | tf_op jit(solution)/shard_map/all_gather | solution.py:176
  123.6 2.6 %convolution_convert_fusion = bf16[512,896]{1,0:T(8,128)(2,1)S(1)} fusion(bf16[512,896]{1,0:T(8,128)(2,1)S(1)} %all_gather.6, bf16[896,896]{0,1:T(8,128)(2,1)} %all-gather.2.cloned.1.call-done), kind=kOutput, calls=%fused_computation.5 | convolution fusion | flops 822542336 | bytes 3440640 | tf_op jit(solution)/shard_map/dot_general | solution.py:177
  126.2 0.5 copy.35
  126.8 32.5 %all_to_all.15 = bf16[8,512,112]{1,2,0:T(8,128)(2,1)S(1)} all-to-all(bf16[8,512,112]{1,2,0:T(8,128)(2,1)S(1)} %bitcast.102), channel_id=1, replica_groups=mesh['x'=4,'z'=8,'c'=2,'mlp'=8] {'z'}, dimensions={0} | all-to-all | bytes 1835008 | tf_op jit(solution)/shard_map/all_to_all | solution.py:181
  159.4 0.7 add_convert_fusion
  (60 shorter events, 3.2 us)
Async XLA Ops:
  7.2 18.4 %copy-start.7 = (bf16[256,128]{1,0:T(8,128)(2,1)S(1)}, bf16[256,128]{1,0:T(8,128)(2,1)}, u32[]{:S(2)}) copy-start(bf16[256,128]{1,0:T(8,128)(2,1)} %param.20) | copy-start | bytes 196612
  7.2 18.4 %copy-start.8 = (bf16[256,128]{1,0:T(8,128)(2,1)S(1)}, bf16[256,128]{1,0:T(8,128)(2,1)}, u32[]{:S(2)}) copy-start(bf16[256,128]{1,0:T(8,128)(2,1)} %param.19) | copy-start | bytes 196612
  7.2 18.5 %copy-start.9 = (bf16[64,128]{1,0:T(8,128)(2,1)S(1)}, bf16[64,128]{1,0:T(8,128)(2,1)}, u32[]{:S(2)}) copy-start(bf16[64,128]{1,0:T(8,128)(2,1)} %param.16) | copy-start | bytes 49156
  7.2 18.6 %copy-start.5 = (bf16[320,128]{1,0:T(8,128)(2,1)S(1)}, bf16[320,128]{1,0:T(8,128)(2,1)}, u32[]{:S(2)}) copy-start(bf16[320,128]{1,0:T(8,128)(2,1)} %param.18) | copy-start | bytes 245764
  7.2 18.6 %copy-start.6 = (bf16[320,128]{1,0:T(8,128)(2,1)S(1)}, bf16[320,128]{1,0:T(8,128)(2,1)}, u32[]{:S(2)}) copy-start(bf16[320,128]{1,0:T(8,128)(2,1)} %param.17) | copy-start | bytes 245764
  7.2 18.8 %copy-start.4 = (bf16[64,896]{1,0:T(8,128)(2,1)S(1)}, bf16[64,896]{1,0:T(8,128)(2,1)}, u32[]{:S(2)}) copy-start(bf16[64,896]{1,0:T(8,128)(2,1)} %param.14) | copy-start | bytes 344068
  7.2 18.8 %collective-permute-start = (bf16[896,112]{0,1:T(8,128)(2,1)}, bf16[896,112]{0,1:T(8,128)(2,1)S(1)}, u32[]{:S(2)}, u32[]{:S(2)}) collective-permute-start(bf16[896,112]{0,1:T(8,128)(2,1)} %param.21), channel_id=1, source_target_pairs={{0,0},{1,16},{2,32},{3,48},{4,64},{5,80},{6,96},{7,112},{16,1},{17... | collective-permute-start | bytes 602120 | tf_op jit(solution)/shard_map/ppermute | solution.py:98
  26.0 0.9 copy-start.1
  26.0 1.2 copy-start
  26.0 0.8 copy-start.2
  28.2 31.6 %all-to-all-start = ((bf16[64,4,256]{2,1,0:T(4,128)(2,1)}), bf16[64,4,256]{2,1,0:T(4,128)(2,1)S(1)}, u32[]{:S(2)}, u32[]{:S(2)}) async-start(bf16[64,4,256]{2,1,0:T(4,128)(2,1)} %reshape.275), calls=%async_computation | async-start | bytes 262144 | tf_op jit(solution)/shard_map/all_to_all | solution.py:132
  49.4 74.2 %all-gather.2.cloned.1.call-start = ((), (), s32[]{:S(2)}) async-start(), calls=%async_computation.3 | async-start | bytes 1806336 | tf_op jit(solution)/shard_map/all_gather | solution.py:100
  62.2 16.9 %all-to-all-start.1 = ((bf16[64,2,4,256]{3,2,1,0:T(4,128)(2,1)}), bf16[64,2,4,256]{3,2,1,0:T(4,128)(2,1)S(1)}, u32[]{:S(2)}, u32[]{:S(2)}) async-start(bf16[64,2,4,256]{3,2,1,0:T(4,128)(2,1)} %broadcast_select_fusion), calls=%async_computation.1 | async-start | bytes 524288 | tf_op jit(solution)/shard_map/all_to_all | solution.py:141
  80.5 0.7 collective-permute-start.1
  126.8 32.7 %copy-start.3 = (bf16[512,112]{0,1:T(8,128)(2,1)S(1)}, bf16[512,112]{0,1:T(8,128)(2,1)}, u32[]{:S(2)}) copy-start(bf16[512,112]{0,1:T(8,128)(2,1)} %param.22) | copy-start | bytes 344068
Sparse Core Ops, SparseCore 0:
  52.3 57.8 all-gather.1

commit v16 on v12

--- a/solution.py
+++ b/solution.py
@@ -172,7 +172,10 @@
                 )
             )
     token_here = lax.ppermute(attended_local, TOK + ("mlp",), spread_route)
-    token_block = lax.all_gather(token_here, ("x", "c"), axis=0, tiled=True)
+    copies = jnp.broadcast_to(token_here[None], (lax.axis_size(("x", "c")),) + token_here.shape)
+    token_block = lax.all_to_all(copies, ("x", "c"), 0, 0, tiled=True).reshape(
+        -1, token_here.shape[1]
+    )
     projected = jnp.dot(token_block, weight_cols, preferred_element_type=jnp.float32).astype(
         jnp.bfloat16
     )

time: 159 us -> 163 us (1.025)
  blocking collectives: 75.3 us -> 77.7 us
    all_to_all x0 -> x1, blocking collectives: none -> 47.3 us  [body(): lax.all_to_all(copies, ('x', 'c'), 0, 0, tiled=True)]
    all_gather x1 -> x0, blocking collectives: 43.1 us -> none  [body(): token_block = lax.all_gather(token_here, ('x', 'c'), axis=0, tiled=True)]
    all_to_all x1, blocking collectives: 32.1 us -> 30.4 us  [body(): arrived = lax.all_to_all(parts, GROUP, 0, 0, tiled=True)]
where the time goes in v16:
time: 163 us; the launch traced here: 161 us
  blocking collectives  77.7 us (48%)
  starting transfers between devices  30.1 us (18%)
  between operations  15.2 us (9%)
  other arithmetic  14.1 us (9%)
  waiting for transfers between devices  11.2 us (7%)
  local copies, waits for them, and re-layouts  8.62 us (5%)
  matrix products  4.27 us (3%)
    all_to_all x1, blocking collectives, body(): lax.all_to_all(copies, ('x', 'c'), 0, 0, tiled=True)  47.3 us
    all_to_all x1, blocking collectives, body(): arrived = lax.all_to_all(parts, GROUP, 0, 0, tiled=True)  30.4 us
    all_to_all x1, starting transfers between devices, body(): spread = lax.all_to_all(pieces, TOK, 0, 0, tiled=True)  17.3 us
    all_to_all x1, waiting for transfers between devices, body(): incoming = lax.all_to_all(outgoing, TOK, 0, 0, tiled=True)  11.2 us
    all_to_all x1, starting transfers between devices, body(): incoming = lax.all_to_all(outgoing, TOK, 0, 0, tiled=True)  10.3 us
    reduce_sum x3, other arithmetic, lookup(): return jnp.sum(jnp.where(jnp.arange(table.shape[0]) == index, table, 0))  5.9 us
  transfers between devices with their start and end apart: 5, of which 1 were waited for; matrix products, arithmetic and copies ran while one was open for 14% of the time, Pallas kernels for 0%

profile of v16, /device:TPU:1, one launch (start us, length us, event | category | flops | bytes accessed | tf_op | source)
XLA Modules:
  0.0 161.1 jit_solution(5445127226006117650)
XLA Ops:
  7.2 1.7 %collective-permute-start = (bf16[896,112]{0,1:T(8,128)(2,1)}, bf16[896,112]{0,1:T(8,128)(2,1)S(1)}, u32[]{:S(2)}, u32[]{:S(2)}) collective-permute-start(bf16[896,112]{0,1:T(8,128)(2,1)} %param.21), channel_id=1, source_target_pairs={{0,0},{1,16},{2,32},{3,48},{4,64},{5,80},{6,96},{7,112},{16,1},{17... | collective-permute-start | bytes 602120 | tf_op jit(solution)/shard_map/ppermute | solution.py:113
  9.0 0.9 pad_maximum_fusion
  9.8 0.7 reshape.317
  10.5 17.3 %all-to-all-start = ((bf16[64,4,256]{2,1,0:T(4,128)(2,1)}), bf16[64,4,256]{2,1,0:T(4,128)(2,1)S(1)}, u32[]{:S(2)}, u32[]{:S(2)}) async-start(bf16[64,4,256]{2,1,0:T(4,128)(2,1)} %reshape.317), calls=%async_computation | async-start | bytes 262144 | tf_op jit(solution)/shard_map/all_to_all | solution.py:97
  27.9 0.8 reshape.316
  28.7 1.3 dynamic_slice.3
  30.6 1.3 fusion.32
  31.9 1.9 %fusion.34 = s32[]{:T(128)} fusion(s32[74]{0:T(128)} %param.25, s32[]{:T(128)} %fusion.32), kind=kLoop, calls=%fused_computation.95 | loop fusion | flops 221 | bytes 304 | tf_op jit(solution)/shard_map/reduce_sum | solution.py:62
  33.9 2.7 %fusion.33 = (s32[]{:T(128)}, s32[]{:T(128)}, s32[]{:T(128)}) fusion(s32[74]{0:T(128)} %param.26, s32[]{:T(128)} %bitcast, s32[]{:T(128)} %fusion.34, s32[]{:T(128)} %fusion.32), kind=kLoop, calls=%fused_computation.94 | loop fusion | flops 663 | bytes 320 | tf_op jit(solution)/shard_map/reduce_sum | solution.py:62
  36.5 1.2 iota_compare_fusion.4
  37.7 1.9 %broadcast_add_fusion = (s32[64]{0:T(128)S(1)}, s32[64]{0:T(128)S(1)}, f32[64]{0:T(128)S(1)}) fusion(s32[]{:T(128)} %get-tuple-element.9, s32[64]{0:T(128)} %param.24, s32[]{:T(128)} %get-tuple-element.8), kind=kLoop, calls=%fused_computation.101 | loop fusion | flops 256 | bytes 1032 | tf_op jit(solution)/shard_map/add | solution.py:135
  39.8 1.4 gather_fusion
  41.5 0.8 gather_fusion.1
  43.0 0.7 iota_compare_fusion.3
  44.5 0.5 copy-done.2
  45.2 0.6 gather_fusion.2
  45.9 0.8 gather_fusion.3
  46.7 0.9 broadcast_select_fusion
  47.7 10.3 %all-to-all-start.1 = ((bf16[64,2,4,256]{3,2,1,0:T(4,128)(2,1)}), bf16[64,2,4,256]{3,2,1,0:T(4,128)(2,1)S(1)}, u32[]{:S(2)}, u32[]{:S(2)}) async-start(bf16[64,2,4,256]{3,2,1,0:T(4,128)(2,1)} %broadcast_select_fusion), calls=%async_computation.1 | async-start | bytes 524288 | tf_op jit(solution)/shard_map/all_to_all | solution.py:106
  58.1 0.4 select_reduce_fusion.1
  58.5 0.3 convert_reduce_fusion.2
  58.8 11.2 %all-to-all-done.1 = bf16[64,2,4,256]{3,2,1,0:T(4,128)(2,1)S(1)} async-done(((bf16[64,2,4,256]{3,2,1,0:T(4,128)(2,1)}), bf16[64,2,4,256]{3,2,1,0:T(4,128)(2,1)S(1)}, u32[]{:S(2)}, u32[]{:S(2)}) %all-to-all-start.1) | async-done | bytes 262176 | tf_op jit(solution)/shard_map/all_to_all | solution.py:106
  70.2 0.4 select_reduce_fusion
  70.6 0.3 convert_reduce_fusion.1
  71.0 0.3 fusion.5
  71.3 0.3 fusion.7
  71.8 0.7 collective-permute-start.1
  72.6 47.3 %all_to_all.20 = bf16[8,64,896]{2,1,0:T(8,128)(2,1)S(1)} all-to-all(bf16[8,64,896]{2,1,0:T(8,128)(2,1)S(1)} %broadcast_in_dim.117), channel_id=1, replica_groups=mesh['x'=4,'z'=8,'c'=2,'mlp'=8] {'x','c'}, dimensions={0} | all-to-all | bytes 1835008 | tf_op jit(solution)/shard_map/all_to_all | solution.py:176
  119.8 2.6 %convolution_convert_fusion = bf16[512,896]{1,0:T(8,128)(2,1)S(1)} fusion(bf16[512,896]{1,0:T(8,128)(2,1)S(1)} %bitcast.74, bf16[896,896]{0,1:T(8,128)(2,1)} %all-gather.2.cloned.1.call-done), kind=kOutput, calls=%fused_computation.5 | convolution fusion | flops 822542336 | bytes 3440640 | tf_op jit(solution)/shard_map/dot_general | solution.py:179
  122.5 0.5 copy.35
  123.0 30.4 %all_to_all.21 = bf16[8,512,112]{1,2,0:T(8,128)(2,1)S(1)} all-to-all(bf16[8,512,112]{1,2,0:T(8,128)(2,1)S(1)} %bitcast.72), channel_id=1, replica_groups=mesh['x'=4,'z'=8,'c'=2,'mlp'=8] {'z'}, dimensions={0} | all-to-all | bytes 1835008 | tf_op jit(solution)/shard_map/all_to_all | solution.py:183
  153.6 0.7 add_convert_fusion
  (63 shorter events, 2.7 us)
Async XLA Ops:
  7.2 34.3 %copy-start = (s32[74]{0:T(128)S(1)}, s32[74]{0:T(128)}, u32[]{:S(2)}) copy-start(s32[74]{0:T(128)} %param.25) | copy-start | bytes 892
  7.2 35.3 %copy-start.10 = (s32[74]{0:T(128)S(1)}, s32[74]{0:T(128)}, u32[]{:S(2)}) copy-start(s32[74]{0:T(128)} %param.27) | copy-start | bytes 892
  7.2 35.4 %copy-start.8 = (bf16[64,128]{1,0:T(8,128)(2,1)S(1)}, bf16[64,128]{1,0:T(8,128)(2,1)}, u32[]{:S(2)}) copy-start(bf16[64,128]{1,0:T(8,128)(2,1)} %param.15) | copy-start | bytes 49156
  7.2 36.7 %copy-start.9 = (bf16[64,128]{1,0:T(8,128)(2,1)S(1)}, bf16[64,128]{1,0:T(8,128)(2,1)}, u32[]{:S(2)}) copy-start(bf16[64,128]{1,0:T(8,128)(2,1)} %param.16) | copy-start | bytes 49156
  7.2 36.8 %copy-start.6 = (bf16[320,128]{1,0:T(8,128)(2,1)S(1)}, bf16[320,128]{1,0:T(8,128)(2,1)}, u32[]{:S(2)}) copy-start(bf16[320,128]{1,0:T(8,128)(2,1)} %param.17) | copy-start | bytes 245764
  7.2 36.8 %copy-start.5 = (bf16[320,128]{1,0:T(8,128)(2,1)S(1)}, bf16[320,128]{1,0:T(8,128)(2,1)}, u32[]{:S(2)}) copy-start(bf16[320,128]{1,0:T(8,128)(2,1)} %param.18) | copy-start | bytes 245764
  7.2 37.1 %copy-start.4 = (bf16[64,896]{1,0:T(8,128)(2,1)S(1)}, bf16[64,896]{1,0:T(8,128)(2,1)}, u32[]{:S(2)}) copy-start(bf16[64,896]{1,0:T(8,128)(2,1)} %param.14) | copy-start | bytes 344068
  7.2 37.1 %collective-permute-start = (bf16[896,112]{0,1:T(8,128)(2,1)}, bf16[896,112]{0,1:T(8,128)(2,1)S(1)}, u32[]{:S(2)}, u32[]{:S(2)}) collective-permute-start(bf16[896,112]{0,1:T(8,128)(2,1)} %param.21), channel_id=1, source_target_pairs={{0,0},{1,16},{2,32},{3,48},{4,64},{5,80},{6,96},{7,112},{16,1},{17... | collective-permute-start | bytes 602120 | tf_op jit(solution)/shard_map/ppermute | solution.py:113
  10.5 34.7 %all-to-all-start = ((bf16[64,4,256]{2,1,0:T(4,128)(2,1)}), bf16[64,4,256]{2,1,0:T(4,128)(2,1)S(1)}, u32[]{:S(2)}, u32[]{:S(2)}) async-start(bf16[64,4,256]{2,1,0:T(4,128)(2,1)} %reshape.317), calls=%async_computation | async-start | bytes 262144 | tf_op jit(solution)/shard_map/all_to_all | solution.py:97
  27.9 92.0 %all-gather.2.cloned.1.call-start = ((), (), s32[]{:S(2)}) async-start(), calls=%async_computation.4 | async-start | bytes 1806336 | tf_op jit(solution)/shard_map/all_gather | solution.py:115
  44.2 13.9 %copy-start.1 = (bf16[320,128]{1,0:T(8,128)(2,1)}, bf16[320,128]{1,0:T(8,128)(2,1)S(1)}, u32[]{:S(2)}) copy-start(bf16[320,128]{1,0:T(8,128)(2,1)S(1)} %get-tuple-element.24) | copy-start | bytes 245764
  44.2 27.1 %copy-start.7 = (bf16[320,128]{1,0:T(8,128)(2,1)}, bf16[320,128]{1,0:T(8,128)(2,1)S(1)}, u32[]{:S(2)}) copy-start(bf16[320,128]{1,0:T(8,128)(2,1)S(1)} %get-tuple-element.23) | copy-start | bytes 245764
  44.4 0.7 copy-start.2
  47.7 22.3 %all-to-all-start.1 = ((bf16[64,2,4,256]{3,2,1,0:T(4,128)(2,1)}), bf16[64,2,4,256]{3,2,1,0:T(4,128)(2,1)S(1)}, u32[]{:S(2)}, u32[]{:S(2)}) async-start(bf16[64,2,4,256]{3,2,1,0:T(4,128)(2,1)} %broadcast_select_fusion), calls=%async_computation.1 | async-start | bytes 524288 | tf_op jit(solution)/shard_map/all_to_all | solution.py:106
  71.8 0.7 collective-permute-start.1
  123.0 30.6 %copy-start.3 = (bf16[512,112]{0,1:T(8,128)(2,1)S(1)}, bf16[512,112]{0,1:T(8,128)(2,1)}, u32[]{:S(2)}) copy-start(bf16[512,112]{0,1:T(8,128)(2,1)} %param.22) | copy-start | bytes 344068
Sparse Core Ops, SparseCore 0:
  45.2 60.7 all-gather.1

commit v17 on v12

--- a/solution.py
+++ b/solution.py
@@ -60,6 +60,19 @@
 
 def lookup(table, index):
     return jnp.sum(jnp.where(jnp.arange(table.shape[0]) == index, table, 0))
+
+
+def exchange(outgoing):
+    x_count = lax.axis_size("x")
+    z_count = lax.axis_size("z")
+    c_count = lax.axis_size("c")
+    rest = outgoing.shape[1:]
+    split = outgoing.reshape((x_count, z_count, c_count) + rest)
+    split = jnp.moveaxis(split, 1, 2).reshape((x_count * c_count, z_count) + rest)
+    first = lax.all_to_all(split, ("x", "c"), 0, 0, tiled=True)
+    second = lax.all_to_all(jnp.swapaxes(first, 0, 1), "z", 0, 0, tiled=True)
+    back = second.reshape((z_count, x_count, c_count) + rest)
+    return jnp.swapaxes(back, 0, 1).reshape(outgoing.shape)
 
 
 def body(
@@ -94,7 +107,7 @@
     node_rows = my_pair.shape[0]
     piece_rows = node_rows // tok_count
     pieces = my_pair.reshape(tok_count, piece_rows, my_pair.shape[1])
-    spread = lax.all_to_all(pieces, TOK, 0, 0, tiled=True)
+    spread = exchange(pieces)
     held = jnp.take(spread, node_owner[:shared_count], axis=0)
     requests = token_request.reshape(-1, tok_rows)[:, 0]
     middles = parents[shared_count + requests]
@@ -103,7 +116,7 @@
     outgoing = jnp.take(held, wanted.reshape(-1), axis=0).reshape(
         (tok_count, 2, piece_rows, my_pair.shape[1])
     )
-    incoming = lax.all_to_all(outgoing, TOK, 0, 0, tiled=True)
+    incoming = exchange(outgoing)
 
     swap = [
         (h * mlp_count + m, m * mlp_count + h)

time: 159 us -> 170 us (1.069)
  waiting for transfers between devices: 11.2 us -> 23.3 us
  blocking collectives: 75.3 us -> 72.7 us
  local copies, waits for them, and re-layouts: 8.5 us -> 10.6 us
    all_to_all x2 -> x4, waiting for transfers between devices: 11.2 us -> 23.3 us  [the longest x2 16.9 us: exchange(): second = lax.all_to_all(jnp.swapaxes(first, 0, 1), 'z', 0, 0, tiled=True)]
    all_to_all x1, blocking collectives: 32.1 us -> 29.8 us  [body(): arrived = lax.all_to_all(parts, GROUP, 0, 0, tiled=True)]
    transpose x0 -> x4, local copies, waits for them, and re-layouts: none -> 2.28 us  [the longest x2 1.5 us: exchange(): second = lax.all_to_all(jnp.swapaxes(first, 0, 1), 'z', 0, 0, tiled=True)]
    all_to_all x2 -> x4, starting transfers between devices: 27.6 us -> 27.8 us  [the longest x2 16.2 us: exchange(): first = lax.all_to_all(split, ('x', 'c'), 0, 0, tiled=True)]
  transfers between devices with their start and end apart: 5 -> 7, of which waited for: 1 -> 3; matrix products, arithmetic and copies ran while one was open for 14% -> 14% of each run, Pallas kernels for 0% -> 0%
where the time goes in v17:
time: 170 us; the launch traced here: 169 us
  blocking collectives  72.7 us (43%)
  starting transfers between devices  30.2 us (18%)
  waiting for transfers between devices  23.3 us (14%)
  between operations  15.2 us (9%)
  other arithmetic  12.5 us (7%)
  local copies, waits for them, and re-layouts  10.6 us (6%)
  matrix products  4.27 us (3%)
    all_gather x1, blocking collectives, body(): token_block = lax.all_gather(token_here, ('x', 'c'), axis=0, tiled=True)  42.9 us
    all_to_all x1, blocking collectives, body(): arrived = lax.all_to_all(parts, GROUP, 0, 0, tiled=True)  29.8 us
    all_to_all x2, waiting for transfers between devices, exchange(): second = lax.all_to_all(jnp.swapaxes(first, 0, 1), 'z', 0, 0, tiled=True)  16.9 us
    all_to_all x2, starting transfers between devices, exchange(): first = lax.all_to_all(split, ('x', 'c'), 0, 0, tiled=True)  16.2 us
    all_to_all x2, starting transfers between devices, exchange(): second = lax.all_to_all(jnp.swapaxes(first, 0, 1), 'z', 0, 0, tiled=True)  11.6 us
    all_to_all x2, waiting for transfers between devices, exchange(): first = lax.all_to_all(split, ('x', 'c'), 0, 0, tiled=True)  6.37 us
    reduce_sum x3, other arithmetic, lookup(): return jnp.sum(jnp.where(jnp.arange(table.shape[0]) == index, table, 0))  5.23 us
  transfers between devices with their start and end apart: 7, of which 3 were waited for; matrix products, arithmetic and copies ran while one was open for 14% of the time, Pallas kernels for 0%

profile of v17, /device:TPU:1, one launch (start us, length us, event | category | flops | bytes accessed | tf_op | source)
XLA Modules:
  0.0 168.8 jit_solution(4105222494944308199)
XLA Ops:
  7.3 1.7 %collective-permute-start = (bf16[896,112]{0,1:T(8,128)(2,1)}, bf16[896,112]{0,1:T(8,128)(2,1)S(1)}, u32[]{:S(2)}, u32[]{:S(2)}) collective-permute-start(bf16[896,112]{0,1:T(8,128)(2,1)} %param.21), channel_id=1, source_target_pairs={{0,0},{1,16},{2,32},{3,48},{4,64},{5,80},{6,96},{7,112},{16,1},{17... | collective-permute-start | bytes 602120 | tf_op jit(solution)/shard_map/ppermute | solution.py:126
  9.0 0.9 pad_maximum_fusion
  9.9 0.7 copy.49
  10.6 10.3 %all-to-all-start = ((bf16[8,8,4,256]{3,1,2,0:T(8,128)(2,1)}), bf16[8,8,4,256]{3,1,2,0:T(8,128)(2,1)S(1)}, u32[]{:S(2)}, u32[]{:S(2)}) async-start(bf16[8,8,4,256]{3,1,2,0:T(8,128)(2,1)} %bitcast.3), calls=%async_computation | async-start | bytes 262144 | tf_op jit(solution)/shard_map/all_to_all | solution.py:72
  20.9 0.8 reshape.331
  21.7 1.3 dynamic_slice.3
  23.6 1.3 fusion.32
  24.9 1.9 %fusion.34 = s32[]{:T(128)} fusion(s32[74]{0:T(128)} %param.25, s32[]{:T(128)} %fusion.32), kind=kLoop, calls=%fused_computation.95 | loop fusion | flops 221 | bytes 304 | tf_op jit(solution)/shard_map/reduce_sum | solution.py:62
  26.9 1.4 gather_fusion
  28.7 0.8 gather_fusion.1
  30.1 2.0 %fusion.33 = (s32[]{:T(128)}, s32[]{:T(128)}, s32[]{:T(128)}) fusion(s32[74]{0:T(128)S(1)} %copy-done.10, s32[]{:T(128)} %bitcast, s32[]{:T(128)} %fusion.34, s32[]{:T(128)} %fusion.32), kind=kLoop, calls=%fused_computation.94 | loop fusion | flops 663 | bytes 320 | tf_op jit(solution)/shard_map/reduce_sum | solution.py:62
  32.1 1.2 broadcast_add_fusion
  33.7 0.6 iota_compare_fusion.3
  34.8 1.2 iota_compare_fusion.4
  36.1 0.7 copy.50
  36.8 8.2 %all-to-all-start.1 = ((bf16[8,8,4,256]{3,2,1,0:T(4,128)(2,1)}), bf16[8,8,4,256]{3,2,1,0:T(4,128)(2,1)S(1)}, u32[]{:S(2)}, u32[]{:S(2)}) async-start(bf16[8,8,4,256]{3,2,1,0:T(4,128)(2,1)} %copy.50), calls=%async_computation.1 | async-start | bytes 262144 | tf_op jit(solution)/shard_map/all_to_all | solution.py:73
  45.3 0.5 copy-done.2
  45.8 7.7 %all-to-all-done.1 = bf16[8,8,4,256]{3,2,1,0:T(4,128)(2,1)S(1)} async-done(((bf16[8,8,4,256]{3,2,1,0:T(4,128)(2,1)}), bf16[8,8,4,256]{3,2,1,0:T(4,128)(2,1)S(1)}, u32[]{:S(2)}, u32[]{:S(2)}) %all-to-all-start.1) | async-done | bytes 131104 | tf_op jit(solution)/shard_map/all_to_all | solution.py:73
  53.5 0.6 gather_fusion.2
  54.2 0.8 gather_fusion.3
  55.0 0.8 copy_select_fusion
  55.8 5.9 %all-to-all-start.2 = ((bf16[8,8,2,4,256]{4,1,3,2,0:T(8,128)(2,1)}), bf16[8,8,2,4,256]{4,1,3,2,0:T(8,128)(2,1)S(1)}, u32[]{:S(2)}, u32[]{:S(2)}) async-start(bf16[8,8,2,4,256]{4,1,3,2,0:T(8,128)(2,1)} %bitcast.12), calls=%async_computation.2 | async-start | bytes 524288 | tf_op jit(solution)/shard_map/all_to_all | solution.py:72
  61.9 6.4 %all-to-all-done.2 = bf16[8,8,2,4,256]{4,1,3,2,0:T(8,128)(2,1)S(1)} async-done(((bf16[8,8,2,4,256]{4,1,3,2,0:T(8,128)(2,1)}), bf16[8,8,2,4,256]{4,1,3,2,0:T(8,128)(2,1)S(1)}, u32[]{:S(2)}, u32[]{:S(2)}) %all-to-all-start.2) | async-done | bytes 262176 | tf_op jit(solution)/shard_map/all_to_all | solution.py:72
  68.3 0.8 copy.54
  69.1 3.4 %all-to-all-start.3 = ((bf16[8,8,2,4,256]{4,3,2,1,0:T(4,128)(2,1)}), bf16[8,8,2,4,256]{4,3,2,1,0:T(4,128)(2,1)S(1)}, u32[]{:S(2)}, u32[]{:S(2)}) async-start(bf16[8,8,2,4,256]{4,3,2,1,0:T(4,128)(2,1)} %copy.54), calls=%async_computation.3 | async-start | bytes 524288 | tf_op jit(solution)/shard_map/all_to_all | solution.py:73
  73.3 9.3 %all-to-all-done.3 = bf16[8,8,2,4,256]{4,3,2,1,0:T(4,128)(2,1)S(1)} async-done(((bf16[8,8,2,4,256]{4,3,2,1,0:T(4,128)(2,1)}), bf16[8,8,2,4,256]{4,3,2,1,0:T(4,128)(2,1)S(1)}, u32[]{:S(2)}, u32[]{:S(2)}) %all-to-all-start.3) | async-done | bytes 262176 | tf_op jit(solution)/shard_map/all_to_all | solution.py:73
  84.6 0.7 collective-permute-start.1
  85.3 42.9 %all_gather.6 = bf16[512,896]{1,0:T(8,128)(2,1)S(1)} all-gather(bf16[64,896]{1,0:T(8,128)(2,1)S(1)} %collective-permute-done.1), channel_id=1, replica_groups=mesh['x'=4,'z'=8,'c'=2,'mlp'=8] {'x','c'}, dimensions={0}, use_global_device_ids=true | all-gather | bytes 1032192 | tf_op jit(solution)/shard_map/all_gather | solution.py:188
  128.2 2.6 %convolution_convert_fusion = bf16[512,896]{1,0:T(8,128)(2,1)S(1)} fusion(bf16[512,896]{1,0:T(8,128)(2,1)S(1)} %all_gather.6, bf16[896,896]{0,1:T(8,128)(2,1)} %all-gather.2.cloned.1.call-done), kind=kOutput, calls=%fused_computation.5 | convolution fusion | flops 822542336 | bytes 3440640 | tf_op jit(solution)/shard_map/dot_general | solution.py:189
  130.8 0.5 copy.60
  131.4 29.8 %all_to_all.25 = bf16[8,512,112]{1,2,0:T(8,128)(2,1)S(1)} all-to-all(bf16[8,512,112]{1,2,0:T(8,128)(2,1)S(1)} %bitcast.86), channel_id=1, replica_groups=mesh['x'=4,'z'=8,'c'=2,'mlp'=8] {'z'}, dimensions={0} | all-to-all | bytes 1835008 | tf_op jit(solution)/shard_map/all_to_all | solution.py:193
  161.3 0.7 add_convert_fusion
  (80 shorter events, 5.3 us)
Async XLA Ops:
  7.2 21.5 %copy-start = (s32[74]{0:T(128)S(1)}, s32[74]{0:T(128)}, u32[]{:S(2)}) copy-start(s32[74]{0:T(128)} %param.25) | copy-start | bytes 892
  7.2 22.7 %copy-start.12 = (s32[74]{0:T(128)S(1)}, s32[74]{0:T(128)}, u32[]{:S(2)}) copy-start(s32[74]{0:T(128)} %param.27) | copy-start | bytes 892
  7.2 22.9 %copy-start.8 = (bf16[64,128]{1,0:T(8,128)(2,1)S(1)}, bf16[64,128]{1,0:T(8,128)(2,1)}, u32[]{:S(2)}) copy-start(bf16[64,128]{1,0:T(8,128)(2,1)} %param.15) | copy-start | bytes 49156
  7.2 22.9 %copy-start.10 = (s32[74]{0:T(128)S(1)}, s32[74]{0:T(128)}, u32[]{:S(2)}) copy-start(s32[74]{0:T(128)} %param.26) | copy-start | bytes 892
  7.2 24.9 %copy-start.11 = (s32[64]{0:T(128)S(1)}, s32[64]{0:T(128)}, u32[]{:S(2)}) copy-start(s32[64]{0:T(128)} %param.24) | copy-start | bytes 772
  7.2 27.2 %copy-start.9 = (bf16[64,128]{1,0:T(8,128)(2,1)S(1)}, bf16[64,128]{1,0:T(8,128)(2,1)}, u32[]{:S(2)}) copy-start(bf16[64,128]{1,0:T(8,128)(2,1)} %param.16) | copy-start | bytes 49156
  7.2 27.4 %copy-start.6 = (bf16[320,128]{1,0:T(8,128)(2,1)S(1)}, bf16[320,128]{1,0:T(8,128)(2,1)}, u32[]{:S(2)}) copy-start(bf16[320,128]{1,0:T(8,128)(2,1)} %param.17) | copy-start | bytes 245764
  7.2 27.4 %copy-start.5 = (bf16[320,128]{1,0:T(8,128)(2,1)S(1)}, bf16[320,128]{1,0:T(8,128)(2,1)}, u32[]{:S(2)}) copy-start(bf16[320,128]{1,0:T(8,128)(2,1)} %param.18) | copy-start | bytes 245764
  7.3 37.9 %collective-permute-start = (bf16[896,112]{0,1:T(8,128)(2,1)}, bf16[896,112]{0,1:T(8,128)(2,1)S(1)}, u32[]{:S(2)}, u32[]{:S(2)}) collective-permute-start(bf16[896,112]{0,1:T(8,128)(2,1)} %param.21), channel_id=1, source_target_pairs={{0,0},{1,16},{2,32},{3,48},{4,64},{5,80},{6,96},{7,112},{16,1},{17... | collective-permute-start | bytes 602120 | tf_op jit(solution)/shard_map/ppermute | solution.py:126
  10.6 34.5 %copy-start.4 = (bf16[64,896]{1,0:T(8,128)(2,1)S(1)}, bf16[64,896]{1,0:T(8,128)(2,1)}, u32[]{:S(2)}) copy-start(bf16[64,896]{1,0:T(8,128)(2,1)} %param.14) | copy-start | bytes 344068
  10.6 25.5 %all-to-all-start = ((bf16[8,8,4,256]{3,1,2,0:T(8,128)(2,1)}), bf16[8,8,4,256]{3,1,2,0:T(8,128)(2,1)S(1)}, u32[]{:S(2)}, u32[]{:S(2)}) async-start(bf16[8,8,4,256]{3,1,2,0:T(8,128)(2,1)} %bitcast.3), calls=%async_computation | async-start | bytes 262144 | tf_op jit(solution)/shard_map/all_to_all | solution.py:72
  34.8 37.8 %copy-start.1 = (bf16[320,128]{1,0:T(8,128)(2,1)}, bf16[320,128]{1,0:T(8,128)(2,1)S(1)}, u32[]{:S(2)}) copy-start(bf16[320,128]{1,0:T(8,128)(2,1)S(1)} %get-tuple-element.24) | copy-start | bytes 245764
  34.8 49.4 %copy-start.7 = (bf16[320,128]{1,0:T(8,128)(2,1)}, bf16[320,128]{1,0:T(8,128)(2,1)S(1)}, u32[]{:S(2)}) copy-start(bf16[320,128]{1,0:T(8,128)(2,1)S(1)} %get-tuple-element.23) | copy-start | bytes 245764
  36.8 16.7 %all-to-all-start.1 = ((bf16[8,8,4,256]{3,2,1,0:T(4,128)(2,1)}), bf16[8,8,4,256]{3,2,1,0:T(4,128)(2,1)S(1)}, u32[]{:S(2)}, u32[]{:S(2)}) async-start(bf16[8,8,4,256]{3,2,1,0:T(4,128)(2,1)} %copy.50), calls=%async_computation.1 | async-start | bytes 262144 | tf_op jit(solution)/shard_map/all_to_all | solution.py:73
  44.9 83.2 %all-gather.2.cloned.1.call-start = ((), (), s32[]{:S(2)}) async-start(), calls=%async_computation.5 | async-start | bytes 1806336 | tf_op jit(solution)/shard_map/all_gather | solution.py:128
  45.1 0.7 copy-start.2
  55.8 12.4 %all-to-all-start.2 = ((bf16[8,8,2,4,256]{4,1,3,2,0:T(8,128)(2,1)}), bf16[8,8,2,4,256]{4,1,3,2,0:T(8,128)(2,1)S(1)}, u32[]{:S(2)}, u32[]{:S(2)}) async-start(bf16[8,8,2,4,256]{4,1,3,2,0:T(8,128)(2,1)} %bitcast.12), calls=%async_computation.2 | async-start | bytes 524288 | tf_op jit(solution)/shard_map/all_to_all | solution.py:72
  69.1 13.5 %all-to-all-start.3 = ((bf16[8,8,2,4,256]{4,3,2,1,0:T(4,128)(2,1)}), bf16[8,8,2,4,256]{4,3,2,1,0:T(4,128)(2,1)S(1)}, u32[]{:S(2)}, u32[]{:S(2)}) async-start(bf16[8,8,2,4,256]{4,3,2,1,0:T(4,128)(2,1)} %copy.54), calls=%async_computation.3 | async-start | bytes 524288 | tf_op jit(solution)/shard_map/all_to_all | solution.py:73
  84.6 0.7 collective-permute-start.1
  131.4 29.9 %copy-start.3 = (bf16[512,112]{0,1:T(8,128)(2,1)S(1)}, bf16[512,112]{0,1:T(8,128)(2,1)}, u32[]{:S(2)}) copy-start(bf16[512,112]{0,1:T(8,128)(2,1)} %param.22) | copy-start | bytes 344068
Sparse Core Ops, SparseCore 0:
  47.9 41.2 all-gather.1

commit v18 on v12

--- a/solution.py
+++ b/solution.py
@@ -112,7 +112,14 @@
     ]
     weight_here = lax.ppermute(out_weight, GROUP + ("mlp",), swap)
     weight_here, queries = lax.optimization_barrier((weight_here, queries))
-    weight_cols = lax.all_gather(weight_here, "mlp", axis=1, tiled=True)
+    half = weight_here.shape[0] // 2
+    weight_cols = jnp.concatenate(
+        [
+            lax.all_gather(weight_here[:half], "mlp", axis=1, tiled=True),
+            lax.all_gather(weight_here[half:], "mlp", axis=1, tiled=True),
+        ],
+        axis=0,
+    )
     query_turned = apply_rotary(queries, positions, q_heads)
     key_turned = apply_rotary(fresh_token_keys, positions, kv_heads)
     my_request = lax.dynamic_slice_in_dim(token_request, my_index * tok_rows, 1)[0]

time: 159 us -> 176 us (1.11)
  blocking collectives: 75.3 us -> 116 us
  between operations: 15.1 us -> 1.74 us
  waiting for transfers between devices: 11.2 us -> 0.01 us
  starting transfers between devices: 30.1 us -> 35.6 us
  other arithmetic: 14.1 us -> 11.5 us
    all_gather x0 -> x2, blocking collectives: none -> 55.3 us  [the longest x1 31.7 us: body(): lax.all_gather(weight_here[half:], 'mlp', axis=1, tiled=True)]
    all_gather x1, blocking collectives: 43.1 us -> 24.5 us  [body(): token_block = lax.all_gather(token_here, ('x', 'c'), axis=0, tiled=True)]
    all_to_all x1, waiting for transfers between devices: 11.2 us -> 0.01 us  [body(): incoming = lax.all_to_all(outgoing, TOK, 0, 0, tiled=True)]
    all_to_all x1, starting transfers between devices: 10.3 us -> 18.4 us  [body(): incoming = lax.all_to_all(outgoing, TOK, 0, 0, tiled=True)]
    all_to_all x1, blocking collectives: 32.1 us -> 36 us  [body(): arrived = lax.all_to_all(parts, GROUP, 0, 0, tiled=True)]
    all_to_all x1, starting transfers between devices: 17.3 us -> 15 us  [body(): spread = lax.all_to_all(pieces, TOK, 0, 0, tiled=True)]
    reduce_sum x3, other arithmetic: 5.9 us -> 3.91 us  [lookup(): return jnp.sum(jnp.where(jnp.arange(table.shape[0]) == index, table, 0))]
  transfers between devices with their start and end apart: 5 -> 4, of which waited for: 1 -> 0; matrix products, arithmetic and copies ran while one was open for 14% -> 8% of each run, Pallas kernels for 0% -> 0%
where the time goes in v18:
time: 176 us
  blocking collectives  116 us (66%)
  starting transfers between devices  35.6 us (20%)
  other arithmetic  11.5 us (7%)
  local copies, waits for them, and re-layouts  8.24 us (5%)
  matrix products  2.93 us (2%)
    all_to_all x1, blocking collectives, body(): arrived = lax.all_to_all(parts, GROUP, 0, 0, tiled=True)  36 us
    all_gather x1, blocking collectives, body(): lax.all_gather(weight_here[half:], 'mlp', axis=1, tiled=True)  31.7 us
    all_gather x1, blocking collectives, body(): token_block = lax.all_gather(token_here, ('x', 'c'), axis=0, tiled=True)  24.5 us
    all_gather x1, blocking collectives, body(): lax.all_gather(weight_here[:half], 'mlp', axis=1, tiled=True)  23.6 us
    all_to_all x1, starting transfers between devices, body(): incoming = lax.all_to_all(outgoing, TOK, 0, 0, tiled=True)  18.4 us
    all_to_all x1, starting transfers between devices, body(): spread = lax.all_to_all(pieces, TOK, 0, 0, tiled=True)  15 us
    reduce_sum x3, other arithmetic, lookup(): return jnp.sum(jnp.where(jnp.arange(table.shape[0]) == index, table, 0))  3.91 us
  transfers between devices with their start and end apart: 4, of which 0 were waited for; matrix products, arithmetic and copies ran while one was open for 8% of the time, Pallas kernels for 0%

profile of v18, /device:TPU:1, one launch (start us, length us, event | category | flops | bytes accessed | tf_op | source)
XLA Modules:
  0.0 175.8 jit_solution(5949553460785203727)
XLA Ops:
  0.6 0.9 pad_maximum_fusion
  1.6 0.7 reshape.313
  2.3 15.0 %all-to-all-start = ((bf16[64,4,256]{2,1,0:T(4,128)(2,1)}), bf16[64,4,256]{2,1,0:T(4,128)(2,1)S(1)}, u32[]{:S(2)}, u32[]{:S(2)}) async-start(bf16[64,4,256]{2,1,0:T(4,128)(2,1)} %reshape.313), calls=%async_computation | async-start | bytes 262144 | tf_op jit(solution)/shard_map/all_to_all | solution.py:97
  17.2 1.6 collective-permute-start
  18.9 0.8 reshape.312
  19.8 0.8 gather_fusion
  20.8 0.8 gather_fusion.1
  21.6 1.3 dynamic_slice.3
  23.6 0.6 fusion.39
  24.2 1.3 fusion.41
  25.5 2.0 %fusion.40 = (s32[]{:T(128)}, s32[]{:T(128)}, s32[]{:T(128)}) fusion(s32[74]{0:T(128)S(1)} %copy-done.9, s32[]{:T(128)} %bitcast, s32[]{:T(128)} %fusion.41, s32[]{:T(128)} %fusion.39), kind=kLoop, calls=%fused_computation.98 | loop fusion | flops 663 | bytes 320 | tf_op jit(solution)/shard_map/reduce_sum | solution.py:62
  27.5 0.6 iota_compare_fusion.3
  28.0 1.3 iota_compare_fusion.4
  29.4 1.3 broadcast_add_fusion
  32.6 0.6 gather_fusion.2
  33.3 0.8 gather_fusion.3
  34.1 0.9 broadcast_select_fusion
  35.0 18.4 %all-to-all-start.1 = ((bf16[64,2,4,256]{3,2,1,0:T(4,128)(2,1)}), bf16[64,2,4,256]{3,2,1,0:T(4,128)(2,1)S(1)}, u32[]{:S(2)}, u32[]{:S(2)}) async-start(bf16[64,2,4,256]{3,2,1,0:T(4,128)(2,1)} %broadcast_select_fusion), calls=%async_computation.1 | async-start | bytes 524288 | tf_op jit(solution)/shard_map/all_to_all | solution.py:106
  53.4 0.4 select_reduce_fusion.1
  54.1 23.6 %all_gather.10 = bf16[448,896]{0,1:T(8,128)(2,1)S(1)} all-gather(bf16[448,112]{0,1:T(8,128)(2,1)S(1)} %get-tuple-element.23), channel_id=1, replica_groups=mesh['x'=4,'z'=8,'c'=2,'mlp'=8] {'mlp'}, dimensions={1}, use_global_device_ids=true | all-gather | bytes 903168 | tf_op jit(solution)/shard_map/all_gather | solution.py:118
  77.9 0.4 select_reduce_fusion
  78.3 0.3 convert_reduce_fusion.1
  78.7 0.3 fusion.12
  79.0 0.3 fusion.14
  79.5 0.7 collective-permute-start.1
  80.2 31.7 %all_gather.11 = bf16[448,896]{0,1:T(8,128)(2,1)S(1)} all-gather(bf16[448,112]{0,1:T(8,128)(2,1)S(1)} %get-tuple-element.24), channel_id=1, replica_groups=mesh['x'=4,'z'=8,'c'=2,'mlp'=8] {'mlp'}, dimensions={1}, use_global_device_ids=true | all-gather | bytes 903168 | tf_op jit(solution)/shard_map/all_gather | solution.py:119
  111.9 24.5 %all_gather.9 = bf16[512,896]{1,0:T(8,128)(2,1)S(1)} all-gather(bf16[64,896]{1,0:T(8,128)(2,1)S(1)} %collective-permute-done.1), channel_id=1, replica_groups=mesh['x'=4,'z'=8,'c'=2,'mlp'=8] {'x','c'}, dimensions={0}, use_global_device_ids=true | all-gather | bytes 1032192 | tf_op jit(solution)/shard_map/all_gather | solution.py:182
  136.4 1.3 fusion.4
  137.7 0.5 copy.35
  138.2 36.0 %all_to_all.15 = bf16[8,512,112]{1,2,0:T(8,128)(2,1)S(1)} all-to-all(bf16[8,512,112]{1,2,0:T(8,128)(2,1)S(1)} %bitcast.70), channel_id=1, replica_groups=mesh['x'=4,'z'=8,'c'=2,'mlp'=8] {'z'}, dimensions={0} | all-to-all | bytes 1835008 | tf_op jit(solution)/shard_map/all_to_all | solution.py:187
  174.4 0.8 copy-done.2
  175.2 0.7 add_convert_fusion
  (64 shorter events, 3.0 us)
Async XLA Ops:
  0.6 19.2 %copy-start = (s32[74]{0:T(128)S(1)}, s32[74]{0:T(128)}, u32[]{:S(2)}) copy-start(s32[74]{0:T(128)} %param.25) | copy-start | bytes 892
  1.5 23.9 %copy-start.9 = (s32[74]{0:T(128)S(1)}, s32[74]{0:T(128)}, u32[]{:S(2)}) copy-start(s32[74]{0:T(128)} %param.26) | copy-start | bytes 892
  1.5 27.8 %copy-start.10 = (s32[64]{0:T(128)S(1)}, s32[64]{0:T(128)}, u32[]{:S(2)}) copy-start(s32[64]{0:T(128)} %param.24) | copy-start | bytes 772
  1.6 29.1 %copy-start.11 = (s32[74]{0:T(128)S(1)}, s32[74]{0:T(128)}, u32[]{:S(2)}) copy-start(s32[74]{0:T(128)} %param.27) | copy-start | bytes 892
  1.6 29.2 %copy-start.7 = (bf16[64,128]{1,0:T(8,128)(2,1)S(1)}, bf16[64,128]{1,0:T(8,128)(2,1)}, u32[]{:S(2)}) copy-start(bf16[64,128]{1,0:T(8,128)(2,1)} %param.15) | copy-start | bytes 49156
  2.3 29.4 %copy-start.8 = (bf16[64,128]{1,0:T(8,128)(2,1)S(1)}, bf16[64,128]{1,0:T(8,128)(2,1)}, u32[]{:S(2)}) copy-start(bf16[64,128]{1,0:T(8,128)(2,1)} %param.16) | copy-start | bytes 49156
  2.3 30.3 %all-to-all-start = ((bf16[64,4,256]{2,1,0:T(4,128)(2,1)}), bf16[64,4,256]{2,1,0:T(4,128)(2,1)S(1)}, u32[]{:S(2)}, u32[]{:S(2)}) async-start(bf16[64,4,256]{2,1,0:T(4,128)(2,1)} %reshape.313), calls=%async_computation | async-start | bytes 262144 | tf_op jit(solution)/shard_map/all_to_all | solution.py:97
  17.2 14.8 %collective-permute-start = (bf16[896,112]{0,1:T(8,128)(2,1)}, bf16[896,112]{0,1:T(8,128)(2,1)S(1)}, u32[]{:S(2)}, u32[]{:S(2)}) collective-permute-start(bf16[896,112]{0,1:T(8,128)(2,1)} %param.21), channel_id=1, source_target_pairs={{0,0},{1,16},{2,32},{3,48},{4,64},{5,80},{6,96},{7,112},{16,1},{17... | collective-permute-start | bytes 602120 | tf_op jit(solution)/shard_map/ppermute | solution.py:113
  18.8 13.0 %copy-start.4 = (bf16[320,128]{1,0:T(8,128)(2,1)S(1)}, bf16[320,128]{1,0:T(8,128)(2,1)}, u32[]{:S(2)}) copy-start(bf16[320,128]{1,0:T(8,128)(2,1)} %param.18) | copy-start | bytes 245764
  18.8 13.0 %copy-start.5 = (bf16[320,128]{1,0:T(8,128)(2,1)S(1)}, bf16[320,128]{1,0:T(8,128)(2,1)}, u32[]{:S(2)}) copy-start(bf16[320,128]{1,0:T(8,128)(2,1)} %param.17) | copy-start | bytes 245764
  20.6 11.5 %copy-start.3 = (bf16[64,896]{1,0:T(8,128)(2,1)S(1)}, bf16[64,896]{1,0:T(8,128)(2,1)}, u32[]{:S(2)}) copy-start(bf16[64,896]{1,0:T(8,128)(2,1)} %param.14) | copy-start | bytes 344068
  31.9 21.5 %copy-start.1 = (bf16[320,128]{1,0:T(8,128)(2,1)}, bf16[320,128]{1,0:T(8,128)(2,1)S(1)}, u32[]{:S(2)}) copy-start(bf16[320,128]{1,0:T(8,128)(2,1)S(1)} %get-tuple-element.26) | copy-start | bytes 245764
  32.0 47.1 %copy-start.6 = (bf16[320,128]{1,0:T(8,128)(2,1)}, bf16[320,128]{1,0:T(8,128)(2,1)S(1)}, u32[]{:S(2)}) copy-start(bf16[320,128]{1,0:T(8,128)(2,1)S(1)} %get-tuple-element.25) | copy-start | bytes 245764
  35.0 42.7 %all-to-all-start.1 = ((bf16[64,2,4,256]{3,2,1,0:T(4,128)(2,1)}), bf16[64,2,4,256]{3,2,1,0:T(4,128)(2,1)S(1)}, u32[]{:S(2)}, u32[]{:S(2)}) async-start(bf16[64,2,4,256]{3,2,1,0:T(4,128)(2,1)} %broadcast_select_fusion), calls=%async_computation.1 | async-start | bytes 524288 | tf_op jit(solution)/shard_map/all_to_all | solution.py:106
  79.5 32.4 %collective-permute-start.1 = (bf16[64,896]{1,0:T(8,128)(2,1)S(1)}, bf16[64,896]{1,0:T(8,128)(2,1)S(1)}, u32[]{:S(2)}, u32[]{:S(2)}) collective-permute-start(bf16[64,896]{1,0:T(8,128)(2,1)S(1)} %bitcast.73), channel_id=1, source_target_pairs={{0,0},{1,16},{2,32},{3,48},{4,64},{5,80},{6,96},{7,112},{8,8},{9,2... | collective-permute-start | bytes 344072 | tf_op jit(solution)/shard_map/ppermute | solution.py:181
  174.3 0.9 copy-start.2

commit v19 on v12

--- a/solution.py
+++ b/solution.py
@@ -173,10 +173,12 @@
             )
     token_here = lax.ppermute(attended_local, TOK + ("mlp",), spread_route)
     token_block = lax.all_gather(token_here, ("x", "c"), axis=0, tiled=True)
-    projected = jnp.dot(token_block, weight_cols, preferred_element_type=jnp.float32).astype(
-        jnp.bfloat16
-    )
-    parts = projected.reshape(projected.shape[0], group_count, -1).transpose(1, 0, 2)
+    parts = jnp.einsum(
+        "tf,fjc->jtc",
+        token_block,
+        weight_cols.reshape(weight_cols.shape[0], group_count, -1),
+        preferred_element_type=jnp.float32,
+    ).astype(jnp.bfloat16)
     arrived = lax.all_to_all(parts, GROUP, 0, 0, tiled=True)
     summed = jnp.sum(arrived.astype(jnp.float32), axis=0)
     hidden = (residual.astype(jnp.float32) + summed).astype(jnp.bfloat16)

time: 159 us -> 159 us (level)
  no operation moved by 1% of the time
where the time goes in v19:
time: 159 us; the launch traced here: 158 us
  blocking collectives  75.3 us (47%)
  starting transfers between devices  30.1 us (19%)
  between operations  15.1 us (9%)
  other arithmetic  14.1 us (9%)
  waiting for transfers between devices  11.2 us (7%)
  local copies, waits for them, and re-layouts  7.97 us (5%)
  matrix products  4.21 us (3%)
    all_gather x1, blocking collectives, body(): token_block = lax.all_gather(token_here, ('x', 'c'), axis=0, tiled=True)  43.2 us
    all_to_all x1, blocking collectives, body(): arrived = lax.all_to_all(parts, GROUP, 0, 0, tiled=True)  32.2 us
    all_to_all x1, starting transfers between devices, body(): spread = lax.all_to_all(pieces, TOK, 0, 0, tiled=True)  17.3 us
    all_to_all x1, waiting for transfers between devices, body(): incoming = lax.all_to_all(outgoing, TOK, 0, 0, tiled=True)  11.2 us
    all_to_all x1, starting transfers between devices, body(): incoming = lax.all_to_all(outgoing, TOK, 0, 0, tiled=True)  10.3 us
    reduce_sum x3, other arithmetic, lookup(): return jnp.sum(jnp.where(jnp.arange(table.shape[0]) == index, table, 0))  5.9 us
  transfers between devices with their start and end apart: 5, of which 1 were waited for; matrix products, arithmetic and copies ran while one was open for 14% of the time, Pallas kernels for 0%

profile of v19, /device:TPU:1, one launch (start us, length us, event | category | flops | bytes accessed | tf_op | source)
XLA Modules:
  0.0 158.0 jit_solution(2801634708151485943)
XLA Ops:
  7.2 1.7 %collective-permute-start = (bf16[896,112]{0,1:T(8,128)(2,1)}, bf16[896,112]{0,1:T(8,128)(2,1)S(1)}, u32[]{:S(2)}, u32[]{:S(2)}) collective-permute-start(bf16[896,112]{0,1:T(8,128)(2,1)} %param.21), channel_id=1, source_target_pairs={{0,0},{1,16},{2,32},{3,48},{4,64},{5,80},{6,96},{7,112},{16,1},{17... | collective-permute-start | bytes 602120 | tf_op jit(solution)/shard_map/ppermute | solution.py:113
  9.0 0.9 pad_maximum_fusion
  9.8 0.7 reshape.314
  10.5 17.3 %all-to-all-start = ((bf16[64,4,256]{2,1,0:T(4,128)(2,1)}), bf16[64,4,256]{2,1,0:T(4,128)(2,1)S(1)}, u32[]{:S(2)}, u32[]{:S(2)}) async-start(bf16[64,4,256]{2,1,0:T(4,128)(2,1)} %reshape.314), calls=%async_computation | async-start | bytes 262144 | tf_op jit(solution)/shard_map/all_to_all | solution.py:97
  27.9 0.8 reshape.313
  28.7 1.3 dynamic_slice.3
  30.6 1.3 fusion.34
  31.9 1.9 %fusion.36 = s32[]{:T(128)} fusion(s32[74]{0:T(128)} %param.25, s32[]{:T(128)} %fusion.34), kind=kLoop, calls=%fused_computation.97 | loop fusion | flops 221 | bytes 304 | tf_op jit(solution)/shard_map/reduce_sum | solution.py:62
  33.9 2.7 %fusion.35 = (s32[]{:T(128)}, s32[]{:T(128)}, s32[]{:T(128)}) fusion(s32[74]{0:T(128)} %param.26, s32[]{:T(128)} %bitcast.1, s32[]{:T(128)} %fusion.36, s32[]{:T(128)} %fusion.34), kind=kLoop, calls=%fused_computation.96 | loop fusion | flops 663 | bytes 320 | tf_op jit(solution)/shard_map/reduce_sum | solution.py:62
  36.5 1.2 iota_compare_fusion.4
  37.7 1.9 %broadcast_add_fusion = (s32[64]{0:T(128)S(1)}, s32[64]{0:T(128)S(1)}, f32[64]{0:T(128)S(1)}) fusion(s32[]{:T(128)} %get-tuple-element.9, s32[64]{0:T(128)} %param.24, s32[]{:T(128)} %get-tuple-element.8), kind=kLoop, calls=%fused_computation.103 | loop fusion | flops 256 | bytes 1032 | tf_op jit(solution)/shard_map/add | solution.py:135
  39.8 1.4 gather_fusion
  41.5 0.8 gather_fusion.1
  42.8 0.2 fusion.24
  43.0 0.7 iota_compare_fusion.3
  44.5 0.5 copy-done.2
  45.2 0.6 gather_fusion.2
  45.9 0.8 gather_fusion.3
  46.7 0.9 broadcast_select_fusion
  47.7 10.3 %all-to-all-start.1 = ((bf16[64,2,4,256]{3,2,1,0:T(4,128)(2,1)}), bf16[64,2,4,256]{3,2,1,0:T(4,128)(2,1)S(1)}, u32[]{:S(2)}, u32[]{:S(2)}) async-start(bf16[64,2,4,256]{3,2,1,0:T(4,128)(2,1)} %broadcast_select_fusion), calls=%async_computation.1 | async-start | bytes 524288 | tf_op jit(solution)/shard_map/all_to_all | solution.py:106
  58.1 0.4 select_reduce_fusion.1
  58.5 0.3 convert_reduce_fusion.2
  58.8 11.2 %all-to-all-done.1 = bf16[64,2,4,256]{3,2,1,0:T(4,128)(2,1)S(1)} async-done(((bf16[64,2,4,256]{3,2,1,0:T(4,128)(2,1)}), bf16[64,2,4,256]{3,2,1,0:T(4,128)(2,1)S(1)}, u32[]{:S(2)}, u32[]{:S(2)}) %all-to-all-start.1) | async-done | bytes 262176 | tf_op jit(solution)/shard_map/all_to_all | solution.py:106
  70.2 0.4 select_reduce_fusion
  70.6 0.3 convert_reduce_fusion.1
  71.0 0.3 fusion.6
  71.3 0.3 fusion.8
  71.8 0.7 collective-permute-start.1
  72.5 43.2 %all_gather.7 = bf16[512,896]{1,0:T(8,128)(2,1)S(1)} all-gather(bf16[64,896]{1,0:T(8,128)(2,1)S(1)} %collective-permute-done.1), channel_id=1, replica_groups=mesh['x'=4,'z'=8,'c'=2,'mlp'=8] {'x','c'}, dimensions={0}, use_global_device_ids=true | all-gather | bytes 1032192 | tf_op jit(solution)/shard_map/all_gather | solution.py:175
  115.6 2.6 %fusion = bf16[8,512,112]{1,2,0:T(8,128)(2,1)S(1)} fusion(bf16[896,8,112]{0,2,1:T(8,128)(2,1)} %bitcast.81, bf16[512,896]{1,0:T(8,128)(2,1)S(1)} %all_gather.7), kind=kOutput, calls=%fused_computation.6 | convolution fusion | flops 822542336 | bytes 3440640 | tf_op jit(solution)/shard_map/tf,fjc->jtc/dot_general | solution.py:176
  118.2 32.2 %all_to_all.15 = bf16[8,512,112]{1,2,0:T(8,128)(2,1)S(1)} all-to-all(bf16[8,512,112]{1,2,0:T(8,128)(2,1)S(1)} %fusion), channel_id=1, replica_groups=mesh['x'=4,'z'=8,'c'=2,'mlp'=8] {'z'}, dimensions={0} | all-to-all | bytes 1835008 | tf_op jit(solution)/shard_map/all_to_all | solution.py:182
  150.5 0.7 add_convert_fusion
  (61 shorter events, 2.4 us)
Async XLA Ops:
  7.2 34.3 %copy-start = (s32[74]{0:T(128)S(1)}, s32[74]{0:T(128)}, u32[]{:S(2)}) copy-start(s32[74]{0:T(128)} %param.25) | copy-start | bytes 892
  7.2 35.3 %copy-start.10 = (s32[74]{0:T(128)S(1)}, s32[74]{0:T(128)}, u32[]{:S(2)}) copy-start(s32[74]{0:T(128)} %param.27) | copy-start | bytes 892
  7.2 35.4 %copy-start.8 = (bf16[64,128]{1,0:T(8,128)(2,1)S(1)}, bf16[64,128]{1,0:T(8,128)(2,1)}, u32[]{:S(2)}) copy-start(bf16[64,128]{1,0:T(8,128)(2,1)} %param.15) | copy-start | bytes 49156
  7.2 36.7 %copy-start.9 = (bf16[64,128]{1,0:T(8,128)(2,1)S(1)}, bf16[64,128]{1,0:T(8,128)(2,1)}, u32[]{:S(2)}) copy-start(bf16[64,128]{1,0:T(8,128)(2,1)} %param.16) | copy-start | bytes 49156
  7.2 36.8 %copy-start.6 = (bf16[320,128]{1,0:T(8,128)(2,1)S(1)}, bf16[320,128]{1,0:T(8,128)(2,1)}, u32[]{:S(2)}) copy-start(bf16[320,128]{1,0:T(8,128)(2,1)} %param.17) | copy-start | bytes 245764
  7.2 36.8 %copy-start.5 = (bf16[320,128]{1,0:T(8,128)(2,1)S(1)}, bf16[320,128]{1,0:T(8,128)(2,1)}, u32[]{:S(2)}) copy-start(bf16[320,128]{1,0:T(8,128)(2,1)} %param.18) | copy-start | bytes 245764
  7.2 37.1 %copy-start.4 = (bf16[64,896]{1,0:T(8,128)(2,1)S(1)}, bf16[64,896]{1,0:T(8,128)(2,1)}, u32[]{:S(2)}) copy-start(bf16[64,896]{1,0:T(8,128)(2,1)} %param.14) | copy-start | bytes 344068
  7.2 37.1 %collective-permute-start = (bf16[896,112]{0,1:T(8,128)(2,1)}, bf16[896,112]{0,1:T(8,128)(2,1)S(1)}, u32[]{:S(2)}, u32[]{:S(2)}) collective-permute-start(bf16[896,112]{0,1:T(8,128)(2,1)} %param.21), channel_id=1, source_target_pairs={{0,0},{1,16},{2,32},{3,48},{4,64},{5,80},{6,96},{7,112},{16,1},{17... | collective-permute-start | bytes 602120 | tf_op jit(solution)/shard_map/ppermute | solution.py:113
  10.5 34.7 %all-to-all-start = ((bf16[64,4,256]{2,1,0:T(4,128)(2,1)}), bf16[64,4,256]{2,1,0:T(4,128)(2,1)S(1)}, u32[]{:S(2)}, u32[]{:S(2)}) async-start(bf16[64,4,256]{2,1,0:T(4,128)(2,1)} %reshape.314), calls=%async_computation | async-start | bytes 262144 | tf_op jit(solution)/shard_map/all_to_all | solution.py:97
  27.9 87.8 %all-gather.2.cloned.1.call-start = ((), (), s32[]{:S(2)}) async-start(), calls=%async_computation.3 | async-start | bytes 1806336 | tf_op jit(solution)/shard_map/all_gather | solution.py:115
  44.2 13.9 %copy-start.1 = (bf16[320,128]{1,0:T(8,128)(2,1)}, bf16[320,128]{1,0:T(8,128)(2,1)S(1)}, u32[]{:S(2)}) copy-start(bf16[320,128]{1,0:T(8,128)(2,1)S(1)} %get-tuple-element.24) | copy-start | bytes 245764
  44.2 27.1 %copy-start.7 = (bf16[320,128]{1,0:T(8,128)(2,1)}, bf16[320,128]{1,0:T(8,128)(2,1)S(1)}, u32[]{:S(2)}) copy-start(bf16[320,128]{1,0:T(8,128)(2,1)S(1)} %get-tuple-element.23) | copy-start | bytes 245764
  44.4 0.7 copy-start.2
  47.7 22.3 %all-to-all-start.1 = ((bf16[64,2,4,256]{3,2,1,0:T(4,128)(2,1)}), bf16[64,2,4,256]{3,2,1,0:T(4,128)(2,1)S(1)}, u32[]{:S(2)}, u32[]{:S(2)}) async-start(bf16[64,2,4,256]{3,2,1,0:T(4,128)(2,1)} %broadcast_select_fusion), calls=%async_computation.1 | async-start | bytes 524288 | tf_op jit(solution)/shard_map/all_to_all | solution.py:106
  71.8 0.7 collective-permute-start.1
  118.2 32.3 %copy-start.3 = (bf16[512,112]{0,1:T(8,128)(2,1)S(1)}, bf16[512,112]{0,1:T(8,128)(2,1)}, u32[]{:S(2)}) copy-start(bf16[512,112]{0,1:T(8,128)(2,1)} %param.22) | copy-start | bytes 344068
Sparse Core Ops, SparseCore 0:
  45.2 60.8 all-gather.1

commit v20 on v19

--- a/solution.py
+++ b/solution.py
@@ -95,12 +95,11 @@
     piece_rows = node_rows // tok_count
     pieces = my_pair.reshape(tok_count, piece_rows, my_pair.shape[1])
     spread = lax.all_to_all(pieces, TOK, 0, 0, tiled=True)
-    held = jnp.take(spread, node_owner[:shared_count], axis=0)
     requests = token_request.reshape(-1, tok_rows)[:, 0]
     middles = parents[shared_count + requests]
     roots = parents[middles]
     wanted = jnp.stack([roots, middles], axis=1)
-    outgoing = jnp.take(held, wanted.reshape(-1), axis=0).reshape(
+    outgoing = jnp.take(spread, node_owner[wanted.reshape(-1)], axis=0).reshape(
         (tok_count, 2, piece_rows, my_pair.shape[1])
     )
     incoming = lax.all_to_all(outgoing, TOK, 0, 0, tiled=True)

time: 159 us -> 157 us (0.987)
  other arithmetic: 14.1 us -> 11.3 us
    reduce_sum x3, other arithmetic: 5.9 us -> 3.91 us  [lookup(): return jnp.sum(jnp.where(jnp.arange(table.shape[0]) == index, table, 0))]
  transfers between devices with their start and end apart: 5 -> 5, of which waited for: 1 -> 1; matrix products, arithmetic and copies ran while one was open for 14% -> 13% of each run, Pallas kernels for 0% -> 0%
where the time goes in v20:
time: 157 us; the launch traced here: 156 us
  blocking collectives  75.2 us (48%)
  starting transfers between devices  30.2 us (19%)
  between operations  15.2 us (10%)
  other arithmetic  11.3 us (7%)
  waiting for transfers between devices  11.2 us (7%)
  local copies, waits for them, and re-layouts  8.65 us (6%)
  matrix products  4.2 us (3%)
    all_gather x1, blocking collectives, body(): token_block = lax.all_gather(token_here, ('x', 'c'), axis=0, tiled=True)  43.3 us
    all_to_all x1, blocking collectives, body(): arrived = lax.all_to_all(parts, GROUP, 0, 0, tiled=True)  31.9 us
    all_to_all x1, starting transfers between devices, body(): spread = lax.all_to_all(pieces, TOK, 0, 0, tiled=True)  17.5 us
    all_to_all x1, waiting for transfers between devices, body(): incoming = lax.all_to_all(outgoing, TOK, 0, 0, tiled=True)  11.2 us
    all_to_all x1, starting transfers between devices, body(): incoming = lax.all_to_all(outgoing, TOK, 0, 0, tiled=True)  10.3 us
    reduce_sum x3, other arithmetic, lookup(): return jnp.sum(jnp.where(jnp.arange(table.shape[0]) == index, table, 0))  3.91 us
  transfers between devices with their start and end apart: 5, of which 1 were waited for; matrix products, arithmetic and copies ran while one was open for 13% of the time, Pallas kernels for 0%

profile of v20, /device:TPU:1, one launch (start us, length us, event | category | flops | bytes accessed | tf_op | source)
XLA Modules:
  0.0 155.9 jit_solution(7371679633803627311)
XLA Ops:
  7.3 1.7 %collective-permute-start = (bf16[896,112]{0,1:T(8,128)(2,1)}, bf16[896,112]{0,1:T(8,128)(2,1)S(1)}, u32[]{:S(2)}, u32[]{:S(2)}) collective-permute-start(bf16[896,112]{0,1:T(8,128)(2,1)} %param.21), channel_id=1, source_target_pairs={{0,0},{1,16},{2,32},{3,48},{4,64},{5,80},{6,96},{7,112},{16,1},{17... | collective-permute-start | bytes 602120 | tf_op jit(solution)/shard_map/ppermute | solution.py:112
  9.0 0.9 pad_maximum_fusion
  9.9 0.7 reshape.323
  10.6 17.5 %all-to-all-start = ((bf16[64,4,256]{2,1,0:T(4,128)(2,1)}), bf16[64,4,256]{2,1,0:T(4,128)(2,1)S(1)}, u32[]{:S(2)}, u32[]{:S(2)}) async-start(bf16[64,4,256]{2,1,0:T(4,128)(2,1)} %reshape.323), calls=%async_computation | async-start | bytes 262144 | tf_op jit(solution)/shard_map/all_to_all | solution.py:97
  28.1 0.8 reshape.321
  29.0 1.4 gather_fusion
  30.7 0.8 gather_fusion.1
  31.7 1.2 gather_fusion.2
  33.1 1.3 dynamic_slice.3
  35.0 0.6 fusion.34
  35.7 1.3 fusion.36
  37.0 2.0 %fusion.35 = (s32[]{:T(128)}, s32[]{:T(128)}, s32[]{:T(128)}) fusion(s32[74]{0:T(128)S(1)} %copy-done.11, s32[]{:T(128)} %bitcast.1, s32[]{:T(128)} %fusion.36, s32[]{:T(128)} %fusion.34), kind=kLoop, calls=%fused_computation.94 | loop fusion | flops 663 | bytes 320 | tf_op jit(solution)/shard_map/reduce_sum | solution.py:62
  39.0 1.2 broadcast_add_fusion
  40.4 0.2 fusion.24
  40.6 0.7 iota_compare_fusion.3
  41.8 1.2 iota_compare_fusion.4
  43.3 0.5 copy-done.3
  43.9 0.8 gather_fusion.3
  44.8 0.9 broadcast_select_fusion
  45.7 10.3 %all-to-all-start.1 = ((bf16[64,2,4,256]{3,2,1,0:T(4,128)(2,1)}), bf16[64,2,4,256]{3,2,1,0:T(4,128)(2,1)S(1)}, u32[]{:S(2)}, u32[]{:S(2)}) async-start(bf16[64,2,4,256]{3,2,1,0:T(4,128)(2,1)} %broadcast_select_fusion), calls=%async_computation.1 | async-start | bytes 524288 | tf_op jit(solution)/shard_map/all_to_all | solution.py:105
  56.2 0.4 select_reduce_fusion.1
  56.6 0.3 convert_reduce_fusion.2
  56.9 11.2 %all-to-all-done.1 = bf16[64,2,4,256]{3,2,1,0:T(4,128)(2,1)S(1)} async-done(((bf16[64,2,4,256]{3,2,1,0:T(4,128)(2,1)}), bf16[64,2,4,256]{3,2,1,0:T(4,128)(2,1)S(1)}, u32[]{:S(2)}, u32[]{:S(2)}) %all-to-all-start.1) | async-done | bytes 262176 | tf_op jit(solution)/shard_map/all_to_all | solution.py:105
  68.3 0.4 select_reduce_fusion
  68.7 0.3 convert_reduce_fusion.1
  69.0 0.3 fusion.6
  69.4 0.3 fusion.8
  69.8 0.7 collective-permute-start.1
  70.5 43.3 %all_gather.7 = bf16[512,896]{1,0:T(8,128)(2,1)S(1)} all-gather(bf16[64,896]{1,0:T(8,128)(2,1)S(1)} %collective-permute-done.1), channel_id=1, replica_groups=mesh['x'=4,'z'=8,'c'=2,'mlp'=8] {'x','c'}, dimensions={0}, use_global_device_ids=true | all-gather | bytes 1032192 | tf_op jit(solution)/shard_map/all_gather | solution.py:174
  113.8 2.6 %fusion = bf16[8,512,112]{1,2,0:T(8,128)(2,1)S(1)} fusion(bf16[896,8,112]{0,2,1:T(8,128)(2,1)} %bitcast.83, bf16[512,896]{1,0:T(8,128)(2,1)S(1)} %all_gather.7), kind=kOutput, calls=%fused_computation.6 | convolution fusion | flops 822542336 | bytes 3440640 | tf_op jit(solution)/shard_map/tf,fjc->jtc/dot_general | solution.py:175
  116.4 31.9 %all_to_all.15 = bf16[8,512,112]{1,2,0:T(8,128)(2,1)S(1)} all-to-all(bf16[8,512,112]{1,2,0:T(8,128)(2,1)S(1)} %fusion), channel_id=1, replica_groups=mesh['x'=4,'z'=8,'c'=2,'mlp'=8] {'z'}, dimensions={0} | all-to-all | bytes 1835008 | tf_op jit(solution)/shard_map/all_to_all | solution.py:181
  148.4 0.7 add_convert_fusion
  (64 shorter events, 2.4 us)
Async XLA Ops:
  7.2 24.6 %copy-start = (s32[74]{0:T(128)S(1)}, s32[74]{0:T(128)}, u32[]{:S(2)}) copy-start(s32[74]{0:T(128)} %param.27) | copy-start | bytes 892
  7.2 23.5 %copy-start.1 = (s32[74]{0:T(128)S(1)}, s32[74]{0:T(128)}, u32[]{:S(2)}) copy-start(s32[74]{0:T(128)} %param.25) | copy-start | bytes 892
  7.2 29.8 %copy-start.9 = (bf16[64,128]{1,0:T(8,128)(2,1)S(1)}, bf16[64,128]{1,0:T(8,128)(2,1)}, u32[]{:S(2)}) copy-start(bf16[64,128]{1,0:T(8,128)(2,1)} %param.15) | copy-start | bytes 49156
  7.2 29.8 %copy-start.11 = (s32[74]{0:T(128)S(1)}, s32[74]{0:T(128)}, u32[]{:S(2)}) copy-start(s32[74]{0:T(128)} %param.26) | copy-start | bytes 892
  7.2 31.8 %copy-start.12 = (s32[64]{0:T(128)S(1)}, s32[64]{0:T(128)}, u32[]{:S(2)}) copy-start(s32[64]{0:T(128)} %param.24) | copy-start | bytes 772
  7.2 34.3 %copy-start.10 = (bf16[64,128]{1,0:T(8,128)(2,1)S(1)}, bf16[64,128]{1,0:T(8,128)(2,1)}, u32[]{:S(2)}) copy-start(bf16[64,128]{1,0:T(8,128)(2,1)} %param.16) | copy-start | bytes 49156
  7.2 34.4 %copy-start.7 = (bf16[320,128]{1,0:T(8,128)(2,1)S(1)}, bf16[320,128]{1,0:T(8,128)(2,1)}, u32[]{:S(2)}) copy-start(bf16[320,128]{1,0:T(8,128)(2,1)} %param.17) | copy-start | bytes 245764
  7.2 34.4 %copy-start.6 = (bf16[320,128]{1,0:T(8,128)(2,1)S(1)}, bf16[320,128]{1,0:T(8,128)(2,1)}, u32[]{:S(2)}) copy-start(bf16[320,128]{1,0:T(8,128)(2,1)} %param.18) | copy-start | bytes 245764
  7.3 35.8 %collective-permute-start = (bf16[896,112]{0,1:T(8,128)(2,1)}, bf16[896,112]{0,1:T(8,128)(2,1)S(1)}, u32[]{:S(2)}, u32[]{:S(2)}) collective-permute-start(bf16[896,112]{0,1:T(8,128)(2,1)} %param.21), channel_id=1, source_target_pairs={{0,0},{1,16},{2,32},{3,48},{4,64},{5,80},{6,96},{7,112},{16,1},{17... | collective-permute-start | bytes 602120 | tf_op jit(solution)/shard_map/ppermute | solution.py:112
  10.6 32.5 %copy-start.5 = (bf16[64,896]{1,0:T(8,128)(2,1)S(1)}, bf16[64,896]{1,0:T(8,128)(2,1)}, u32[]{:S(2)}) copy-start(bf16[64,896]{1,0:T(8,128)(2,1)} %param.14) | copy-start | bytes 344068
  10.6 33.4 %all-to-all-start = ((bf16[64,4,256]{2,1,0:T(4,128)(2,1)}), bf16[64,4,256]{2,1,0:T(4,128)(2,1)S(1)}, u32[]{:S(2)}, u32[]{:S(2)}) async-start(bf16[64,4,256]{2,1,0:T(4,128)(2,1)} %reshape.323), calls=%async_computation | async-start | bytes 262144 | tf_op jit(solution)/shard_map/all_to_all | solution.py:97
  28.0 85.8 %all-gather.2.cloned.1.call-start = ((), (), s32[]{:S(2)}) async-start(), calls=%async_computation.3 | async-start | bytes 1806336 | tf_op jit(solution)/shard_map/all_gather | solution.py:114
  41.8 14.3 %copy-start.2 = (bf16[320,128]{1,0:T(8,128)(2,1)}, bf16[320,128]{1,0:T(8,128)(2,1)S(1)}, u32[]{:S(2)}) copy-start(bf16[320,128]{1,0:T(8,128)(2,1)S(1)} %get-tuple-element.22) | copy-start | bytes 245764
  41.8 27.6 %copy-start.8 = (bf16[320,128]{1,0:T(8,128)(2,1)}, bf16[320,128]{1,0:T(8,128)(2,1)S(1)}, u32[]{:S(2)}) copy-start(bf16[320,128]{1,0:T(8,128)(2,1)S(1)} %get-tuple-element.21) | copy-start | bytes 245764
  43.1 0.7 copy-start.3
  45.7 22.3 %all-to-all-start.1 = ((bf16[64,2,4,256]{3,2,1,0:T(4,128)(2,1)}), bf16[64,2,4,256]{3,2,1,0:T(4,128)(2,1)S(1)}, u32[]{:S(2)}, u32[]{:S(2)}) async-start(bf16[64,2,4,256]{3,2,1,0:T(4,128)(2,1)} %broadcast_select_fusion), calls=%async_computation.1 | async-start | bytes 524288 | tf_op jit(solution)/shard_map/all_to_all | solution.py:105
  69.8 0.7 collective-permute-start.1
  116.4 32.0 %copy-start.4 = (bf16[512,112]{0,1:T(8,128)(2,1)S(1)}, bf16[512,112]{0,1:T(8,128)(2,1)}, u32[]{:S(2)}) copy-start(bf16[512,112]{0,1:T(8,128)(2,1)} %param.22) | copy-start | bytes 344068
Sparse Core Ops, SparseCore 0:
  43.9 60.4 all-gather.1

commit v21 on v20

--- a/solution.py
+++ b/solution.py
@@ -138,19 +138,10 @@
         leaf_value_output.reshape(leaf_rows, kv_heads, width),
         leaf_row_mask,
     )
-    root_pair = incoming[:, 0].reshape(my_pair.shape)
-    middle_pair = incoming[:, 1].reshape(my_pair.shape)
-    root_keys = root_pair[:, :kv_width]
-    root_values = root_pair[:, kv_width:]
-    middle_keys = middle_pair[:, :kv_width]
-    middle_values = middle_pair[:, kv_width:]
     node_ids = jnp.arange(node_rows)
-    both_keys = jnp.concatenate([root_keys, middle_keys], axis=0).reshape(
-        2 * node_rows, kv_heads, width
-    )
-    both_values = jnp.concatenate([root_values, middle_values], axis=0).reshape(
-        2 * node_rows, kv_heads, width
-    )
+    both_pairs = jnp.swapaxes(incoming, 0, 1).reshape(2 * node_rows, my_pair.shape[1])
+    both_keys = both_pairs[:, :kv_width].reshape(2 * node_rows, kv_heads, width)
+    both_values = both_pairs[:, kv_width:].reshape(2 * node_rows, kv_heads, width)
     both_valid = jnp.concatenate([node_ids < root_length, node_ids < middle_length], axis=0)
     shared_state = attend_key_block(token_queries, both_keys, both_values, both_valid[None, :])
     final = merge_state(shared_state, leaf_state)

time: 157 us -> 158 us (level)
  transfers between devices with their start and end apart: 5 -> 5, of which waited for: 1 -> 1; matrix products, arithmetic and copies ran while one was open for 13% -> 14% of each run, Pallas kernels for 0% -> 0%
where the time goes in v21:
time: 158 us; the launch traced here: 156 us
  blocking collectives  74.3 us (47%)
  starting transfers between devices  30.1 us (19%)
  between operations  15.2 us (10%)
  other arithmetic  12.7 us (8%)
  waiting for transfers between devices  11.2 us (7%)
  local copies, waits for them, and re-layouts  8.76 us (6%)
  matrix products  4.19 us (3%)
    all_gather x1, blocking collectives, body(): token_block = lax.all_gather(token_here, ('x', 'c'), axis=0, tiled=True)  43.4 us
    all_to_all x1, blocking collectives, body(): arrived = lax.all_to_all(parts, GROUP, 0, 0, tiled=True)  30.9 us
    all_to_all x1, starting transfers between devices, body(): spread = lax.all_to_all(pieces, TOK, 0, 0, tiled=True)  17.3 us
    all_to_all x1, waiting for transfers between devices, body(): incoming = lax.all_to_all(outgoing, TOK, 0, 0, tiled=True)  11.2 us
    all_to_all x1, starting transfers between devices, body(): incoming = lax.all_to_all(outgoing, TOK, 0, 0, tiled=True)  10.3 us
    reduce_sum x3, other arithmetic, lookup(): return jnp.sum(jnp.where(jnp.arange(table.shape[0]) == index, table, 0))  5.24 us
  transfers between devices with their start and end apart: 5, of which 1 were waited for; matrix products, arithmetic and copies ran while one was open for 14% of the time, Pallas kernels for 0%

profile of v21, /device:TPU:1, one launch (start us, length us, event | category | flops | bytes accessed | tf_op | source)
XLA Modules:
  0.0 156.4 jit_solution(14840513258216203519)
XLA Ops:
  7.3 1.7 %collective-permute-start = (bf16[896,112]{0,1:T(8,128)(2,1)}, bf16[896,112]{0,1:T(8,128)(2,1)S(1)}, u32[]{:S(2)}, u32[]{:S(2)}) collective-permute-start(bf16[896,112]{0,1:T(8,128)(2,1)} %param.21), channel_id=1, source_target_pairs={{0,0},{1,16},{2,32},{3,48},{4,64},{5,80},{6,96},{7,112},{16,1},{17... | collective-permute-start | bytes 602120 | tf_op jit(solution)/shard_map/ppermute | solution.py:112
  9.0 0.9 pad_maximum_fusion
  9.9 0.7 reshape.326
  10.6 17.3 %all-to-all-start = ((bf16[64,4,256]{2,1,0:T(4,128)(2,1)}), bf16[64,4,256]{2,1,0:T(4,128)(2,1)S(1)}, u32[]{:S(2)}, u32[]{:S(2)}) async-start(bf16[64,4,256]{2,1,0:T(4,128)(2,1)} %reshape.326), calls=%async_computation | async-start | bytes 262144 | tf_op jit(solution)/shard_map/all_to_all | solution.py:97
  28.0 0.8 reshape.324
  28.8 1.3 dynamic_slice.3
  30.7 1.3 fusion.30
  32.0 1.9 %fusion.32 = s32[]{:T(128)} fusion(s32[74]{0:T(128)} %param.25, s32[]{:T(128)} %fusion.30), kind=kLoop, calls=%fused_computation.91 | loop fusion | flops 221 | bytes 304 | tf_op jit(solution)/shard_map/reduce_sum | solution.py:62
  34.0 1.4 gather_fusion
  35.7 0.8 gather_fusion.1
  36.8 1.2 gather_fusion.2
  38.2 2.0 %fusion.31 = (s32[]{:T(128)}, s32[]{:T(128)}, s32[]{:T(128)}) fusion(s32[74]{0:T(128)S(1)} %copy-done.11, s32[]{:T(128)} %bitcast.1, s32[]{:T(128)} %fusion.32, s32[]{:T(128)} %fusion.30), kind=kLoop, calls=%fused_computation.90 | loop fusion | flops 663 | bytes 320 | tf_op jit(solution)/shard_map/reduce_sum | solution.py:62
  40.2 1.2 broadcast_add_fusion
  41.6 0.2 fusion.20
  41.8 0.7 iota_compare_fusion.3
  43.1 0.7 copy-done.3
  43.8 1.2 iota_compare_fusion.4
  45.4 0.8 gather_fusion.3
  46.2 0.9 broadcast_select_fusion
  47.1 10.3 %all-to-all-start.1 = ((bf16[64,2,4,256]{3,2,1,0:T(4,128)(2,1)}), bf16[64,2,4,256]{3,2,1,0:T(4,128)(2,1)S(1)}, u32[]{:S(2)}, u32[]{:S(2)}) async-start(bf16[64,2,4,256]{3,2,1,0:T(4,128)(2,1)} %broadcast_select_fusion), calls=%async_computation.1 | async-start | bytes 524288 | tf_op jit(solution)/shard_map/all_to_all | solution.py:105
  57.6 0.4 select_reduce_fusion.1
  58.0 0.3 convert_reduce_fusion.2
  58.3 11.2 %all-to-all-done.1 = bf16[64,2,4,256]{3,2,1,0:T(4,128)(2,1)S(1)} async-done(((bf16[64,2,4,256]{3,2,1,0:T(4,128)(2,1)}), bf16[64,2,4,256]{3,2,1,0:T(4,128)(2,1)S(1)}, u32[]{:S(2)}, u32[]{:S(2)}) %all-to-all-start.1) | async-done | bytes 262176 | tf_op jit(solution)/shard_map/all_to_all | solution.py:105
  69.6 0.4 select_reduce_fusion
  70.0 0.3 convert_reduce_fusion.1
  70.4 0.3 fusion.6
  70.7 0.3 fusion.8
  71.2 0.7 collective-permute-start.1
  71.9 43.4 %all_gather.7 = bf16[512,896]{1,0:T(8,128)(2,1)S(1)} all-gather(bf16[64,896]{1,0:T(8,128)(2,1)S(1)} %collective-permute-done.1), channel_id=1, replica_groups=mesh['x'=4,'z'=8,'c'=2,'mlp'=8] {'x','c'}, dimensions={0}, use_global_device_ids=true | all-gather | bytes 1032192 | tf_op jit(solution)/shard_map/all_gather | solution.py:165
  115.2 2.6 %fusion = bf16[8,512,112]{1,2,0:T(8,128)(2,1)S(1)} fusion(bf16[896,8,112]{0,2,1:T(8,128)(2,1)} %bitcast.85, bf16[512,896]{1,0:T(8,128)(2,1)S(1)} %all_gather.7), kind=kOutput, calls=%fused_computation.6 | convolution fusion | flops 822542336 | bytes 3440640 | tf_op jit(solution)/shard_map/tf,fjc->jtc/dot_general | solution.py:166
  117.8 30.9 %all_to_all.15 = bf16[8,512,112]{1,2,0:T(8,128)(2,1)S(1)} all-to-all(bf16[8,512,112]{1,2,0:T(8,128)(2,1)S(1)} %fusion), channel_id=1, replica_groups=mesh['x'=4,'z'=8,'c'=2,'mlp'=8] {'z'}, dimensions={0} | all-to-all | bytes 1835008 | tf_op jit(solution)/shard_map/all_to_all | solution.py:172
  148.9 0.7 add_convert_fusion
  (62 shorter events, 2.3 us)
Async XLA Ops:
  7.2 29.6 %copy-start = (s32[74]{0:T(128)S(1)}, s32[74]{0:T(128)}, u32[]{:S(2)}) copy-start(s32[74]{0:T(128)} %param.27) | copy-start | bytes 892
  7.2 28.5 %copy-start.1 = (s32[74]{0:T(128)S(1)}, s32[74]{0:T(128)}, u32[]{:S(2)}) copy-start(s32[74]{0:T(128)} %param.25) | copy-start | bytes 892
  7.2 31.0 %copy-start.9 = (bf16[64,128]{1,0:T(8,128)(2,1)S(1)}, bf16[64,128]{1,0:T(8,128)(2,1)}, u32[]{:S(2)}) copy-start(bf16[64,128]{1,0:T(8,128)(2,1)} %param.15) | copy-start | bytes 49156
  7.2 31.0 %copy-start.11 = (s32[74]{0:T(128)S(1)}, s32[74]{0:T(128)}, u32[]{:S(2)}) copy-start(s32[74]{0:T(128)} %param.26) | copy-start | bytes 892
  7.2 33.0 %copy-start.12 = (s32[64]{0:T(128)S(1)}, s32[64]{0:T(128)}, u32[]{:S(2)}) copy-start(s32[64]{0:T(128)} %param.24) | copy-start | bytes 772
  7.2 35.5 %copy-start.10 = (bf16[64,128]{1,0:T(8,128)(2,1)S(1)}, bf16[64,128]{1,0:T(8,128)(2,1)}, u32[]{:S(2)}) copy-start(bf16[64,128]{1,0:T(8,128)(2,1)} %param.16) | copy-start | bytes 49156
  7.2 35.7 %copy-start.7 = (bf16[320,128]{1,0:T(8,128)(2,1)S(1)}, bf16[320,128]{1,0:T(8,128)(2,1)}, u32[]{:S(2)}) copy-start(bf16[320,128]{1,0:T(8,128)(2,1)} %param.17) | copy-start | bytes 245764
  7.2 35.7 %copy-start.6 = (bf16[320,128]{1,0:T(8,128)(2,1)S(1)}, bf16[320,128]{1,0:T(8,128)(2,1)}, u32[]{:S(2)}) copy-start(bf16[320,128]{1,0:T(8,128)(2,1)} %param.18) | copy-start | bytes 245764
  7.3 35.8 %collective-permute-start = (bf16[896,112]{0,1:T(8,128)(2,1)}, bf16[896,112]{0,1:T(8,128)(2,1)S(1)}, u32[]{:S(2)}, u32[]{:S(2)}) collective-permute-start(bf16[896,112]{0,1:T(8,128)(2,1)} %param.21), channel_id=1, source_target_pairs={{0,0},{1,16},{2,32},{3,48},{4,64},{5,80},{6,96},{7,112},{16,1},{17... | collective-permute-start | bytes 602120 | tf_op jit(solution)/shard_map/ppermute | solution.py:112
  10.6 34.8 %all-to-all-start = ((bf16[64,4,256]{2,1,0:T(4,128)(2,1)}), bf16[64,4,256]{2,1,0:T(4,128)(2,1)S(1)}, u32[]{:S(2)}, u32[]{:S(2)}) async-start(bf16[64,4,256]{2,1,0:T(4,128)(2,1)} %reshape.326), calls=%async_computation | async-start | bytes 262144 | tf_op jit(solution)/shard_map/all_to_all | solution.py:97
  27.9 17.2 %copy-start.5 = (bf16[64,896]{1,0:T(8,128)(2,1)S(1)}, bf16[64,896]{1,0:T(8,128)(2,1)}, u32[]{:S(2)}) copy-start(bf16[64,896]{1,0:T(8,128)(2,1)} %param.14) | copy-start | bytes 344068
  27.9 87.3 %all-gather.2.cloned.1.call-start = ((), (), s32[]{:S(2)}) async-start(), calls=%async_computation.3 | async-start | bytes 1806336 | tf_op jit(solution)/shard_map/all_gather | solution.py:114
  43.0 14.5 %copy-start.2 = (bf16[320,128]{1,0:T(8,128)(2,1)}, bf16[320,128]{1,0:T(8,128)(2,1)S(1)}, u32[]{:S(2)}) copy-start(bf16[320,128]{1,0:T(8,128)(2,1)S(1)} %get-tuple-element.20) | copy-start | bytes 245764
  43.0 27.7 %copy-start.8 = (bf16[320,128]{1,0:T(8,128)(2,1)}, bf16[320,128]{1,0:T(8,128)(2,1)S(1)}, u32[]{:S(2)}) copy-start(bf16[320,128]{1,0:T(8,128)(2,1)S(1)} %get-tuple-element.19) | copy-start | bytes 245764
  43.1 0.7 copy-start.3
  47.1 22.3 %all-to-all-start.1 = ((bf16[64,2,4,256]{3,2,1,0:T(4,128)(2,1)}), bf16[64,2,4,256]{3,2,1,0:T(4,128)(2,1)S(1)}, u32[]{:S(2)}, u32[]{:S(2)}) async-start(bf16[64,2,4,256]{3,2,1,0:T(4,128)(2,1)} %broadcast_select_fusion), calls=%async_computation.1 | async-start | bytes 524288 | tf_op jit(solution)/shard_map/all_to_all | solution.py:105
  71.2 0.7 collective-permute-start.1
  117.8 31.1 %copy-start.4 = (bf16[512,112]{0,1:T(8,128)(2,1)S(1)}, bf16[512,112]{0,1:T(8,128)(2,1)}, u32[]{:S(2)}) copy-start(bf16[512,112]{0,1:T(8,128)(2,1)} %param.22) | copy-start | bytes 344068
Sparse Core Ops, SparseCore 0:
  43.9 60.6 all-gather.1
